TPU v7x, 512 devices: a whole 4x4x16 slice. The times are simulated.
512 devices in a mesh: walker: 32 (over z, y_lo), orb: 16 (over x, y_hi, core).
Axes of the slice: x: 4, y: 4 (y_hi: 2, y_lo: 2; y = y_hi * 2 + y_lo), z: 16, core: 2. Of those that a mesh axis runs over, the one named last changes fastest.
Arguments:
- tile_index: int32 [32768], P('walker'), may hold values from 0 to 63
- weights: bfloat16 [32768, 64], P('walker'), may hold values from -0.75 to 0.75
- electron: int32 [32768], P('walker'), may hold values from 0 to 767
- strength: float32 [32768], P('walker'), may hold values from -1.5 to 1.5
- spline_table: bfloat16 [4096, 4096], P(None, 'orb'), may hold values from -6 to 6
- rotation: bfloat16 [4096, 768], P('orb'), may hold values from -0.09375 to 0.09375
- inverse: bfloat16 [32, 768, 768], P('walker', 'orb'), may hold values from -0.21875 to 0.21875
Outputs:
- ratios: float32 [32768], P(('walker', 'orb'))
- gradient: float32 [4096, 768], P('orb')
All inputs are finite; a program needn't handle non-finite values.
Results may differ from a plain program's by a relative error of at most 0.0042.
Values may be sent and summed in bfloat16 or wider, within the bound.
No kernel may reach another device: no remote copies, remote signals or barrier semaphores. Data moves between devices by JAX's collectives and lax.ppermute only.
A program may use at most 64 MiB of HBM per device.

v0:
```python
import jax
import jax.numpy as jnp
from jax import lax
from jax.sharding import PartitionSpec as P


def body(tile_index, weights, electron, strength, spline_table, rotation, inverse):
    points = tile_index.shape[0]
    coeffs = weights.shape[1]
    tiles_count = spline_table.shape[0] // coeffs
    shards = lax.axis_size("orb")
    own_rows = points // shards
    first_point = lax.axis_index("orb") * own_rows
    onehot = (tile_index[:, None] == jnp.arange(tiles_count, dtype=jnp.int32)[None, :]).astype(
        jnp.bfloat16
    )
    stencil_matrix = (onehot[:, :, None] * weights[:, None, :]).reshape(
        points, tiles_count * coeffs
    )
    orbital_values = jnp.dot(
        stencil_matrix, spline_table, preferred_element_type=jnp.float32
    ).astype(jnp.bfloat16)
    local_inverse = inverse[0]
    rotated = lax.psum_scatter(
        lax.dot_general(
            rotation, orbital_values, (((0,), (1,)), ((), ())), preferred_element_type=jnp.float32
        ),
        "orb",
        scatter_dimension=0,
        tiled=True,
    )
    columns = jnp.take(local_inverse, electron, axis=1).astype(jnp.float32)
    partial_ratio = jnp.sum(rotated * columns, axis=0)
    ratio_total = lax.psum(partial_ratio, "orb")
    ratios = lax.dynamic_slice_in_dim(ratio_total, first_point, own_rows, 0)
    adjoint = (columns * strength[None, :]).astype(jnp.bfloat16)
    local_gradient = lax.dot_general(
        orbital_values,
        lax.all_gather(adjoint, "orb", axis=0, tiled=True),
        (((0,), (1,)), ((), ())),
        preferred_element_type=jnp.float32,
    )
    gradient = lax.psum(local_gradient, "walker")
    return (ratios, gradient)


def solution(mesh):
    in_specs = (
        P("walker"),
        P("walker", None),
        P("walker"),
        P("walker"),
        P(None, "orb"),
        P("orb", None),
        P("walker", "orb", None),
    )
    out_specs = (P(("walker", "orb")), P("orb", None))
    return jax.shard_map(body, mesh=mesh, in_specs=in_specs, out_specs=out_specs, check_vma=False)
```

profile of v0, /device:TPU:2, one launch (start us, length us, event | category | flops | bytes accessed | tf_op | source)
XLA Modules:
  0.0 463.4 jit_solution(13601765400764669437)
XLA Ops:
  7.2 0.0 copy-start
  7.2 0.0 reduce-scatter.4.cloned.1.call-start
  7.2 0.9 fusion
  8.1 1.5 broadcast_multiply_fusion
  9.5 0.0 copy-done
  9.5 0.0 copy-start.1
  9.6 2.5 convolution_convert_fusion
  12.0 0.0 copy-done.1
  12.0 2.2 convolution_bitcast_fusion
  14.3 3.5 copy.17
  17.8 0.0 copy-start.2
  17.8 0.0 copy-start.3
  17.8 0.0 copy-start.4
  17.8 0.0 reduce-scatter.4.cloned.1.call-update
  17.8 0.0 all-gather.2.cloned.1.call-start
  17.9 0.8 copy-done.2
  18.7 0.2 copy.14
  18.8 0.0 copy-done.3
  18.9 3.2 gather_fusion
  22.1 0.1 copy.15
  22.2 98.4 %reduce-scatter.4.cloned.1.call-done = f32[48,1024]{1,0:T(8,128)} async-done(((f32[768,1024]{1,0:T(8,128)}), f32[48,1024]{1,0:T(8,128)}) %reduce-scatter.4.cloned.1.call-update) | async-done | bytes 196624 | tf_op jit(solution)/shard_map/reduce_scatter | solution.py:24
  120.6 0.0 copy-done.4
  120.6 1.6 fusion.2
  122.2 0.0 all-gather.2.cloned.1.call-update
  122.2 0.0 all-reduce.2.cloned.1.call-start
  122.3 63.0 %all-gather.2.cloned.1.call-done = bf16[768,1024]{1,0:T(8,128)(2,1)} async-done(((bf16[48,1024]{1,0:T(8,128)(2,1)}), bf16[768,1024]{1,0:T(8,128)(2,1)}) %all-gather.2.cloned.1.call-update) | async-done | bytes 1572880 | tf_op jit(solution)/shard_map/all_gather | solution.py:39
  185.3 2.9 fusion.4
  188.2 0.0 all-reduce.2.cloned.1.call-update
  188.2 29.0 %psum.14 = f32[1024]{0:T(1024)S(1)} all-reduce(f32[1024]{0:T(1024)S(1)} %get-tuple-element.3), channel_id=1, replica_groups=mesh['walker'=32,'orb'=16] {'orb'}, use_global_device_ids=true, to_apply=%region_2.3 | all-reduce | flops 1024 | bytes 8192 | tf_op jit(solution)/shard_map/psum | solution.py:34
  217.2 0.6 dynamic_slice.3
  217.8 237.0 %all-reduce.2.cloned.1.call-done = f32[256,768]{1,0:T(8,128)} async-done(((f32[256,768]{1,0:T(8,128)}), f32[256,768]{1,0:T(8,128)}) %all-reduce.2.cloned.1.call-update) | async-done | bytes 786448 | tf_op jit(solution)/shard_map/psum | solution.py:43
  454.8 2.1 copy.20
  (2 shorter events, 0.0 us)
Async XLA Ops:
  7.2 2.4 copy-start
  7.2 113.4 %reduce-scatter.4.cloned.1.call-start = ((), (), s32[]{:S(2)}) async-start(), calls=%async_computation.3 | async-start | bytes 3342336 | tf_op jit(solution)/shard_map/reduce_scatter | solution.py:24
  9.5 2.5 copy-start.1
  17.8 0.9 copy-start.2
  17.8 1.1 copy-start.3
  17.8 102.8 %copy-start.4 = (f32[1024]{0:T(1024)S(1)}, f32[1024]{0:T(1024)}, u32[]{:S(2)}) copy-start(f32[1024]{0:T(1024)} %param.10) | copy-start | bytes 12292
  17.8 167.5 %all-gather.2.cloned.1.call-start = ((), (), s32[]{:S(2)}) async-start(), calls=%async_computation.1 | async-start | bytes 1671168 | tf_op jit(solution)/shard_map/all_gather | solution.py:39
  122.2 332.6 %all-reduce.2.cloned.1.call-start = ((), (), s32[]{:S(2)}) async-start(), calls=%async_computation.2 | async-start | bytes 1572864 | tf_op jit(solution)/shard_map/psum | solution.py:43
Sparse Core Ops, SparseCore 0:
  17.9 102.6 reduce-scatter.3
  124.5 60.7 all-gather.1
  188.8 266.0 all-reduce.1
where the time goes:
time: 464 us; the launch traced here: 463 us
  waiting for transfers between devices  398 us (86%)
  blocking collectives  29 us (6%)
  between operations  13.8 us (3%)
  local copies, waits for them, and re-layouts  10.5 us (2%)
  matrix products  7.6 us (2%)
    psum x1, waiting for transfers between devices, body(): gradient = lax.psum(local_gradient, 'walker')  237 us
    reduce_scatter x1, waiting for transfers between devices, body(): lax.psum_scatter(lax.dot_general(rotation, orbital_values, (((0,), (1,)),...  98.4 us
    all_gather x1, waiting for transfers between devices, body(): lax.all_gather(adjoint, 'orb', axis=0, tiled=True)  63 us
    psum x1, blocking collectives, body(): ratio_total = lax.psum(partial_ratio, 'orb')  29 us
  transfers between devices with their start and end apart: 3, of which 3 were waited for; matrix products, arithmetic and copies ran while one was open for 1% of the time, Pallas kernels for 0%

commit v1 on v0

v1 whole, which is shorter than its diff:
```python
import jax
import jax.numpy as jnp
from jax import lax
from jax.sharding import PartitionSpec as P


def body(tile_index, weights, electron, strength, spline_table, rotation, inverse):
    points = tile_index.shape[0]
    coeffs = weights.shape[1]
    tiles_count = spline_table.shape[0] // coeffs
    electrons = inverse.shape[2]
    inverse_full = lax.all_gather(inverse[0], "orb", axis=0, tiled=True)
    onehot = (tile_index[:, None] == jnp.arange(tiles_count, dtype=jnp.int32)[None, :]).astype(
        jnp.bfloat16
    )
    stencil_matrix = (onehot[:, :, None] * weights[:, None, :]).reshape(
        points, tiles_count * coeffs
    )
    orbital_values = jnp.dot(
        stencil_matrix, spline_table, preferred_element_type=jnp.float32
    ).astype(jnp.bfloat16)
    pick = (electron[:, None] == jnp.arange(electrons, dtype=jnp.int32)[None, :]).astype(
        jnp.bfloat16
    )
    columns = lax.dot_general(
        pick, inverse_full, (((1,), (1,)), ((), ())), preferred_element_type=jnp.float32
    )
    adjoint = (columns * strength[:, None]).astype(jnp.bfloat16)
    local_gradient = lax.dot_general(
        orbital_values, adjoint, (((0,), (0,)), ((), ())), preferred_element_type=jnp.float32
    )
    rotated_columns = lax.dot_general(
        columns.astype(jnp.bfloat16),
        rotation,
        (((1,), (1,)), ((), ())),
        preferred_element_type=jnp.float32,
    )
    partial_ratio = jnp.sum(orbital_values.astype(jnp.float32) * rotated_columns, axis=1)
    ratios = lax.psum_scatter(partial_ratio, "orb", scatter_dimension=0, tiled=True)
    gradient = lax.psum(local_gradient, "walker")
    return (ratios, gradient)


def solution(mesh):
    in_specs = (
        P("walker"),
        P("walker", None),
        P("walker"),
        P("walker"),
        P(None, "orb"),
        P("orb", None),
        P("walker", "orb", None),
    )
    out_specs = (P(("walker", "orb")), P("orb", None))
    return jax.shard_map(body, mesh=mesh, in_specs=in_specs, out_specs=out_specs, check_vma=False)
```

time: 464 us -> 357 us (0.77)
  the two profiles are of different devices: /device:TPU:2 before, /device:TPU:4 now
where the time goes in v1:
time: 357 us
  waiting for transfers between devices  295 us (83%)
  blocking collectives  30.2 us (8%)
  between operations  14.8 us (4%)
  matrix products  9.31 us (3%)
  local copies, waits for them, and re-layouts  5.59 us (2%)
    psum x1, waiting for transfers between devices, body(): gradient = lax.psum(local_gradient, 'walker')  232 us
    all_gather x1, waiting for transfers between devices, body(): inverse_full = lax.all_gather(inverse[0], 'orb', axis=0, tiled=True)  62.3 us
    unnamed x1, blocking collectives  30.2 us
  transfers between devices with their start and end apart: 2, of which 2 were waited for; matrix products, arithmetic and copies ran while one was open for 3% of the time, Pallas kernels for 0%

profile of v1, /device:TPU:4, one launch (start us, length us, event | category | flops | bytes accessed | tf_op | source)
XLA Modules:
  0.0 357.1 jit_solution(11248412728367267794)
XLA Ops:
  7.2 0.0 copy-start
  7.2 0.0 all-gather.3.cloned.1.call-start
  7.2 0.7 all-gather.3.cloned.1.call-update
  7.9 0.0 all-reduce.3.cloned.1.call-start
  8.0 0.7 fusion.13
  8.7 1.5 broadcast_multiply_fusion
  10.1 0.0 copy-done
  10.1 0.0 copy-start.4
  10.2 2.4 convolution_convert_fusion
  12.6 0.0 copy-start.3
  12.6 62.3 %all-gather.3.cloned.1.call-done = bf16[1,768,768]{2,1,0:T(8,128)(2,1)} async-done(((bf16[1,48,768]{2,1,0:T(8,128)(2,1)}), bf16[1,768,768]{2,1,0:T(8,128)(2,1)}) %all-gather.3.cloned.1.call-update) | async-done | bytes 1179664 | tf_op jit(solution)/shard_map/all_gather | solution.py:12
  74.9 0.0 copy-done.4
  74.9 2.8 fusion
  77.7 0.0 copy-start.1
  77.7 1.6 copy-done.1
  79.4 0.0 copy-done.3
  79.4 0.0 copy-start.2
  79.4 1.6 fusion.1
  81.0 0.0 all-reduce.3.cloned.1.call-update
  81.0 1.3 dynamic-slice
  82.9 0.0 copy-done.2
  82.9 2.5 fusion.9
  85.5 30.2 %all-reduce = f32[1024]{0:T(1024)S(1)} all-reduce(f32[1024]{0:T(1024)S(1)} %fusion.9), channel_id=3, replica_groups=mesh['walker'=32,'orb'=16] {'orb'}, use_global_device_ids=true, to_apply=%region_1.0.clone | all-reduce | flops 1024 | bytes 8192
  115.7 0.6 dynamic-slice.1
  116.3 232.0 %all-reduce.3.cloned.1.call-done = f32[256,768]{1,0:T(8,128)} async-done(((f32[256,768]{1,0:T(8,128)}), f32[256,768]{1,0:T(8,128)}) %all-reduce.3.cloned.1.call-update) | async-done | bytes 786448 | tf_op jit(solution)/shard_map/psum | solution.py:40
  348.2 2.1 copy.11
Async XLA Ops:
  7.2 3.0 copy-start
  7.2 67.7 %all-gather.3.cloned.1.call-start = ((), (), s32[]{:S(2)}) async-start(), calls=%async_computation.1 | async-start | bytes 1253376 | tf_op jit(solution)/shard_map/all_gather | solution.py:12
  7.9 340.3 %all-reduce.3.cloned.1.call-start = ((), (), s32[]{:S(2)}) async-start(), calls=%async_computation | async-start | bytes 1572864 | tf_op jit(solution)/shard_map/psum | solution.py:40
  10.1 64.8 %copy-start.4 = (s32[1024]{0:T(1024)S(1)}, s32[1024]{0:T(1024)}, u32[]{:S(2)}) copy-start(s32[1024]{0:T(1024)} %param.9) | copy-start | bytes 12292
  12.6 66.8 %copy-start.3 = (f32[1024]{0:T(1024)S(1)}, f32[1024]{0:T(1024)}, u32[]{:S(2)}) copy-start(f32[1024]{0:T(1024)} %param.10) | copy-start | bytes 12292
  77.7 1.7 copy-start.1
  79.4 3.6 copy-start.2
Sparse Core Ops, SparseCore 0:
  11.3 63.6 all-gather.2
  81.1 267.0 all-reduce.2

commit v2 on v1

--- a/solution.py
+++ b/solution.py
@@ -2,6 +2,53 @@
 import jax.numpy as jnp
 from jax import lax
 from jax.sharding import PartitionSpec as P
+
+
+def _bits(axis):
+    size = lax.axis_size(axis)
+    count = size.bit_length() - 1
+    assert 1 << count == size
+    return size, count
+
+
+def _exchange(x, axis, size, bit):
+    pairs = [(i, i ^ (1 << bit)) for i in range(size)]
+    return lax.ppermute(x, axis, pairs)
+
+
+def _pick(x, which):
+    return lax.dynamic_index_in_dim(x, which, 0, keepdims=False)
+
+
+def reduce_scatter_bits(x, axis, order):
+    size, _ = _bits(axis)
+    me = lax.axis_index(axis)
+    for bit in order:
+        mine = (me >> bit) & 1
+        keep = _pick(x, mine)
+        send = _pick(x, 1 - mine)
+        x = keep + _exchange(send, axis, size, bit)
+    return x
+
+
+def all_gather_bits(x, axis, order):
+    size, _ = _bits(axis)
+    me = lax.axis_index(axis)
+    for bit in order:
+        mine = (me >> bit) & 1
+        other = _exchange(x, axis, size, bit)
+        x = jnp.where(mine == 0, jnp.stack([x, other]), jnp.stack([other, x]))
+    return x
+
+
+def all_reduce_bits(x, axis):
+    size, count = _bits(axis)
+    tail = x.shape
+    rows = tail[0] >> count
+    parts = x.reshape((2,) * count + (rows,) + tail[1:])
+    order = list(range(count))
+    reduced = reduce_scatter_bits(parts, axis, order)
+    return all_gather_bits(reduced, axis, order[::-1]).reshape(tail)
 
 
 def body(tile_index, weights, electron, strength, spline_table, rotation, inverse):
@@ -9,7 +56,9 @@
     coeffs = weights.shape[1]
     tiles_count = spline_table.shape[0] // coeffs
     electrons = inverse.shape[2]
-    inverse_full = lax.all_gather(inverse[0], "orb", axis=0, tiled=True)
+    _, orb_bits = _bits("orb")
+    inverse_full = all_gather_bits(inverse[0], "orb", list(range(orb_bits)))
+    inverse_full = inverse_full.reshape(-1, electrons)
     onehot = (tile_index[:, None] == jnp.arange(tiles_count, dtype=jnp.int32)[None, :]).astype(
         jnp.bfloat16
     )
@@ -36,8 +85,10 @@
         preferred_element_type=jnp.float32,
     )
     partial_ratio = jnp.sum(orbital_values.astype(jnp.float32) * rotated_columns, axis=1)
-    ratios = lax.psum_scatter(partial_ratio, "orb", scatter_dimension=0, tiled=True)
-    gradient = lax.psum(local_gradient, "walker")
+    share = points >> orb_bits
+    ratio_parts = partial_ratio.reshape((2,) * orb_bits + (share,))
+    ratios = reduce_scatter_bits(ratio_parts, "orb", list(range(orb_bits - 1, -1, -1)))
+    gradient = all_reduce_bits(local_gradient, "walker")
     return (ratios, gradient)
 
 

time: 357 us -> 160 us (0.45)
  the two profiles are of different devices: /device:TPU:4 before, /device:TPU:22 now
where the time goes in v2:
time: 160 us; the launch traced here: 159 us
  starting transfers between devices  81.8 us (51%)
  waiting for transfers between devices  50.9 us (32%)
  other arithmetic  12.7 us (8%)
  matrix products  10.6 us (7%)
  local copies, waits for them, and re-layouts  1.89 us (1%)
    ppermute x18, starting transfers between devices, _exchange(): return lax.ppermute(x, axis, pairs)  81.8 us
    ppermute x18, waiting for transfers between devices, _exchange(): return lax.ppermute(x, axis, pairs)  50.9 us
    dot_general x1, matrix products, body(): jnp.dot(stencil_matrix, spline_table, preferred_element_type=jnp.float32)  5.75 us
    select_n x16, other arithmetic, all_gather_bits(): x = jnp.where(mine == 0, jnp.stack([x, other]), jnp.stack([other, x]))  5.56 us
    mul x1, other arithmetic, body(): onehot[:, :, None] * weights[:, None, :]  4.68 us
  transfers between devices with their start and end apart: 18, of which 13 were waited for; matrix products, arithmetic and copies ran while one was open for 11% of the time, Pallas kernels for 0%

profile of v2, /device:TPU:22, one launch (start us, length us, event | category | flops | bytes accessed | tf_op | source)
XLA Modules:
  0.0 159.0 jit_solution(9182432687622324608)
XLA Ops:
  0.6 2.1 %collective-permute-start = (bf16[48,768]{1,0:T(8,128)(2,1)}, bf16[48,768]{1,0:T(8,128)(2,1)S(1)}, u32[]{:S(2)}, u32[]{:S(2)}) collective-permute-start(bf16[48,768]{1,0:T(8,128)(2,1)} %bitcast.98), channel_id=1, source_target_pairs={{0,1},{1,0},{2,3},{3,2},{4,5},{5,4},{6,7},{7,6},{8,9},{9,8},{10,11... | collective-permute-start | bytes 221192 | tf_op jit(solution)/shard_map/ppermute | solution.py:16
  5.1 2.2 %collective-permute-start.1 = (bf16[2,48,768]{2,1,0:T(8,128)(2,1)S(1)}, bf16[2,48,768]{2,1,0:T(8,128)(2,1)S(1)}, u32[]{:S(2)}, u32[]{:S(2)}) collective-permute-start(bf16[2,48,768]{2,1,0:T(8,128)(2,1)S(1)} %maximum_select_fusion.11), channel_id=1, source_target_pairs={{0,2},{1,3},{2,0},{3,1},{4,6},{5,7},{6,4},{7,5},{8,10},{9,11},{10,... | collective-permute-start | bytes 442376 | tf_op jit(solution)/shard_map/ppermute | solution.py:16
  9.1 5.3 %collective-permute-done.1 = bf16[2,48,768]{2,1,0:T(8,128)(2,1)S(1)} collective-permute-done((bf16[2,48,768]{2,1,0:T(8,128)(2,1)S(1)}, bf16[2,48,768]{2,1,0:T(8,128)(2,1)S(1)}, u32[]{:S(2)}, u32[]{:S(2)}) %collective-permute-start.1) | collective-permute-done | bytes 147488 | tf_op jit(solution)/shard_map/ppermute | solution.py:16
  14.5 2.9 %collective-permute-start.2 = (bf16[2,2,48,768]{3,2,1,0:T(8,128)(2,1)S(1)}, bf16[2,2,48,768]{3,2,1,0:T(8,128)(2,1)S(1)}, u32[]{:S(2)}, u32[]{:S(2)}) collective-permute-start(bf16[2,2,48,768]{3,2,1,0:T(8,128)(2,1)S(1)} %maximum_select_fusion.7), channel_id=1, source_target_pairs={{0,4},{1,5},{2,6},{3,7},{4,0},{5,1},{6,2},{7,3},{8,12},{9,13},{10,... | collective-permute-start | bytes 884744 | tf_op jit(solution)/shard_map/ppermute | solution.py:16
  17.4 4.7 %broadcast_multiply_fusion = bf16[1024,64,64]{0,2,1:T(8,128)(2,1)} fusion(bf16[1024,64]{0,1:T(8,128)(2,1)} %param.8, bf16[1024,64]{0,1:T(8,128)(2,1)S(1)} %fusion.12), kind=kLoop, calls=%fused_computation | loop fusion | flops 4194304 | bytes 8650752 | tf_op jit(solution)/shard_map/mul | solution.py:65
  22.1 2.6 %collective-permute-done.2 = bf16[2,2,48,768]{3,2,1,0:T(8,128)(2,1)S(1)} collective-permute-done((bf16[2,2,48,768]{3,2,1,0:T(8,128)(2,1)S(1)}, bf16[2,2,48,768]{3,2,1,0:T(8,128)(2,1)S(1)}, u32[]{:S(2)}, u32[]{:S(2)}) %collective-permute-start.2) | collective-permute-done | bytes 294944 | tf_op jit(solution)/shard_map/ppermute | solution.py:16
  25.6 4.8 %collective-permute-start.3 = (bf16[2,2,2,48,768]{4,3,2,1,0:T(8,128)(2,1)}, bf16[2,2,2,48,768]{4,3,2,1,0:T(8,128)(2,1)}, u32[]{:S(2)}, u32[]{:S(2)}) collective-permute-start(bf16[2,2,2,48,768]{4,3,2,1,0:T(8,128)(2,1)} %maximum_select_fusion.3), channel_id=1, source_target_pairs={{0,8},{1,9},{2,10},{3,11},{4,12},{5,13},{6,14},{7,15},{8,0},{9,1},... | collective-permute-start | bytes 1769480 | tf_op jit(solution)/shard_map/ppermute | solution.py:16
  30.5 5.8 %convolution_convert_fusion = bf16[1024,256]{0,1:T(8,128)(2,1)S(1)} fusion(bf16[1024,4096]{0,1:T(8,128)(2,1)} %bitcast.83, bf16[4096,256]{1,0:T(8,128)(2,1)S(1)} %copy-done), kind=kOutput, calls=%fused_computation.10 | convolution fusion | flops 2147745792 | bytes 11010048 | tf_op jit(solution)/shard_map/dot_general | solution.py:68
  36.4 6.8 %collective-permute-done.3 = bf16[2,2,2,48,768]{4,3,2,1,0:T(8,128)(2,1)} collective-permute-done((bf16[2,2,2,48,768]{4,3,2,1,0:T(8,128)(2,1)}, bf16[2,2,2,48,768]{4,3,2,1,0:T(8,128)(2,1)}, u32[]{:S(2)}, u32[]{:S(2)}) %collective-permute-start.3) | collective-permute-done | bytes 589856 | tf_op jit(solution)/shard_map/ppermute | solution.py:16
  43.3 1.5 maximum_select_fusion
  44.7 1.5 fusion
  48.7 2.9 %collective-permute-start.8 = (f32[2,2,2,2,8,768]{5,4,3,2,1,0:T(8,128)}, f32[2,2,2,2,8,768]{5,4,3,2,1,0:T(8,128)}, u32[]{:S(2)}, u32[]{:S(2)}) collective-permute-start(f32[2,2,2,2,8,768]{5,4,3,2,1,0:T(8,128)} %dynamic-slice_bitcast_fusion), channel_id=1, source_target_pairs={{0,16},{16,0},{32,48},{48,32},{64,80},{80,64},{96,112},{112,96},{1... | collective-permute-start | bytes 1179656 | tf_op jit(solution)/shard_map/ppermute | solution.py:16
  51.7 2.6 %fusion.9 = f32[1024]{0:T(1024)S(1)} fusion(bf16[256,768]{1,0:T(8,128)(2,1)} %param.12, f32[1024,768]{1,0:T(8,128)} %copy-done.1, bf16[1024,256]{0,1:T(8,128)(2,1)S(1)} %convolution_convert_fusion), kind=kOutput, calls=%fused_computation.11 | convolution fusion | flops 404225024 | bytes 4067328 | tf_op jit(solution)/shard_map/dot_general | solution.py:81
  54.3 4.1 %collective-permute-start.4 = (f32[2,2,2,64]{3,2,1,0:T(2,128)S(1)}, f32[2,2,2,64]{3,2,1,0:T(2,128)S(1)}, u32[]{:S(2)}, u32[]{:S(2)}) collective-permute-start(f32[2,2,2,64]{3,2,1,0:T(2,128)S(1)} %fusion.15), channel_id=1, source_target_pairs={{0,8},{1,9},{2,10},{3,11},{4,12},{5,13},{6,14},{7,15},{8,0},{9,1},... | collective-permute-start | bytes 6152 | tf_op jit(solution)/shard_map/ppermute | solution.py:16
  60.9 3.3 %collective-permute-start.9 = (f32[2,2,2,8,768]{4,3,2,1,0:T(8,128)S(1)}, f32[2,2,2,8,768]{4,3,2,1,0:T(8,128)S(1)}, u32[]{:S(2)}, u32[]{:S(2)}) collective-permute-start(f32[2,2,2,8,768]{4,3,2,1,0:T(8,128)S(1)} %dynamic-slice_bitcast_fusion.1), channel_id=1, source_target_pairs={{0,32},{16,48},{32,0},{48,16},{64,96},{80,112},{96,64},{112,80},{1... | collective-permute-start | bytes 589832 | tf_op jit(solution)/shard_map/ppermute | solution.py:16
  64.2 2.7 %collective-permute-start.5 = (f32[2,2,64]{2,1,0:T(2,128)S(1)}, f32[2,2,64]{2,1,0:T(2,128)S(1)}, u32[]{:S(2)}, u32[]{:S(2)}) collective-permute-start(f32[2,2,64]{2,1,0:T(2,128)S(1)} %fusion.18), channel_id=1, source_target_pairs={{0,4},{1,5},{2,6},{3,7},{4,0},{5,1},{6,2},{7,3},{8,12},{9,13},{10,... | collective-permute-start | bytes 3080 | tf_op jit(solution)/shard_map/ppermute | solution.py:16
  68.5 4.7 %collective-permute-start.10 = (f32[2,2,8,768]{3,2,1,0:T(8,128)S(1)}, f32[2,2,8,768]{3,2,1,0:T(8,128)S(1)}, u32[]{:S(2)}, u32[]{:S(2)}) collective-permute-start(f32[2,2,8,768]{3,2,1,0:T(8,128)S(1)} %dynamic-slice_bitcast_fusion.2), channel_id=1, source_target_pairs={{0,64},{16,80},{32,96},{48,112},{64,0},{80,16},{96,32},{112,48},{1... | collective-permute-start | bytes 294920 | tf_op jit(solution)/shard_map/ppermute | solution.py:16
  73.2 2.7 %collective-permute-done.10 = f32[2,2,8,768]{3,2,1,0:T(8,128)S(1)} collective-permute-done((f32[2,2,8,768]{3,2,1,0:T(8,128)S(1)}, f32[2,2,8,768]{3,2,1,0:T(8,128)S(1)}, u32[]{:S(2)}, u32[]{:S(2)}) %collective-permute-start.10) | collective-permute-done | bytes 98336 | tf_op jit(solution)/shard_map/ppermute | solution.py:16
  75.9 9.0 %collective-permute-start.11 = (f32[2,8,768]{2,1,0:T(8,128)S(1)}, f32[2,8,768]{2,1,0:T(8,128)S(1)}, u32[]{:S(2)}, u32[]{:S(2)}) collective-permute-start(f32[2,8,768]{2,1,0:T(8,128)S(1)} %dynamic-slice_bitcast_fusion.3), channel_id=1, source_target_pairs={{0,128},{16,144},{32,160},{48,176},{64,192},{80,208},{96,224},{112... | collective-permute-start | bytes 147464 | tf_op jit(solution)/shard_map/ppermute | solution.py:16
  84.9 2.2 %collective-permute-start.6 = (f32[2,64]{1,0:T(2,128)S(1)}, f32[2,64]{1,0:T(2,128)S(1)}, u32[]{:S(2)}, u32[]{:S(2)}) collective-permute-start(f32[2,64]{1,0:T(2,128)S(1)} %fusion.21), channel_id=1, source_target_pairs={{0,2},{1,3},{2,0},{3,1},{4,6},{5,7},{6,4},{7,5},{8,10},{9,11},{10,... | collective-permute-start | bytes 1544 | tf_op jit(solution)/shard_map/ppermute | solution.py:16
  87.2 15.5 %collective-permute-start.12 = (f32[8,768]{1,0:T(8,128)S(1)}, f32[8,768]{1,0:T(8,128)S(1)}, u32[]{:S(2)}, u32[]{:S(2)}) collective-permute-start(f32[8,768]{1,0:T(8,128)S(1)} %dynamic-slice_bitcast_fusion.4), channel_id=1, source_target_pairs={{0,256},{16,272},{32,288},{48,304},{64,320},{80,336},{96,352},{112... | collective-permute-start | bytes 73736 | tf_op jit(solution)/shard_map/ppermute | solution.py:16
  102.8 2.0 %collective-permute-done.12 = f32[8,768]{1,0:T(8,128)S(1)} collective-permute-done((f32[8,768]{1,0:T(8,128)S(1)}, f32[8,768]{1,0:T(8,128)S(1)}, u32[]{:S(2)}, u32[]{:S(2)}) %collective-permute-start.12) | collective-permute-done | bytes 24608 | tf_op jit(solution)/shard_map/ppermute | solution.py:16
  104.9 12.4 %collective-permute-start.13 = (f32[8,768]{1,0:T(8,128)S(1)}, f32[8,768]{1,0:T(8,128)S(1)}, u32[]{:S(2)}, u32[]{:S(2)}) collective-permute-start(f32[8,768]{1,0:T(8,128)S(1)} %bitcast_add_fusion.4), channel_id=1, source_target_pairs={{0,256},{16,272},{32,288},{48,304},{64,320},{80,336},{96,352},{112... | collective-permute-start | bytes 73736 | tf_op jit(solution)/shard_map/ppermute | solution.py:16
  117.2 1.9 %collective-permute-start.7 = (f32[64]{0:T(128)S(1)}, f32[64]{0:T(128)S(1)}, u32[]{:S(2)}, u32[]{:S(2)}) collective-permute-start(f32[64]{0:T(128)S(1)} %fusion.24), channel_id=1, source_target_pairs={{0,1},{1,0},{2,3},{3,2},{4,5},{5,4},{6,7},{7,6},{8,9},{9,8},{10,11... | collective-permute-start | bytes 776 | tf_op jit(solution)/shard_map/ppermute | solution.py:16
  119.3 4.4 %collective-permute-start.14 = (f32[2,8,768]{2,1,0:T(8,128)S(1)}, f32[2,8,768]{2,1,0:T(8,128)S(1)}, u32[]{:S(2)}, u32[]{:S(2)}) collective-permute-start(f32[2,8,768]{2,1,0:T(8,128)S(1)} %maximum_select_fusion.15), channel_id=1, source_target_pairs={{0,128},{16,144},{32,160},{48,176},{64,192},{80,208},{96,224},{112... | collective-permute-start | bytes 147464 | tf_op jit(solution)/shard_map/ppermute | solution.py:16
  123.7 7.5 %collective-permute-done.14 = f32[2,8,768]{2,1,0:T(8,128)S(1)} collective-permute-done((f32[2,8,768]{2,1,0:T(8,128)S(1)}, f32[2,8,768]{2,1,0:T(8,128)S(1)}, u32[]{:S(2)}, u32[]{:S(2)}) %collective-permute-start.14) | collective-permute-done | bytes 49184 | tf_op jit(solution)/shard_map/ppermute | solution.py:16
  131.2 1.9 %collective-permute-start.15 = (f32[2,2,8,768]{3,2,1,0:T(8,128)S(1)}, f32[2,2,8,768]{3,2,1,0:T(8,128)S(1)}, u32[]{:S(2)}, u32[]{:S(2)}) collective-permute-start(f32[2,2,8,768]{3,2,1,0:T(8,128)S(1)} %maximum_select_fusion.13), channel_id=1, source_target_pairs={{0,64},{16,80},{32,96},{48,112},{64,0},{80,16},{96,32},{112,48},{1... | collective-permute-start | bytes 294920 | tf_op jit(solution)/shard_map/ppermute | solution.py:16
  133.2 5.6 %collective-permute-done.15 = f32[2,2,8,768]{3,2,1,0:T(8,128)S(1)} collective-permute-done((f32[2,2,8,768]{3,2,1,0:T(8,128)S(1)}, f32[2,2,8,768]{3,2,1,0:T(8,128)S(1)}, u32[]{:S(2)}, u32[]{:S(2)}) %collective-permute-start.15) | collective-permute-done | bytes 98336 | tf_op jit(solution)/shard_map/ppermute | solution.py:16
  138.8 1.9 %collective-permute-start.16 = (f32[2,2,2,8,768]{4,3,2,1,0:T(8,128)S(1)}, f32[2,2,2,8,768]{4,3,2,1,0:T(8,128)S(1)}, u32[]{:S(2)}, u32[]{:S(2)}) collective-permute-start(f32[2,2,2,8,768]{4,3,2,1,0:T(8,128)S(1)} %maximum_select_fusion.9), channel_id=1, source_target_pairs={{0,32},{16,48},{32,0},{48,16},{64,96},{80,112},{96,64},{112,80},{1... | collective-permute-start | bytes 589832 | tf_op jit(solution)/shard_map/ppermute | solution.py:16
  140.8 5.9 %collective-permute-done.16 = f32[2,2,2,8,768]{4,3,2,1,0:T(8,128)S(1)} collective-permute-done((f32[2,2,2,8,768]{4,3,2,1,0:T(8,128)S(1)}, f32[2,2,2,8,768]{4,3,2,1,0:T(8,128)S(1)}, u32[]{:S(2)}, u32[]{:S(2)}) %collective-permute-start.16) | collective-permute-done | bytes 196640 | tf_op jit(solution)/shard_map/ppermute | solution.py:16
  146.8 2.7 %collective-permute-start.17 = (f32[2,2,2,2,8,768]{5,4,3,2,1,0:T(8,128)S(1)}, f32[2,2,2,2,8,768]{5,4,3,2,1,0:T(8,128)S(1)}, u32[]{:S(2)}, u32[]{:S(2)}) collective-permute-start(f32[2,2,2,2,8,768]{5,4,3,2,1,0:T(8,128)S(1)} %maximum_select_fusion.5), channel_id=1, source_target_pairs={{0,16},{16,0},{32,48},{48,32},{64,80},{80,64},{96,112},{112,96},{1... | collective-permute-start | bytes 1179656 | tf_op jit(solution)/shard_map/ppermute | solution.py:16
  150.0 8.0 %collective-permute-done.17 = f32[2,2,2,2,8,768]{5,4,3,2,1,0:T(8,128)S(1)} collective-permute-done((f32[2,2,2,2,8,768]{5,4,3,2,1,0:T(8,128)S(1)}, f32[2,2,2,2,8,768]{5,4,3,2,1,0:T(8,128)S(1)}, u32[]{:S(2)}, u32[]{:S(2)}) %collective-permute-start.17) | collective-permute-done | bytes 393248 | tf_op jit(solution)/shard_map/ppermute | solution.py:16
  (60 shorter events, 13.5 us)
Async XLA Ops:
  0.6 29.8 %copy-start = (bf16[4096,256]{1,0:T(8,128)(2,1)S(1)}, bf16[4096,256]{1,0:T(8,128)(2,1)}, u32[]{:S(2)}) copy-start(bf16[4096,256]{1,0:T(8,128)(2,1)} %param.11) | copy-start | bytes 6291460
  0.6 3.5 %collective-permute-start = (bf16[48,768]{1,0:T(8,128)(2,1)}, bf16[48,768]{1,0:T(8,128)(2,1)S(1)}, u32[]{:S(2)}, u32[]{:S(2)}) collective-permute-start(bf16[48,768]{1,0:T(8,128)(2,1)} %bitcast.98), channel_id=1, source_target_pairs={{0,1},{1,0},{2,3},{3,2},{4,5},{5,4},{6,7},{7,6},{8,9},{9,8},{10,11... | collective-permute-start | bytes 221192 | tf_op jit(solution)/shard_map/ppermute | solution.py:16
  5.1 9.3 %collective-permute-start.1 = (bf16[2,48,768]{2,1,0:T(8,128)(2,1)S(1)}, bf16[2,48,768]{2,1,0:T(8,128)(2,1)S(1)}, u32[]{:S(2)}, u32[]{:S(2)}) collective-permute-start(bf16[2,48,768]{2,1,0:T(8,128)(2,1)S(1)} %maximum_select_fusion.11), channel_id=1, source_target_pairs={{0,2},{1,3},{2,0},{3,1},{4,6},{5,7},{6,4},{7,5},{8,10},{9,11},{10,... | collective-permute-start | bytes 442376 | tf_op jit(solution)/shard_map/ppermute | solution.py:16
  14.5 7.6 %copy-start.2 = (bf16[1,48,768]{2,1,0:T(8,128)(2,1)S(1)}, bf16[1,48,768]{2,1,0:T(8,128)(2,1)}, u32[]{:S(2)}) copy-start(bf16[1,48,768]{2,1,0:T(8,128)(2,1)} %param.13) | copy-start | bytes 221188
  14.5 10.2 %collective-permute-start.2 = (bf16[2,2,48,768]{3,2,1,0:T(8,128)(2,1)S(1)}, bf16[2,2,48,768]{3,2,1,0:T(8,128)(2,1)S(1)}, u32[]{:S(2)}, u32[]{:S(2)}) collective-permute-start(bf16[2,2,48,768]{3,2,1,0:T(8,128)(2,1)S(1)} %maximum_select_fusion.7), channel_id=1, source_target_pairs={{0,4},{1,5},{2,6},{3,7},{4,0},{5,1},{6,2},{7,3},{8,12},{9,13},{10,... | collective-permute-start | bytes 884744 | tf_op jit(solution)/shard_map/ppermute | solution.py:16
  25.6 17.6 %collective-permute-start.3 = (bf16[2,2,2,48,768]{4,3,2,1,0:T(8,128)(2,1)}, bf16[2,2,2,48,768]{4,3,2,1,0:T(8,128)(2,1)}, u32[]{:S(2)}, u32[]{:S(2)}) collective-permute-start(bf16[2,2,2,48,768]{4,3,2,1,0:T(8,128)(2,1)} %maximum_select_fusion.3), channel_id=1, source_target_pairs={{0,8},{1,9},{2,10},{3,11},{4,12},{5,13},{6,14},{7,15},{8,0},{9,1},... | collective-permute-start | bytes 1769480 | tf_op jit(solution)/shard_map/ppermute | solution.py:16
  36.2 8.5 %copy-start.4 = (s32[1024]{0:T(1024)S(1)}, s32[1024]{0:T(1024)}, u32[]{:S(2)}) copy-start(s32[1024]{0:T(1024)} %param.9) | copy-start | bytes 12292
  44.7 1.6 copy-start.3
  46.3 1.7 %copy-start.1 = (f32[1024,768]{1,0:T(8,128)}, f32[1024,768]{1,0:T(8,128)S(1)}, u32[]{:S(2)}) copy-start(f32[1024,768]{1,0:T(8,128)S(1)} %fusion) | copy-start | bytes 9437188
  48.7 11.1 %collective-permute-start.8 = (f32[2,2,2,2,8,768]{5,4,3,2,1,0:T(8,128)}, f32[2,2,2,2,8,768]{5,4,3,2,1,0:T(8,128)}, u32[]{:S(2)}, u32[]{:S(2)}) collective-permute-start(f32[2,2,2,2,8,768]{5,4,3,2,1,0:T(8,128)} %dynamic-slice_bitcast_fusion), channel_id=1, source_target_pairs={{0,16},{16,0},{32,48},{48,32},{64,80},{80,64},{96,112},{112,96},{1... | collective-permute-start | bytes 1179656 | tf_op jit(solution)/shard_map/ppermute | solution.py:16
  54.3 9.9 %collective-permute-start.4 = (f32[2,2,2,64]{3,2,1,0:T(2,128)S(1)}, f32[2,2,2,64]{3,2,1,0:T(2,128)S(1)}, u32[]{:S(2)}, u32[]{:S(2)}) collective-permute-start(f32[2,2,2,64]{3,2,1,0:T(2,128)S(1)} %fusion.15), channel_id=1, source_target_pairs={{0,8},{1,9},{2,10},{3,11},{4,12},{5,13},{6,14},{7,15},{8,0},{9,1},... | collective-permute-start | bytes 6152 | tf_op jit(solution)/shard_map/ppermute | solution.py:16
  60.9 7.6 %collective-permute-start.9 = (f32[2,2,2,8,768]{4,3,2,1,0:T(8,128)S(1)}, f32[2,2,2,8,768]{4,3,2,1,0:T(8,128)S(1)}, u32[]{:S(2)}, u32[]{:S(2)}) collective-permute-start(f32[2,2,2,8,768]{4,3,2,1,0:T(8,128)S(1)} %dynamic-slice_bitcast_fusion.1), channel_id=1, source_target_pairs={{0,32},{16,48},{32,0},{48,16},{64,96},{80,112},{96,64},{112,80},{1... | collective-permute-start | bytes 589832 | tf_op jit(solution)/shard_map/ppermute | solution.py:16
  64.2 8.9 %collective-permute-start.5 = (f32[2,2,64]{2,1,0:T(2,128)S(1)}, f32[2,2,64]{2,1,0:T(2,128)S(1)}, u32[]{:S(2)}, u32[]{:S(2)}) collective-permute-start(f32[2,2,64]{2,1,0:T(2,128)S(1)} %fusion.18), channel_id=1, source_target_pairs={{0,4},{1,5},{2,6},{3,7},{4,0},{5,1},{6,2},{7,3},{8,12},{9,13},{10,... | collective-permute-start | bytes 3080 | tf_op jit(solution)/shard_map/ppermute | solution.py:16
  68.5 7.4 %collective-permute-start.10 = (f32[2,2,8,768]{3,2,1,0:T(8,128)S(1)}, f32[2,2,8,768]{3,2,1,0:T(8,128)S(1)}, u32[]{:S(2)}, u32[]{:S(2)}) collective-permute-start(f32[2,2,8,768]{3,2,1,0:T(8,128)S(1)} %dynamic-slice_bitcast_fusion.2), channel_id=1, source_target_pairs={{0,64},{16,80},{32,96},{48,112},{64,0},{80,16},{96,32},{112,48},{1... | collective-permute-start | bytes 294920 | tf_op jit(solution)/shard_map/ppermute | solution.py:16
  75.9 11.3 %collective-permute-start.11 = (f32[2,8,768]{2,1,0:T(8,128)S(1)}, f32[2,8,768]{2,1,0:T(8,128)S(1)}, u32[]{:S(2)}, u32[]{:S(2)}) collective-permute-start(f32[2,8,768]{2,1,0:T(8,128)S(1)} %dynamic-slice_bitcast_fusion.3), channel_id=1, source_target_pairs={{0,128},{16,144},{32,160},{48,176},{64,192},{80,208},{96,224},{112... | collective-permute-start | bytes 147464 | tf_op jit(solution)/shard_map/ppermute | solution.py:16
  84.9 17.9 %collective-permute-start.6 = (f32[2,64]{1,0:T(2,128)S(1)}, f32[2,64]{1,0:T(2,128)S(1)}, u32[]{:S(2)}, u32[]{:S(2)}) collective-permute-start(f32[2,64]{1,0:T(2,128)S(1)} %fusion.21), channel_id=1, source_target_pairs={{0,2},{1,3},{2,0},{3,1},{4,6},{5,7},{6,4},{7,5},{8,10},{9,11},{10,... | collective-permute-start | bytes 1544 | tf_op jit(solution)/shard_map/ppermute | solution.py:16
  87.2 17.6 %collective-permute-start.12 = (f32[8,768]{1,0:T(8,128)S(1)}, f32[8,768]{1,0:T(8,128)S(1)}, u32[]{:S(2)}, u32[]{:S(2)}) collective-permute-start(f32[8,768]{1,0:T(8,128)S(1)} %dynamic-slice_bitcast_fusion.4), channel_id=1, source_target_pairs={{0,256},{16,272},{32,288},{48,304},{64,320},{80,336},{96,352},{112... | collective-permute-start | bytes 73736 | tf_op jit(solution)/shard_map/ppermute | solution.py:16
  104.9 14.4 %collective-permute-start.13 = (f32[8,768]{1,0:T(8,128)S(1)}, f32[8,768]{1,0:T(8,128)S(1)}, u32[]{:S(2)}, u32[]{:S(2)}) collective-permute-start(f32[8,768]{1,0:T(8,128)S(1)} %bitcast_add_fusion.4), channel_id=1, source_target_pairs={{0,256},{16,272},{32,288},{48,304},{64,320},{80,336},{96,352},{112... | collective-permute-start | bytes 73736 | tf_op jit(solution)/shard_map/ppermute | solution.py:16
  117.2 32.2 %collective-permute-start.7 = (f32[64]{0:T(128)S(1)}, f32[64]{0:T(128)S(1)}, u32[]{:S(2)}, u32[]{:S(2)}) collective-permute-start(f32[64]{0:T(128)S(1)} %fusion.24), channel_id=1, source_target_pairs={{0,1},{1,0},{2,3},{3,2},{4,5},{5,4},{6,7},{7,6},{8,9},{9,8},{10,11... | collective-permute-start | bytes 776 | tf_op jit(solution)/shard_map/ppermute | solution.py:16
  119.3 11.9 %collective-permute-start.14 = (f32[2,8,768]{2,1,0:T(8,128)S(1)}, f32[2,8,768]{2,1,0:T(8,128)S(1)}, u32[]{:S(2)}, u32[]{:S(2)}) collective-permute-start(f32[2,8,768]{2,1,0:T(8,128)S(1)} %maximum_select_fusion.15), channel_id=1, source_target_pairs={{0,128},{16,144},{32,160},{48,176},{64,192},{80,208},{96,224},{112... | collective-permute-start | bytes 147464 | tf_op jit(solution)/shard_map/ppermute | solution.py:16
  131.2 7.6 %collective-permute-start.15 = (f32[2,2,8,768]{3,2,1,0:T(8,128)S(1)}, f32[2,2,8,768]{3,2,1,0:T(8,128)S(1)}, u32[]{:S(2)}, u32[]{:S(2)}) collective-permute-start(f32[2,2,8,768]{3,2,1,0:T(8,128)S(1)} %maximum_select_fusion.13), channel_id=1, source_target_pairs={{0,64},{16,80},{32,96},{48,112},{64,0},{80,16},{96,32},{112,48},{1... | collective-permute-start | bytes 294920 | tf_op jit(solution)/shard_map/ppermute | solution.py:16
  138.8 7.9 %collective-permute-start.16 = (f32[2,2,2,8,768]{4,3,2,1,0:T(8,128)S(1)}, f32[2,2,2,8,768]{4,3,2,1,0:T(8,128)S(1)}, u32[]{:S(2)}, u32[]{:S(2)}) collective-permute-start(f32[2,2,2,8,768]{4,3,2,1,0:T(8,128)S(1)} %maximum_select_fusion.9), channel_id=1, source_target_pairs={{0,32},{16,48},{32,0},{48,16},{64,96},{80,112},{96,64},{112,80},{1... | collective-permute-start | bytes 589832 | tf_op jit(solution)/shard_map/ppermute | solution.py:16
  146.8 11.3 %collective-permute-start.17 = (f32[2,2,2,2,8,768]{5,4,3,2,1,0:T(8,128)S(1)}, f32[2,2,2,2,8,768]{5,4,3,2,1,0:T(8,128)S(1)}, u32[]{:S(2)}, u32[]{:S(2)}) collective-permute-start(f32[2,2,2,2,8,768]{5,4,3,2,1,0:T(8,128)S(1)} %maximum_select_fusion.5), channel_id=1, source_target_pairs={{0,16},{16,0},{32,48},{48,32},{64,80},{80,64},{96,112},{112,96},{1... | collective-permute-start | bytes 1179656 | tf_op jit(solution)/shard_map/ppermute | solution.py:16

commit v3 on v2

--- a/solution.py
+++ b/solution.py
@@ -51,14 +51,25 @@
     return all_gather_bits(reduced, axis, order[::-1]).reshape(tail)
 
 
+def gather_by_all_to_all(x, axis):
+    size = lax.axis_size(axis)
+    copies = jnp.broadcast_to(x[None], (size,) + x.shape)
+    return lax.all_to_all(copies, axis, 0, 0, tiled=True)
+
+
+def reduce_scatter_by_all_to_all(x, axis):
+    size = lax.axis_size(axis)
+    parts = x.reshape((size, x.shape[0] // size) + x.shape[1:])
+    return jnp.sum(lax.all_to_all(parts, axis, 0, 0, tiled=True), axis=0)
+
+
 def body(tile_index, weights, electron, strength, spline_table, rotation, inverse):
     points = tile_index.shape[0]
     coeffs = weights.shape[1]
     tiles_count = spline_table.shape[0] // coeffs
     electrons = inverse.shape[2]
     _, orb_bits = _bits("orb")
-    inverse_full = all_gather_bits(inverse[0], "orb", list(range(orb_bits)))
-    inverse_full = inverse_full.reshape(-1, electrons)
+    inverse_full = gather_by_all_to_all(inverse[0], "orb").reshape(-1, electrons)
     onehot = (tile_index[:, None] == jnp.arange(tiles_count, dtype=jnp.int32)[None, :]).astype(
         jnp.bfloat16
     )
@@ -85,10 +96,9 @@
         preferred_element_type=jnp.float32,
     )
     partial_ratio = jnp.sum(orbital_values.astype(jnp.float32) * rotated_columns, axis=1)
-    share = points >> orb_bits
-    ratio_parts = partial_ratio.reshape((2,) * orb_bits + (share,))
-    ratios = reduce_scatter_bits(ratio_parts, "orb", list(range(orb_bits - 1, -1, -1)))
-    gradient = all_reduce_bits(local_gradient, "walker")
+    ratios = reduce_scatter_by_all_to_all(partial_ratio, "orb")
+    reduced = reduce_scatter_by_all_to_all(local_gradient, "walker")
+    gradient = gather_by_all_to_all(reduced, "walker").reshape(local_gradient.shape)
     return (ratios, gradient)
 
 

time: 160 us -> 157 us (0.981)
  the two profiles are of different devices: /device:TPU:22 before, /device:TPU:8 now
where the time goes in v3:
time: 157 us
  waiting for transfers between devices  108 us (69%)
  starting transfers between devices  31.3 us (20%)
  matrix products  9.38 us (6%)
  local copies, waits for them, and re-layouts  6.3 us (4%)
    all_to_all x2, waiting for transfers between devices, gather_by_all_to_all(): return lax.all_to_all(copies, axis, 0, 0, tiled=True)  60.3 us
    all_to_all x2, waiting for transfers between devices, reduce_scatter_by_all_to_all(): return jnp.sum(lax.all_to_all(parts, axis, 0, 0, tiled=True), axis=0)  47.8 us
    all_to_all x2, starting transfers between devices, reduce_scatter_by_all_to_all(): return jnp.sum(lax.all_to_all(parts, axis, 0, 0, tiled=True), axis=0)  20.1 us
    all_to_all x2, starting transfers between devices, gather_by_all_to_all(): return lax.all_to_all(copies, axis, 0, 0, tiled=True)  11.2 us
  transfers between devices with their start and end apart: 4, of which 4 were waited for; matrix products, arithmetic and copies ran while one was open for 4% of the time, Pallas kernels for 0%

profile of v3, /device:TPU:8, one launch (start us, length us, event | category | flops | bytes accessed | tf_op | source)
XLA Modules:
  0.0 157.0 jit_solution(16172814718964203103)
XLA Ops:
  0.6 0.0 copy-start
  0.6 0.0 copy-start.4
  0.7 0.0 copy-start.2
  0.7 2.1 %broadcast_in_dim.7 = bf16[16,48,768]{2,1,0:T(8,128)(2,1)} broadcast(bf16[48,768]{1,0:T(8,128)(2,1)} %bitcast.14), dimensions={1,2} | broadcast | bytes 1253376 | tf_op jit(solution)/shard_map/broadcast_in_dim | solution.py:56
  2.8 6.2 %all-to-all-start = ((bf16[16,48,768]{2,1,0:T(8,128)(2,1)}), bf16[16,48,768]{2,1,0:T(8,128)(2,1)}, u32[]{:S(2)}, u32[]{:S(2)}) async-start(bf16[16,48,768]{2,1,0:T(8,128)(2,1)} %broadcast_in_dim.7), calls=%async_computation | async-start | bytes 2359296 | tf_op jit(solution)/shard_map/all_to_all | solution.py:57
  9.0 0.0 copy-done.4
  9.0 0.0 copy-done.2
  9.0 0.6 broadcast_multiply_fusion
  9.6 0.0 copy-done
  9.6 0.0 copy-start.5
  9.6 2.4 %convolution_convert_fusion = bf16[1024,256]{0,1:T(8,128)(2,1)S(1)} fusion(bf16[1024,4096]{0,1:T(8,128)(2,1)S(1)} %bitcast.12, bf16[4096,256]{1,0:T(8,128)(2,1)S(1)} %copy-done), kind=kOutput, calls=%fused_computation.11 | convolution fusion | flops 2147745792 | bytes 11010048 | tf_op jit(solution)/shard_map/dot_general | solution.py:79
  12.0 16.4 %all-to-all-done = bf16[16,48,768]{2,1,0:T(8,128)(2,1)} async-done(((bf16[16,48,768]{2,1,0:T(8,128)(2,1)}), bf16[16,48,768]{2,1,0:T(8,128)(2,1)}, u32[]{:S(2)}, u32[]{:S(2)}) %all-to-all-start) | async-done | bytes 1179680 | tf_op jit(solution)/shard_map/all_to_all | solution.py:57
  28.4 0.0 copy-done.5
  28.4 0.0 copy-start.3
  28.4 2.8 %fusion = f32[1024,768]{1,0:T(8,128)S(1)} fusion(bf16[768,768]{1,0:T(8,128)(2,1)} %bitcast.2, s32[1024]{0:T(1024)S(1)} %copy-done.5), kind=kOutput, calls=%fused_computation.3 | convolution fusion | flops 1208745984 | bytes 4329472 | tf_op jit(solution)/shard_map/dot_general | solution.py:85
  31.2 0.0 copy-start.1
  31.2 1.6 %copy-done.1 = f32[1024,768]{1,0:T(8,128)} copy-done((f32[1024,768]{1,0:T(8,128)}, f32[1024,768]{1,0:T(8,128)S(1)}, u32[]{:S(2)}) %copy-start.1) | copy-done | bytes 3145752
  32.9 0.0 copy-done.3
  32.9 1.6 %fusion.9 = f32[32,8,768]{2,1,0:T(8,128)} fusion(bf16[1024,256]{0,1:T(8,128)(2,1)S(1)} %convolution_convert_fusion, f32[1024,768]{1,0:T(8,128)S(1)} %fusion, f32[1024]{0:T(1024)S(1)} %copy-done.3), kind=kOutput, calls=%fused_computation.10 | convolution fusion | flops 404226048 | bytes 4460544 | tf_op jit(solution)/shard_map/dot_general | solution.py:89
  34.5 16.7 %all-to-all-start.2 = ((f32[32,8,768]{2,1,0:T(8,128)}), f32[32,8,768]{2,1,0:T(8,128)S(1)}, u32[]{:S(2)}, u32[]{:S(2)}) async-start(f32[32,8,768]{2,1,0:T(8,128)} %fusion.9), calls=%async_computation.2 | async-start | bytes 1572864 | tf_op jit(solution)/shard_map/all_to_all | solution.py:63
  51.2 2.6 %fusion.10 = f32[1024]{0:T(1024)S(1)} fusion(bf16[256,768]{1,0:T(8,128)(2,1)} %param.12, f32[1024,768]{1,0:T(8,128)} %copy-done.1, bf16[1024,256]{0,1:T(8,128)(2,1)S(1)} %convolution_convert_fusion), kind=kOutput, calls=%fused_computation.12 | convolution fusion | flops 404225024 | bytes 4067328 | tf_op jit(solution)/shard_map/dot_general | solution.py:92
  53.8 0.7 all_to_all.16
  54.5 40.3 %all-to-all-done.2 = f32[32,8,768]{2,1,0:T(8,128)S(1)} async-done(((f32[32,8,768]{2,1,0:T(8,128)}), f32[32,8,768]{2,1,0:T(8,128)S(1)}, u32[]{:S(2)}, u32[]{:S(2)}) %all-to-all-start.2) | async-done | bytes 786464 | tf_op jit(solution)/shard_map/all_to_all | solution.py:63
  94.8 3.4 %all-to-all-start.1 = ((f32[16,1,64]{2,1,0:T(1,128)}), f32[16,1,64]{2,1,0:T(1,128)S(1)}, u32[]{:S(2)}, u32[]{:S(2)}) async-start(f32[16,1,64]{2,1,0:T(1,128)} %all_to_all.16), calls=%async_computation.1 | async-start | bytes 16384 | tf_op jit(solution)/shard_map/all_to_all | solution.py:63
  98.2 0.1 reduce_sum.29
  98.2 7.5 %all-to-all-done.1 = f32[16,1,64]{2,1,0:T(1,128)S(1)} async-done(((f32[16,1,64]{2,1,0:T(1,128)}), f32[16,1,64]{2,1,0:T(1,128)S(1)}, u32[]{:S(2)}, u32[]{:S(2)}) %all-to-all-start.1) | async-done | bytes 4128 | tf_op jit(solution)/shard_map/all_to_all | solution.py:63
  105.7 0.9 broadcast_in_dim.8
  106.6 5.0 %all-to-all-start.3 = ((f32[32,8,768]{2,1,0:T(8,128)}), f32[32,8,768]{2,1,0:T(8,128)S(1)}, u32[]{:S(2)}, u32[]{:S(2)}) async-start(f32[32,8,768]{2,1,0:T(8,128)} %broadcast_in_dim.8), calls=%async_computation.3 | async-start | bytes 1572864 | tf_op jit(solution)/shard_map/all_to_all | solution.py:57
  111.6 0.5 reduce_sum.28
  112.2 43.9 %all-to-all-done.3 = f32[32,8,768]{2,1,0:T(8,128)S(1)} async-done(((f32[32,8,768]{2,1,0:T(8,128)}), f32[32,8,768]{2,1,0:T(8,128)S(1)}, u32[]{:S(2)}, u32[]{:S(2)}) %all-to-all-start.3) | async-done | bytes 786464 | tf_op jit(solution)/shard_map/all_to_all | solution.py:57
  156.1 0.9 copy.12
  (1 shorter events, 0.0 us)
Async XLA Ops:
  0.6 9.0 %copy-start = (bf16[4096,256]{1,0:T(8,128)(2,1)S(1)}, bf16[4096,256]{1,0:T(8,128)(2,1)}, u32[]{:S(2)}) copy-start(bf16[4096,256]{1,0:T(8,128)(2,1)} %param.11) | copy-start | bytes 6291460
  0.6 8.4 %copy-start.4 = (s32[1024]{0:T(1024)S(1)}, s32[1024]{0:T(1024)}, u32[]{:S(2)}) copy-start(s32[1024]{0:T(1024)} %param.7) | copy-start | bytes 12292
  0.7 8.4 %copy-start.2 = (bf16[1024,64]{0,1:T(8,128)(2,1)S(1)}, bf16[1024,64]{0,1:T(8,128)(2,1)}, u32[]{:S(2)}) copy-start(bf16[1024,64]{0,1:T(8,128)(2,1)} %param.8) | copy-start | bytes 393220
  2.8 25.6 %all-to-all-start = ((bf16[16,48,768]{2,1,0:T(8,128)(2,1)}), bf16[16,48,768]{2,1,0:T(8,128)(2,1)}, u32[]{:S(2)}, u32[]{:S(2)}) async-start(bf16[16,48,768]{2,1,0:T(8,128)(2,1)} %broadcast_in_dim.7), calls=%async_computation | async-start | bytes 2359296 | tf_op jit(solution)/shard_map/all_to_all | solution.py:57
  9.6 18.8 %copy-start.5 = (s32[1024]{0:T(1024)S(1)}, s32[1024]{0:T(1024)}, u32[]{:S(2)}) copy-start(s32[1024]{0:T(1024)} %param.9) | copy-start | bytes 12292
  28.4 4.5 %copy-start.3 = (f32[1024]{0:T(1024)S(1)}, f32[1024]{0:T(1024)}, u32[]{:S(2)}) copy-start(f32[1024]{0:T(1024)} %param.10) | copy-start | bytes 12292
  31.2 1.7 %copy-start.1 = (f32[1024,768]{1,0:T(8,128)}, f32[1024,768]{1,0:T(8,128)S(1)}, u32[]{:S(2)}) copy-start(f32[1024,768]{1,0:T(8,128)S(1)} %fusion) | copy-start | bytes 9437188
  34.5 60.3 %all-to-all-start.2 = ((f32[32,8,768]{2,1,0:T(8,128)}), f32[32,8,768]{2,1,0:T(8,128)S(1)}, u32[]{:S(2)}, u32[]{:S(2)}) async-start(f32[32,8,768]{2,1,0:T(8,128)} %fusion.9), calls=%async_computation.2 | async-start | bytes 1572864 | tf_op jit(solution)/shard_map/all_to_all | solution.py:63
  94.8 10.9 %all-to-all-start.1 = ((f32[16,1,64]{2,1,0:T(1,128)}), f32[16,1,64]{2,1,0:T(1,128)S(1)}, u32[]{:S(2)}, u32[]{:S(2)}) async-start(f32[16,1,64]{2,1,0:T(1,128)} %all_to_all.16), calls=%async_computation.1 | async-start | bytes 16384 | tf_op jit(solution)/shard_map/all_to_all | solution.py:63
  106.6 49.4 %all-to-all-start.3 = ((f32[32,8,768]{2,1,0:T(8,128)}), f32[32,8,768]{2,1,0:T(8,128)S(1)}, u32[]{:S(2)}, u32[]{:S(2)}) async-start(f32[32,8,768]{2,1,0:T(8,128)} %broadcast_in_dim.8), calls=%async_computation.3 | async-start | bytes 1572864 | tf_op jit(solution)/shard_map/all_to_all | solution.py:57

commit v4 on v3

--- a/solution.py
+++ b/solution.py
@@ -1,7 +1,7 @@
 import jax
 import jax.numpy as jnp
 from jax import lax
-from jax.sharding import PartitionSpec as P
+from jax.sharding import Mesh, PartitionSpec as P
 
 
 def _bits(axis):
@@ -51,6 +51,17 @@
     return all_gather_bits(reduced, axis, order[::-1]).reshape(tail)
 
 
+def all_reduce_walker(x):
+    me = lax.axis_index("wy")
+    halves = x.reshape((2, x.shape[0] // 2) + x.shape[1:])
+    keep = _pick(halves, me)
+    half = keep + lax.ppermute(_pick(halves, 1 - me), "wy", [(0, 1), (1, 0)])
+    reduced = reduce_scatter_by_all_to_all(half, "wz")
+    half = gather_by_all_to_all(reduced, "wz").reshape(half.shape)
+    other = lax.ppermute(half, "wy", [(0, 1), (1, 0)])
+    return jnp.where(me == 0, jnp.stack([half, other]), jnp.stack([other, half])).reshape(x.shape)
+
+
 def gather_by_all_to_all(x, axis):
     size = lax.axis_size(axis)
     copies = jnp.broadcast_to(x[None], (size,) + x.shape)
@@ -97,20 +108,24 @@
     )
     partial_ratio = jnp.sum(orbital_values.astype(jnp.float32) * rotated_columns, axis=1)
     ratios = reduce_scatter_by_all_to_all(partial_ratio, "orb")
-    reduced = reduce_scatter_by_all_to_all(local_gradient, "walker")
-    gradient = gather_by_all_to_all(reduced, "walker").reshape(local_gradient.shape)
+    gradient = all_reduce_walker(local_gradient)
     return (ratios, gradient)
 
 
 def solution(mesh):
+    sizes = dict(mesh.shape)
+    split = Mesh(
+        mesh.devices.reshape(sizes["walker"] // 2, 2, sizes["orb"]), ("wz", "wy", "orb")
+    )
+    walker = ("wz", "wy")
     in_specs = (
-        P("walker"),
-        P("walker", None),
-        P("walker"),
-        P("walker"),
+        P(walker),
+        P(walker, None),
+        P(walker),
+        P(walker),
         P(None, "orb"),
         P("orb", None),
-        P("walker", "orb", None),
+        P(walker, "orb", None),
     )
-    out_specs = (P(("walker", "orb")), P("orb", None))
-    return jax.shard_map(body, mesh=mesh, in_specs=in_specs, out_specs=out_specs, check_vma=False)
+    out_specs = (P(walker + ("orb",)), P("orb", None))
+    return jax.shard_map(body, mesh=split, in_specs=in_specs, out_specs=out_specs, check_vma=False)

time: 157 us -> 138 us (0.88)
  the two profiles are of different devices: /device:TPU:8 before, /device:TPU:1 now
where the time goes in v4:
time: 138 us; the launch traced here: 137 us
  blocking collectives  57.8 us (42%)
  starting transfers between devices  29.2 us (21%)
  waiting for transfers between devices  26 us (19%)
  matrix products  11.9 us (9%)
  other arithmetic  6.35 us (5%)
  local copies, waits for them, and re-layouts  5.28 us (4%)
    all_to_all x1, blocking collectives, reduce_scatter_by_all_to_all(): return jnp.sum(lax.all_to_all(parts, axis, 0, 0, tiled=True), axis=0)  30.2 us
    all_to_all x1, blocking collectives, gather_by_all_to_all(): return lax.all_to_all(copies, axis, 0, 0, tiled=True)  27.6 us
    all_to_all x1, starting transfers between devices, reduce_scatter_by_all_to_all(): return jnp.sum(lax.all_to_all(parts, axis, 0, 0, tiled=True), axis=0)  14.1 us
    all_to_all x1, starting transfers between devices, gather_by_all_to_all(): return lax.all_to_all(copies, axis, 0, 0, tiled=True)  11 us
    ppermute x1, waiting for transfers between devices, all_reduce_walker(): half = keep + lax.ppermute(_pick(halves, 1 - me), 'wy', [(0, 1), (1, 0)])  9.98 us
    all_to_all x1, waiting for transfers between devices, gather_by_all_to_all(): return lax.all_to_all(copies, axis, 0, 0, tiled=True)  9.07 us
    all_to_all x1, waiting for transfers between devices, reduce_scatter_by_all_to_all(): return jnp.sum(lax.all_to_all(parts, axis, 0, 0, tiled=True), axis=0)  6.95 us
    dot_general x1, matrix products, body(): jnp.dot(stencil_matrix, spline_table, preferred_element_type=jnp.float32)  5.76 us
  transfers between devices with their start and end apart: 4, of which 3 were waited for; matrix products, arithmetic and copies ran while one was open for 9% of the time, Pallas kernels for 0%

profile of v4, /device:TPU:1, one launch (start us, length us, event | category | flops | bytes accessed | tf_op | source)
XLA Modules:
  0.0 137.3 jit_solution(9180314671315109964)
XLA Ops:
  0.6 0.0 copy-start
  0.6 0.0 copy-start.4
  0.7 0.0 copy-start.2
  0.7 2.1 %broadcast_in_dim.7 = bf16[16,48,768]{2,1,0:T(8,128)(2,1)} broadcast(bf16[48,768]{1,0:T(8,128)(2,1)} %bitcast.29), dimensions={1,2} | broadcast | bytes 1253376 | tf_op jit(solution)/shard_map/broadcast_in_dim | solution.py:67
  2.8 11.0 %all-to-all-start = ((bf16[16,48,768]{2,1,0:T(8,128)(2,1)}), bf16[16,48,768]{2,1,0:T(8,128)(2,1)}, u32[]{:S(2)}, u32[]{:S(2)}) async-start(bf16[16,48,768]{2,1,0:T(8,128)(2,1)} %broadcast_in_dim.7), calls=%async_computation | async-start | bytes 2359296 | tf_op jit(solution)/shard_map/all_to_all | solution.py:68
  13.8 0.0 copy-done.4
  13.8 0.0 copy-done.2
  13.8 3.8 %broadcast_multiply_fusion = bf16[1024,64,64]{0,2,1:T(8,128)(2,1)} fusion(bf16[1024,64]{0,1:T(8,128)(2,1)S(1)} %copy-done.2, bf16[1024,64]{0,1:T(8,128)(2,1)S(1)} %fusion.13), kind=kLoop, calls=%fused_computation | loop fusion | flops 4194304 | bytes 8650752 | tf_op jit(solution)/shard_map/mul | solution.py:87
  17.6 0.0 copy-done
  17.6 0.0 copy-start.5
  17.6 5.8 %convolution_convert_fusion = bf16[1024,256]{0,1:T(8,128)(2,1)S(1)} fusion(bf16[1024,4096]{0,1:T(8,128)(2,1)} %bitcast.22, bf16[4096,256]{1,0:T(8,128)(2,1)S(1)} %copy-done), kind=kOutput, calls=%fused_computation.10 | convolution fusion | flops 2147745792 | bytes 11010048 | tf_op jit(solution)/shard_map/dot_general | solution.py:90
  23.4 9.1 %all-to-all-done = bf16[16,48,768]{2,1,0:T(8,128)(2,1)} async-done(((bf16[16,48,768]{2,1,0:T(8,128)(2,1)}), bf16[16,48,768]{2,1,0:T(8,128)(2,1)}, u32[]{:S(2)}, u32[]{:S(2)}) %all-to-all-start) | async-done | bytes 1179680 | tf_op jit(solution)/shard_map/all_to_all | solution.py:68
  32.4 0.0 copy-done.5
  32.4 2.8 %fusion = f32[1024,768]{1,0:T(8,128)S(1)} fusion(bf16[768,768]{1,0:T(8,128)(2,1)} %bitcast.2, s32[1024]{0:T(1024)S(1)} %copy-done.5), kind=kOutput, calls=%fused_computation.3 | convolution fusion | flops 1208745984 | bytes 4329472 | tf_op jit(solution)/shard_map/dot_general | solution.py:96
  35.3 0.0 copy-start.1
  35.3 1.6 %copy-done.1 = f32[1024,768]{1,0:T(8,128)} copy-done((f32[1024,768]{1,0:T(8,128)}, f32[1024,768]{1,0:T(8,128)S(1)}, u32[]{:S(2)}) %copy-start.1) | copy-done | bytes 3145752
  36.9 0.0 copy-done.3
  36.9 0.7 fusion.1
  37.7 0.8 dynamic-slice_bitcast_fusion
  38.4 1.9 %collective-permute-start = (f32[128,768]{1,0:T(8,128)}, f32[128,768]{1,0:T(8,128)}, u32[]{:S(2)}, u32[]{:S(2)}) collective-permute-start(f32[128,768]{1,0:T(8,128)} %dynamic-slice_bitcast_fusion), channel_id=1, source_target_pairs={{0,16},{16,0},{1,17},{17,1},{2,18},{18,2},{3,19},{19,3},{4,20},{20... | collective-permute-start | bytes 1179656 | tf_op jit(solution)/shard_map/ppermute | solution.py:58
  40.4 10.0 %collective-permute-done = f32[128,768]{1,0:T(8,128)} collective-permute-done((f32[128,768]{1,0:T(8,128)}, f32[128,768]{1,0:T(8,128)}, u32[]{:S(2)}, u32[]{:S(2)}) %collective-permute-start) | collective-permute-done | bytes 393248 | tf_op jit(solution)/shard_map/ppermute | solution.py:58
  50.3 1.0 fusion.12
  51.4 30.2 %all_to_all.24 = f32[16,8,768]{2,1,0:T(8,128)S(1)} all-to-all(f32[16,8,768]{2,1,0:T(8,128)S(1)} %fusion.12), channel_id=1, replica_groups=mesh['wz'=16,'wy'=2,'orb'=16] {'wz'}, dimensions={0} | all-to-all | bytes 786432 | tf_op jit(solution)/shard_map/all_to_all | solution.py:74
  81.6 27.6 %all_to_all.25 = f32[16,8,768]{2,1,0:T(8,128)S(1)} all-to-all(f32[16,8,768]{2,1,0:T(8,128)S(1)} %broadcast_in_dim.8), channel_id=1, replica_groups=mesh['wz'=16,'wy'=2,'orb'=16] {'wz'}, dimensions={0} | all-to-all | bytes 786432 | tf_op jit(solution)/shard_map/all_to_all | solution.py:68
  109.3 2.3 %collective-permute-start.1 = (f32[128,768]{1,0:T(8,128)S(1)}, f32[128,768]{1,0:T(8,128)S(1)}, u32[]{:S(2)}, u32[]{:S(2)}) collective-permute-start(f32[128,768]{1,0:T(8,128)S(1)} %bitcast.25), channel_id=1, source_target_pairs={{0,16},{16,0},{1,17},{17,1},{2,18},{18,2},{3,19},{19,3},{4,20},{20... | collective-permute-start | bytes 1179656 | tf_op jit(solution)/shard_map/ppermute | solution.py:61
  111.6 2.6 %fusion.9 = f32[1024]{0:T(1024)S(1)} fusion(bf16[256,768]{1,0:T(8,128)(2,1)} %param.12, f32[1024,768]{1,0:T(8,128)} %copy-done.1, bf16[1024,256]{0,1:T(8,128)(2,1)S(1)} %convolution_convert_fusion), kind=kOutput, calls=%fused_computation.11 | convolution fusion | flops 404225024 | bytes 4067328 | tf_op jit(solution)/shard_map/dot_general | solution.py:103
  114.2 0.7 all_to_all.16
  114.8 14.1 %all-to-all-start.1 = ((f32[16,1,64]{2,1,0:T(1,128)}), f32[16,1,64]{2,1,0:T(1,128)S(1)}, u32[]{:S(2)}, u32[]{:S(2)}) async-start(f32[16,1,64]{2,1,0:T(1,128)} %all_to_all.16), calls=%async_computation.1 | async-start | bytes 16384 | tf_op jit(solution)/shard_map/all_to_all | solution.py:74
  128.9 6.9 %all-to-all-done.1 = f32[16,1,64]{2,1,0:T(1,128)S(1)} async-done(((f32[16,1,64]{2,1,0:T(1,128)}), f32[16,1,64]{2,1,0:T(1,128)S(1)}, u32[]{:S(2)}, u32[]{:S(2)}) %all-to-all-start.1) | async-done | bytes 4128 | tf_op jit(solution)/shard_map/all_to_all | solution.py:74
  135.8 0.5 reduce_sum.28
  136.4 0.0 collective-permute-done.1
  136.4 0.9 maximum_select_fusion
  (4 shorter events, 0.1 us)
Async XLA Ops:
  0.6 17.0 %copy-start = (bf16[4096,256]{1,0:T(8,128)(2,1)S(1)}, bf16[4096,256]{1,0:T(8,128)(2,1)}, u32[]{:S(2)}) copy-start(bf16[4096,256]{1,0:T(8,128)(2,1)} %param.11) | copy-start | bytes 6291460
  0.6 13.1 %copy-start.4 = (s32[1024]{0:T(1024)S(1)}, s32[1024]{0:T(1024)}, u32[]{:S(2)}) copy-start(s32[1024]{0:T(1024)} %param.7) | copy-start | bytes 12292
  0.7 13.1 %copy-start.2 = (bf16[1024,64]{0,1:T(8,128)(2,1)S(1)}, bf16[1024,64]{0,1:T(8,128)(2,1)}, u32[]{:S(2)}) copy-start(bf16[1024,64]{0,1:T(8,128)(2,1)} %param.8) | copy-start | bytes 393220
  2.8 29.6 %all-to-all-start = ((bf16[16,48,768]{2,1,0:T(8,128)(2,1)}), bf16[16,48,768]{2,1,0:T(8,128)(2,1)}, u32[]{:S(2)}, u32[]{:S(2)}) async-start(bf16[16,48,768]{2,1,0:T(8,128)(2,1)} %broadcast_in_dim.7), calls=%async_computation | async-start | bytes 2359296 | tf_op jit(solution)/shard_map/all_to_all | solution.py:68
  17.6 14.8 %copy-start.5 = (s32[1024]{0:T(1024)S(1)}, s32[1024]{0:T(1024)}, u32[]{:S(2)}) copy-start(s32[1024]{0:T(1024)} %param.9) | copy-start | bytes 12292
  32.4 4.5 %copy-start.3 = (f32[1024]{0:T(1024)S(1)}, f32[1024]{0:T(1024)}, u32[]{:S(2)}) copy-start(f32[1024]{0:T(1024)} %param.10) | copy-start | bytes 12292
  35.3 1.6 %copy-start.1 = (f32[1024,768]{1,0:T(8,128)}, f32[1024,768]{1,0:T(8,128)S(1)}, u32[]{:S(2)}) copy-start(f32[1024,768]{1,0:T(8,128)S(1)} %fusion) | copy-start | bytes 9437188
  38.4 11.9 %collective-permute-start = (f32[128,768]{1,0:T(8,128)}, f32[128,768]{1,0:T(8,128)}, u32[]{:S(2)}, u32[]{:S(2)}) collective-permute-start(f32[128,768]{1,0:T(8,128)} %dynamic-slice_bitcast_fusion), channel_id=1, source_target_pairs={{0,16},{16,0},{1,17},{17,1},{2,18},{18,2},{3,19},{19,3},{4,20},{20... | collective-permute-start | bytes 1179656 | tf_op jit(solution)/shard_map/ppermute | solution.py:58
  109.3 27.1 %collective-permute-start.1 = (f32[128,768]{1,0:T(8,128)S(1)}, f32[128,768]{1,0:T(8,128)S(1)}, u32[]{:S(2)}, u32[]{:S(2)}) collective-permute-start(f32[128,768]{1,0:T(8,128)S(1)} %bitcast.25), channel_id=1, source_target_pairs={{0,16},{16,0},{1,17},{17,1},{2,18},{18,2},{3,19},{19,3},{4,20},{20... | collective-permute-start | bytes 1179656 | tf_op jit(solution)/shard_map/ppermute | solution.py:61
  114.8 21.0 %all-to-all-start.1 = ((f32[16,1,64]{2,1,0:T(1,128)}), f32[16,1,64]{2,1,0:T(1,128)S(1)}, u32[]{:S(2)}, u32[]{:S(2)}) async-start(f32[16,1,64]{2,1,0:T(1,128)} %all_to_all.16), calls=%async_computation.1 | async-start | bytes 16384 | tf_op jit(solution)/shard_map/all_to_all | solution.py:74

commit v5 on v4

--- a/solution.py
+++ b/solution.py
@@ -51,15 +51,17 @@
     return all_gather_bits(reduced, axis, order[::-1]).reshape(tail)
 
 
-def all_reduce_walker(x):
+def all_reduce_walker(x, rider):
     me = lax.axis_index("wy")
     halves = x.reshape((2, x.shape[0] // 2) + x.shape[1:])
     keep = _pick(halves, me)
     half = keep + lax.ppermute(_pick(halves, 1 - me), "wy", [(0, 1), (1, 0)])
+    half, rider = lax.optimization_barrier((half, rider))
     reduced = reduce_scatter_by_all_to_all(half, "wz")
     half = gather_by_all_to_all(reduced, "wz").reshape(half.shape)
     other = lax.ppermute(half, "wy", [(0, 1), (1, 0)])
-    return jnp.where(me == 0, jnp.stack([half, other]), jnp.stack([other, half])).reshape(x.shape)
+    full = jnp.where(me == 0, jnp.stack([half, other]), jnp.stack([other, half]))
+    return full.reshape(x.shape), rider
 
 
 def gather_by_all_to_all(x, axis):
@@ -108,7 +110,7 @@
     )
     partial_ratio = jnp.sum(orbital_values.astype(jnp.float32) * rotated_columns, axis=1)
     ratios = reduce_scatter_by_all_to_all(partial_ratio, "orb")
-    gradient = all_reduce_walker(local_gradient)
+    gradient, ratios = all_reduce_walker(local_gradient, ratios)
     return (ratios, gradient)
 
 

time: 138 us -> 130 us (0.942)
  the two profiles are of different devices: /device:TPU:1 before, /device:TPU:32 now
where the time goes in v5:
time: 130 us
  blocking collectives  66.7 us (51%)
  waiting for transfers between devices  26.2 us (20%)
  starting transfers between devices  16.3 us (13%)
  matrix products  9.94 us (8%)
  other arithmetic  6.35 us (5%)
  local copies, waits for them, and re-layouts  3.64 us (3%)
    all_to_all x1, blocking collectives, reduce_scatter_by_all_to_all(): return jnp.sum(lax.all_to_all(parts, axis, 0, 0, tiled=True), axis=0)  37.1 us
    all_to_all x1, blocking collectives, gather_by_all_to_all(): return lax.all_to_all(copies, axis, 0, 0, tiled=True)  29.6 us
    all_to_all x1, waiting for transfers between devices, gather_by_all_to_all(): return lax.all_to_all(copies, axis, 0, 0, tiled=True)  9.79 us
    ppermute x1, waiting for transfers between devices, all_reduce_walker(): other = lax.ppermute(half, 'wy', [(0, 1), (1, 0)])  8.93 us
    all_to_all x1, waiting for transfers between devices, reduce_scatter_by_all_to_all(): return jnp.sum(lax.all_to_all(parts, axis, 0, 0, tiled=True), axis=0)  7.44 us
    all_to_all x1, starting transfers between devices, gather_by_all_to_all(): return lax.all_to_all(copies, axis, 0, 0, tiled=True)  7.08 us
    dot_general x1, matrix products, body(): jnp.dot(stencil_matrix, spline_table, preferred_element_type=jnp.float32)  5.76 us
    all_to_all x1, starting transfers between devices, reduce_scatter_by_all_to_all(): return jnp.sum(lax.all_to_all(parts, axis, 0, 0, tiled=True), axis=0)  3.95 us
  transfers between devices with their start and end apart: 4, of which 3 were waited for; matrix products, arithmetic and copies ran while one was open for 8% of the time, Pallas kernels for 0%

profile of v5, /device:TPU:32, one launch (start us, length us, event | category | flops | bytes accessed | tf_op | source)
XLA Modules:
  0.0 129.9 jit_solution(11689154661449001301)
XLA Ops:
  0.6 0.0 copy-start
  0.6 0.0 copy-start.4
  0.7 0.0 copy-start.2
  0.7 2.1 %broadcast_in_dim.7 = bf16[16,48,768]{2,1,0:T(8,128)(2,1)} broadcast(bf16[48,768]{1,0:T(8,128)(2,1)} %bitcast.27), dimensions={1,2} | broadcast | bytes 1253376 | tf_op jit(solution)/shard_map/broadcast_in_dim | solution.py:69
  2.8 7.1 %all-to-all-start = ((bf16[16,48,768]{2,1,0:T(8,128)(2,1)}), bf16[16,48,768]{2,1,0:T(8,128)(2,1)}, u32[]{:S(2)}, u32[]{:S(2)}) async-start(bf16[16,48,768]{2,1,0:T(8,128)(2,1)} %broadcast_in_dim.7), calls=%async_computation | async-start | bytes 2359296 | tf_op jit(solution)/shard_map/all_to_all | solution.py:70
  9.9 0.0 copy-done.4
  9.9 0.0 copy-done.2
  9.9 3.8 %broadcast_multiply_fusion = bf16[1024,64,64]{0,2,1:T(8,128)(2,1)} fusion(bf16[1024,64]{0,1:T(8,128)(2,1)S(1)} %copy-done.2, bf16[1024,64]{0,1:T(8,128)(2,1)S(1)} %fusion.12), kind=kLoop, calls=%fused_computation | loop fusion | flops 4194304 | bytes 8650752 | tf_op jit(solution)/shard_map/mul | solution.py:89
  13.7 0.0 copy-done
  13.7 5.8 %convolution_convert_fusion = bf16[1024,256]{0,1:T(8,128)(2,1)S(1)} fusion(bf16[1024,4096]{0,1:T(8,128)(2,1)} %bitcast.19, bf16[4096,256]{1,0:T(8,128)(2,1)S(1)} %copy-done), kind=kOutput, calls=%fused_computation.10 | convolution fusion | flops 2147745792 | bytes 11010048 | tf_op jit(solution)/shard_map/dot_general | solution.py:92
  19.5 9.8 %all-to-all-done = bf16[16,48,768]{2,1,0:T(8,128)(2,1)} async-done(((bf16[16,48,768]{2,1,0:T(8,128)(2,1)}), bf16[16,48,768]{2,1,0:T(8,128)(2,1)}, u32[]{:S(2)}, u32[]{:S(2)}) %all-to-all-start) | async-done | bytes 1179680 | tf_op jit(solution)/shard_map/all_to_all | solution.py:70
  29.3 0.0 copy-done.5
  29.3 0.0 copy-start.3
  29.3 2.8 %fusion = f32[1024,768]{1,0:T(8,128)S(1)} fusion(bf16[768,768]{1,0:T(8,128)(2,1)} %bitcast.2, s32[1024]{0:T(1024)S(1)} %copy-done.5), kind=kOutput, calls=%fused_computation.3 | convolution fusion | flops 1208745984 | bytes 4329472 | tf_op jit(solution)/shard_map/dot_general | solution.py:98
  32.1 0.0 copy-done.3
  32.1 0.0 copy-start.1
  32.1 0.7 fusion.1
  32.9 0.8 dynamic-slice_bitcast_fusion
  33.7 2.6 %collective-permute-start = (f32[128,768]{1,0:T(8,128)}, f32[128,768]{1,0:T(8,128)}, u32[]{:S(2)}, u32[]{:S(2)}) collective-permute-start(f32[128,768]{1,0:T(8,128)} %dynamic-slice_bitcast_fusion), channel_id=1, source_target_pairs={{0,16},{16,0},{1,17},{17,1},{2,18},{18,2},{3,19},{19,3},{4,20},{20... | collective-permute-start | bytes 1179656 | tf_op jit(solution)/shard_map/ppermute | solution.py:58
  36.2 0.0 copy-done.1
  36.3 0.6 fusion.9
  36.9 0.7 all_to_all.16
  37.6 4.0 %all-to-all-start.1 = ((f32[16,1,64]{2,1,0:T(1,128)}), f32[16,1,64]{2,1,0:T(1,128)S(1)}, u32[]{:S(2)}, u32[]{:S(2)}) async-start(f32[16,1,64]{2,1,0:T(1,128)} %all_to_all.16), calls=%async_computation.1 | async-start | bytes 16384 | tf_op jit(solution)/shard_map/all_to_all | solution.py:76
  41.5 7.4 %all-to-all-done.1 = f32[16,1,64]{2,1,0:T(1,128)S(1)} async-done(((f32[16,1,64]{2,1,0:T(1,128)}), f32[16,1,64]{2,1,0:T(1,128)S(1)}, u32[]{:S(2)}, u32[]{:S(2)}) %all-to-all-start.1) | async-done | bytes 4128 | tf_op jit(solution)/shard_map/all_to_all | solution.py:76
  49.0 0.5 reduce_sum.28
  49.5 0.0 collective-permute-done
  49.5 1.0 bitcast_add_fusion
  50.5 37.1 %all_to_all.24 = f32[16,8,768]{2,1,0:T(8,128)S(1)} all-to-all(f32[16,8,768]{2,1,0:T(8,128)S(1)} %bitcast.24), channel_id=1, replica_groups=mesh['wz'=16,'wy'=2,'orb'=16] {'wz'}, dimensions={0} | all-to-all | bytes 786432 | tf_op jit(solution)/shard_map/all_to_all | solution.py:76
  87.7 29.6 %all_to_all.25 = f32[16,8,768]{2,1,0:T(8,128)S(1)} all-to-all(f32[16,8,768]{2,1,0:T(8,128)S(1)} %broadcast_in_dim.8), channel_id=1, replica_groups=mesh['wz'=16,'wy'=2,'orb'=16] {'wz'}, dimensions={0} | all-to-all | bytes 786432 | tf_op jit(solution)/shard_map/all_to_all | solution.py:70
  117.3 2.7 %collective-permute-start.1 = (f32[128,768]{1,0:T(8,128)S(1)}, f32[128,768]{1,0:T(8,128)S(1)}, u32[]{:S(2)}, u32[]{:S(2)}) collective-permute-start(f32[128,768]{1,0:T(8,128)S(1)} %bitcast.22), channel_id=1, source_target_pairs={{0,16},{16,0},{1,17},{17,1},{2,18},{18,2},{3,19},{19,3},{4,20},{20... | collective-permute-start | bytes 1179656 | tf_op jit(solution)/shard_map/ppermute | solution.py:62
  120.0 8.9 %collective-permute-done.1 = f32[128,768]{1,0:T(8,128)S(1)} collective-permute-done((f32[128,768]{1,0:T(8,128)S(1)}, f32[128,768]{1,0:T(8,128)S(1)}, u32[]{:S(2)}, u32[]{:S(2)}) %collective-permute-start.1) | collective-permute-done | bytes 393248 | tf_op jit(solution)/shard_map/ppermute | solution.py:62
  128.9 0.9 maximum_select_fusion
  (4 shorter events, 0.1 us)
Async XLA Ops:
  0.6 13.1 %copy-start = (bf16[4096,256]{1,0:T(8,128)(2,1)S(1)}, bf16[4096,256]{1,0:T(8,128)(2,1)}, u32[]{:S(2)}) copy-start(bf16[4096,256]{1,0:T(8,128)(2,1)} %param.11) | copy-start | bytes 6291460
  0.6 9.2 %copy-start.4 = (s32[1024]{0:T(1024)S(1)}, s32[1024]{0:T(1024)}, u32[]{:S(2)}) copy-start(s32[1024]{0:T(1024)} %param.7) | copy-start | bytes 12292
  0.7 9.3 %copy-start.2 = (bf16[1024,64]{0,1:T(8,128)(2,1)S(1)}, bf16[1024,64]{0,1:T(8,128)(2,1)}, u32[]{:S(2)}) copy-start(bf16[1024,64]{0,1:T(8,128)(2,1)} %param.8) | copy-start | bytes 393220
  2.8 26.5 %all-to-all-start = ((bf16[16,48,768]{2,1,0:T(8,128)(2,1)}), bf16[16,48,768]{2,1,0:T(8,128)(2,1)}, u32[]{:S(2)}, u32[]{:S(2)}) async-start(bf16[16,48,768]{2,1,0:T(8,128)(2,1)} %broadcast_in_dim.7), calls=%async_computation | async-start | bytes 2359296 | tf_op jit(solution)/shard_map/all_to_all | solution.py:70
  13.7 15.6 %copy-start.5 = (s32[1024]{0:T(1024)S(1)}, s32[1024]{0:T(1024)}, u32[]{:S(2)}) copy-start(s32[1024]{0:T(1024)} %param.9) | copy-start | bytes 12292
  29.3 2.8 %copy-start.3 = (f32[1024]{0:T(1024)S(1)}, f32[1024]{0:T(1024)}, u32[]{:S(2)}) copy-start(f32[1024]{0:T(1024)} %param.10) | copy-start | bytes 12292
  32.1 4.1 %copy-start.1 = (bf16[256,768]{1,0:T(8,128)(2,1)S(1)}, bf16[256,768]{1,0:T(8,128)(2,1)}, u32[]{:S(2)}) copy-start(bf16[256,768]{1,0:T(8,128)(2,1)} %param.12) | copy-start | bytes 1179652
  33.7 15.8 %collective-permute-start = (f32[128,768]{1,0:T(8,128)}, f32[128,768]{1,0:T(8,128)}, u32[]{:S(2)}, u32[]{:S(2)}) collective-permute-start(f32[128,768]{1,0:T(8,128)} %dynamic-slice_bitcast_fusion), channel_id=1, source_target_pairs={{0,16},{16,0},{1,17},{17,1},{2,18},{18,2},{3,19},{19,3},{4,20},{20... | collective-permute-start | bytes 1179656 | tf_op jit(solution)/shard_map/ppermute | solution.py:58
  37.6 11.4 %all-to-all-start.1 = ((f32[16,1,64]{2,1,0:T(1,128)}), f32[16,1,64]{2,1,0:T(1,128)S(1)}, u32[]{:S(2)}, u32[]{:S(2)}) async-start(f32[16,1,64]{2,1,0:T(1,128)} %all_to_all.16), calls=%async_computation.1 | async-start | bytes 16384 | tf_op jit(solution)/shard_map/all_to_all | solution.py:76
  117.3 11.6 %collective-permute-start.1 = (f32[128,768]{1,0:T(8,128)S(1)}, f32[128,768]{1,0:T(8,128)S(1)}, u32[]{:S(2)}, u32[]{:S(2)}) collective-permute-start(f32[128,768]{1,0:T(8,128)S(1)} %bitcast.22), channel_id=1, source_target_pairs={{0,16},{16,0},{1,17},{17,1},{2,18},{18,2},{3,19},{19,3},{4,20},{20... | collective-permute-start | bytes 1179656 | tf_op jit(solution)/shard_map/ppermute | solution.py:62

commit v6 on v5

--- a/solution.py
+++ b/solution.py
@@ -57,11 +57,11 @@
     keep = _pick(halves, me)
     half = keep + lax.ppermute(_pick(halves, 1 - me), "wy", [(0, 1), (1, 0)])
     half, rider = lax.optimization_barrier((half, rider))
-    reduced = reduce_scatter_by_all_to_all(half, "wz")
+    reduced = reduce_scatter_by_all_to_all(half, "wz").astype(jnp.bfloat16)
     half = gather_by_all_to_all(reduced, "wz").reshape(half.shape)
     other = lax.ppermute(half, "wy", [(0, 1), (1, 0)])
     full = jnp.where(me == 0, jnp.stack([half, other]), jnp.stack([other, half]))
-    return full.reshape(x.shape), rider
+    return full.reshape(x.shape).astype(x.dtype), rider
 
 
 def gather_by_all_to_all(x, axis):

time: 130 us -> 121 us (0.931)
  blocking collectives: 66.7 us -> 60.8 us
  waiting for transfers between devices: 26.2 us -> 22.6 us
    all_to_all x1, blocking collectives: 29.6 us -> 23.7 us  [gather_by_all_to_all(): return lax.all_to_all(copies, axis, 0, 0, tiled=True)]
    ppermute x1, waiting for transfers between devices: 8.93 us -> 5.34 us  [all_reduce_walker(): other = lax.ppermute(half, 'wy', [(0, 1), (1, 0)])]
  transfers between devices with their start and end apart: 4 -> 4, of which waited for: 3 -> 3; matrix products, arithmetic and copies ran while one was open for 8% -> 9% of each run, Pallas kernels for 0% -> 0%
where the time goes in v6:
time: 121 us; the launch traced here: 120 us
  blocking collectives  60.8 us (50%)
  waiting for transfers between devices  22.6 us (19%)
  starting transfers between devices  16.3 us (13%)
  matrix products  9.94 us (8%)
  other arithmetic  6.42 us (5%)
  local copies, waits for them, and re-layouts  3.63 us (3%)
    all_to_all x1, blocking collectives, reduce_scatter_by_all_to_all(): return jnp.sum(lax.all_to_all(parts, axis, 0, 0, tiled=True), axis=0)  37.1 us
    all_to_all x1, blocking collectives, gather_by_all_to_all(): return lax.all_to_all(copies, axis, 0, 0, tiled=True)  23.7 us
    all_to_all x1, waiting for transfers between devices, gather_by_all_to_all(): return lax.all_to_all(copies, axis, 0, 0, tiled=True)  9.79 us
    all_to_all x1, waiting for transfers between devices, reduce_scatter_by_all_to_all(): return jnp.sum(lax.all_to_all(parts, axis, 0, 0, tiled=True), axis=0)  7.44 us
    all_to_all x1, starting transfers between devices, gather_by_all_to_all(): return lax.all_to_all(copies, axis, 0, 0, tiled=True)  7.08 us
    dot_general x1, matrix products, body(): jnp.dot(stencil_matrix, spline_table, preferred_element_type=jnp.float32)  5.76 us
    ppermute x1, waiting for transfers between devices, all_reduce_walker(): other = lax.ppermute(half, 'wy', [(0, 1), (1, 0)])  5.34 us
    all_to_all x1, starting transfers between devices, reduce_scatter_by_all_to_all(): return jnp.sum(lax.all_to_all(parts, axis, 0, 0, tiled=True), axis=0)  3.95 us
  transfers between devices with their start and end apart: 4, of which 3 were waited for; matrix products, arithmetic and copies ran while one was open for 9% of the time, Pallas kernels for 0%

profile of v6, /device:TPU:32, one launch (start us, length us, event | category | flops | bytes accessed | tf_op | source)
XLA Modules:
  0.0 120.4 jit_solution(8644097959678956854)
XLA Ops:
  0.6 0.0 copy-start
  0.6 0.0 copy-start.4
  0.7 0.0 copy-start.2
  0.7 2.1 %broadcast_in_dim.7 = bf16[16,48,768]{2,1,0:T(8,128)(2,1)} broadcast(bf16[48,768]{1,0:T(8,128)(2,1)} %bitcast.28), dimensions={1,2} | broadcast | bytes 1253376 | tf_op jit(solution)/shard_map/broadcast_in_dim | solution.py:69
  2.8 7.1 %all-to-all-start = ((bf16[16,48,768]{2,1,0:T(8,128)(2,1)}), bf16[16,48,768]{2,1,0:T(8,128)(2,1)}, u32[]{:S(2)}, u32[]{:S(2)}) async-start(bf16[16,48,768]{2,1,0:T(8,128)(2,1)} %broadcast_in_dim.7), calls=%async_computation | async-start | bytes 2359296 | tf_op jit(solution)/shard_map/all_to_all | solution.py:70
  9.9 0.0 copy-done.4
  9.9 0.0 copy-done.2
  9.9 3.8 %broadcast_multiply_fusion = bf16[1024,64,64]{0,2,1:T(8,128)(2,1)} fusion(bf16[1024,64]{0,1:T(8,128)(2,1)S(1)} %copy-done.2, bf16[1024,64]{0,1:T(8,128)(2,1)S(1)} %fusion.12), kind=kLoop, calls=%fused_computation | loop fusion | flops 4194304 | bytes 8650752 | tf_op jit(solution)/shard_map/mul | solution.py:89
  13.7 0.0 copy-done
  13.7 5.8 %convolution_convert_fusion = bf16[1024,256]{0,1:T(8,128)(2,1)S(1)} fusion(bf16[1024,4096]{0,1:T(8,128)(2,1)} %bitcast.21, bf16[4096,256]{1,0:T(8,128)(2,1)S(1)} %copy-done), kind=kOutput, calls=%fused_computation.10 | convolution fusion | flops 2147745792 | bytes 11010048 | tf_op jit(solution)/shard_map/dot_general | solution.py:92
  19.5 9.8 %all-to-all-done = bf16[16,48,768]{2,1,0:T(8,128)(2,1)} async-done(((bf16[16,48,768]{2,1,0:T(8,128)(2,1)}), bf16[16,48,768]{2,1,0:T(8,128)(2,1)}, u32[]{:S(2)}, u32[]{:S(2)}) %all-to-all-start) | async-done | bytes 1179680 | tf_op jit(solution)/shard_map/all_to_all | solution.py:70
  29.3 0.0 copy-done.5
  29.3 0.0 copy-start.3
  29.3 2.8 %fusion = f32[1024,768]{1,0:T(8,128)S(1)} fusion(bf16[768,768]{1,0:T(8,128)(2,1)} %bitcast.2, s32[1024]{0:T(1024)S(1)} %copy-done.5), kind=kOutput, calls=%fused_computation.3 | convolution fusion | flops 1208745984 | bytes 4329472 | tf_op jit(solution)/shard_map/dot_general | solution.py:98
  32.1 0.0 copy-done.3
  32.1 0.0 copy-start.1
  32.1 0.7 fusion.1
  32.9 0.8 dynamic-slice_bitcast_fusion
  33.7 2.6 %collective-permute-start = (f32[128,768]{1,0:T(8,128)}, f32[128,768]{1,0:T(8,128)}, u32[]{:S(2)}, u32[]{:S(2)}) collective-permute-start(f32[128,768]{1,0:T(8,128)} %dynamic-slice_bitcast_fusion), channel_id=1, source_target_pairs={{0,16},{16,0},{1,17},{17,1},{2,18},{18,2},{3,19},{19,3},{4,20},{20... | collective-permute-start | bytes 1179656 | tf_op jit(solution)/shard_map/ppermute | solution.py:58
  36.2 0.0 copy-done.1
  36.3 0.6 fusion.9
  36.9 0.7 all_to_all.16
  37.6 4.0 %all-to-all-start.1 = ((f32[16,1,64]{2,1,0:T(1,128)}), f32[16,1,64]{2,1,0:T(1,128)S(1)}, u32[]{:S(2)}, u32[]{:S(2)}) async-start(f32[16,1,64]{2,1,0:T(1,128)} %all_to_all.16), calls=%async_computation.1 | async-start | bytes 16384 | tf_op jit(solution)/shard_map/all_to_all | solution.py:76
  41.5 7.4 %all-to-all-done.1 = f32[16,1,64]{2,1,0:T(1,128)S(1)} async-done(((f32[16,1,64]{2,1,0:T(1,128)}), f32[16,1,64]{2,1,0:T(1,128)S(1)}, u32[]{:S(2)}, u32[]{:S(2)}) %all-to-all-start.1) | async-done | bytes 4128 | tf_op jit(solution)/shard_map/all_to_all | solution.py:76
  49.0 0.5 reduce_sum.28
  49.5 0.0 collective-permute-done
  49.5 1.0 bitcast_add_fusion
  50.5 37.1 %all_to_all.24 = f32[16,8,768]{2,1,0:T(8,128)S(1)} all-to-all(f32[16,8,768]{2,1,0:T(8,128)S(1)} %bitcast.24), channel_id=1, replica_groups=mesh['wz'=16,'wy'=2,'orb'=16] {'wz'}, dimensions={0} | all-to-all | bytes 786432 | tf_op jit(solution)/shard_map/all_to_all | solution.py:76
  87.7 23.7 %all_to_all.25 = bf16[16,8,768]{2,1,0:T(8,128)(2,1)S(1)} all-to-all(bf16[16,8,768]{2,1,0:T(8,128)(2,1)S(1)} %broadcast_in_dim.8), channel_id=1, replica_groups=mesh['wz'=16,'wy'=2,'orb'=16] {'wz'}, dimensions={0} | all-to-all | bytes 393216 | tf_op jit(solution)/shard_map/all_to_all | solution.py:70
  111.3 2.7 %collective-permute-start.1 = (bf16[128,768]{1,0:T(8,128)(2,1)S(1)}, bf16[128,768]{1,0:T(8,128)(2,1)S(1)}, u32[]{:S(2)}, u32[]{:S(2)}) collective-permute-start(bf16[128,768]{1,0:T(8,128)(2,1)S(1)} %bitcast.25), channel_id=1, source_target_pairs={{0,16},{16,0},{1,17},{17,1},{2,18},{18,2},{3,19},{19,3},{4,20},{20... | collective-permute-start | bytes 589832 | tf_op jit(solution)/shard_map/ppermute | solution.py:62
  114.1 5.3 %collective-permute-done.1 = bf16[128,768]{1,0:T(8,128)(2,1)S(1)} collective-permute-done((bf16[128,768]{1,0:T(8,128)(2,1)S(1)}, bf16[128,768]{1,0:T(8,128)(2,1)S(1)}, u32[]{:S(2)}, u32[]{:S(2)}) %collective-permute-start.1) | collective-permute-done | bytes 196640 | tf_op jit(solution)/shard_map/ppermute | solution.py:62
  119.5 1.0 bitcast_convert_fusion
  (5 shorter events, 0.1 us)
Async XLA Ops:
  0.6 13.1 %copy-start = (bf16[4096,256]{1,0:T(8,128)(2,1)S(1)}, bf16[4096,256]{1,0:T(8,128)(2,1)}, u32[]{:S(2)}) copy-start(bf16[4096,256]{1,0:T(8,128)(2,1)} %param.11) | copy-start | bytes 6291460
  0.6 9.2 %copy-start.4 = (s32[1024]{0:T(1024)S(1)}, s32[1024]{0:T(1024)}, u32[]{:S(2)}) copy-start(s32[1024]{0:T(1024)} %param.7) | copy-start | bytes 12292
  0.7 9.3 %copy-start.2 = (bf16[1024,64]{0,1:T(8,128)(2,1)S(1)}, bf16[1024,64]{0,1:T(8,128)(2,1)}, u32[]{:S(2)}) copy-start(bf16[1024,64]{0,1:T(8,128)(2,1)} %param.8) | copy-start | bytes 393220
  2.8 26.5 %all-to-all-start = ((bf16[16,48,768]{2,1,0:T(8,128)(2,1)}), bf16[16,48,768]{2,1,0:T(8,128)(2,1)}, u32[]{:S(2)}, u32[]{:S(2)}) async-start(bf16[16,48,768]{2,1,0:T(8,128)(2,1)} %broadcast_in_dim.7), calls=%async_computation | async-start | bytes 2359296 | tf_op jit(solution)/shard_map/all_to_all | solution.py:70
  13.7 15.6 %copy-start.5 = (s32[1024]{0:T(1024)S(1)}, s32[1024]{0:T(1024)}, u32[]{:S(2)}) copy-start(s32[1024]{0:T(1024)} %param.9) | copy-start | bytes 12292
  29.3 2.8 %copy-start.3 = (f32[1024]{0:T(1024)S(1)}, f32[1024]{0:T(1024)}, u32[]{:S(2)}) copy-start(f32[1024]{0:T(1024)} %param.10) | copy-start | bytes 12292
  32.1 4.1 %copy-start.1 = (bf16[256,768]{1,0:T(8,128)(2,1)S(1)}, bf16[256,768]{1,0:T(8,128)(2,1)}, u32[]{:S(2)}) copy-start(bf16[256,768]{1,0:T(8,128)(2,1)} %param.12) | copy-start | bytes 1179652
  33.7 15.8 %collective-permute-start = (f32[128,768]{1,0:T(8,128)}, f32[128,768]{1,0:T(8,128)}, u32[]{:S(2)}, u32[]{:S(2)}) collective-permute-start(f32[128,768]{1,0:T(8,128)} %dynamic-slice_bitcast_fusion), channel_id=1, source_target_pairs={{0,16},{16,0},{1,17},{17,1},{2,18},{18,2},{3,19},{19,3},{4,20},{20... | collective-permute-start | bytes 1179656 | tf_op jit(solution)/shard_map/ppermute | solution.py:58
  37.6 11.4 %all-to-all-start.1 = ((f32[16,1,64]{2,1,0:T(1,128)}), f32[16,1,64]{2,1,0:T(1,128)S(1)}, u32[]{:S(2)}, u32[]{:S(2)}) async-start(f32[16,1,64]{2,1,0:T(1,128)} %all_to_all.16), calls=%async_computation.1 | async-start | bytes 16384 | tf_op jit(solution)/shard_map/all_to_all | solution.py:76
  111.3 8.0 %collective-permute-start.1 = (bf16[128,768]{1,0:T(8,128)(2,1)S(1)}, bf16[128,768]{1,0:T(8,128)(2,1)S(1)}, u32[]{:S(2)}, u32[]{:S(2)}) collective-permute-start(bf16[128,768]{1,0:T(8,128)(2,1)S(1)} %bitcast.25), channel_id=1, source_target_pairs={{0,16},{16,0},{1,17},{17,1},{2,18},{18,2},{3,19},{19,3},{4,20},{20... | collective-permute-start | bytes 589832 | tf_op jit(solution)/shard_map/ppermute | solution.py:62

commit v7 on v6

--- a/solution.py
+++ b/solution.py
@@ -57,8 +57,10 @@
     keep = _pick(halves, me)
     half = keep + lax.ppermute(_pick(halves, 1 - me), "wy", [(0, 1), (1, 0)])
     half, rider = lax.optimization_barrier((half, rider))
-    reduced = reduce_scatter_by_all_to_all(half, "wz").astype(jnp.bfloat16)
-    half = gather_by_all_to_all(reduced, "wz").reshape(half.shape)
+    reduced = reduce_scatter_by_all_to_all(half, "zb")
+    reduced = reduce_scatter_by_all_to_all(reduced, "za").astype(jnp.bfloat16)
+    near = gather_by_all_to_all(reduced, "za").reshape((-1,) + reduced.shape[1:])
+    half = gather_by_all_to_all(near, "zb").reshape(half.shape)
     other = lax.ppermute(half, "wy", [(0, 1), (1, 0)])
     full = jnp.where(me == 0, jnp.stack([half, other]), jnp.stack([other, half]))
     return full.reshape(x.shape).astype(x.dtype), rider
@@ -116,10 +118,12 @@
 
 def solution(mesh):
     sizes = dict(mesh.shape)
+    z_size = sizes["walker"] // 2
+    near = 4 if z_size % 4 == 0 else z_size
     split = Mesh(
-        mesh.devices.reshape(sizes["walker"] // 2, 2, sizes["orb"]), ("wz", "wy", "orb")
+        mesh.devices.reshape(z_size // near, near, 2, sizes["orb"]), ("za", "zb", "wy", "orb")
     )
-    walker = ("wz", "wy")
+    walker = ("za", "zb", "wy")
     in_specs = (
         P(walker),
         P(walker, None),

time: 121 us -> 127 us (1.050)
  blocking collectives: 60.8 us -> 67.2 us
    all_to_all x1 -> x2, blocking collectives: 37.1 us -> 41.3 us  [reduce_scatter_by_all_to_all(): return jnp.sum(lax.all_to_all(parts, axis, 0, 0, tiled=True), axis=0)]
    all_to_all x1 -> x2, blocking collectives: 23.7 us -> 25.8 us  [gather_by_all_to_all(): return lax.all_to_all(copies, axis, 0, 0, tiled=True)]
  transfers between devices with their start and end apart: 4 -> 4, of which waited for: 3 -> 3; matrix products, arithmetic and copies ran while one was open for 9% -> 8% of each run, Pallas kernels for 0% -> 0%
where the time goes in v7:
time: 127 us
  blocking collectives  67.2 us (53%)
  waiting for transfers between devices  22.3 us (18%)
  starting transfers between devices  16.3 us (13%)
  matrix products  9.94 us (8%)
  other arithmetic  6.42 us (5%)
  local copies, waits for them, and re-layouts  3.63 us (3%)
    all_to_all x2, blocking collectives, reduce_scatter_by_all_to_all(): return jnp.sum(lax.all_to_all(parts, axis, 0, 0, tiled=True), axis=0)  41.3 us
    all_to_all x2, blocking collectives, gather_by_all_to_all(): return lax.all_to_all(copies, axis, 0, 0, tiled=True)  25.8 us
    all_to_all x1, waiting for transfers between devices, gather_by_all_to_all(): return lax.all_to_all(copies, axis, 0, 0, tiled=True)  9.8 us
    all_to_all x1, waiting for transfers between devices, reduce_scatter_by_all_to_all(): return jnp.sum(lax.all_to_all(parts, axis, 0, 0, tiled=True), axis=0)  7.58 us
    all_to_all x1, starting transfers between devices, gather_by_all_to_all(): return lax.all_to_all(copies, axis, 0, 0, tiled=True)  7.08 us
    dot_general x1, matrix products, body(): jnp.dot(stencil_matrix, spline_table, preferred_element_type=jnp.float32)  5.76 us
    ppermute x1, waiting for transfers between devices, all_reduce_walker(): other = lax.ppermute(half, 'wy', [(0, 1), (1, 0)])  4.88 us
    all_to_all x1, starting transfers between devices, reduce_scatter_by_all_to_all(): return jnp.sum(lax.all_to_all(parts, axis, 0, 0, tiled=True), axis=0)  3.95 us
  transfers between devices with their start and end apart: 4, of which 3 were waited for; matrix products, arithmetic and copies ran while one was open for 8% of the time, Pallas kernels for 0%

profile of v7, /device:TPU:32, one launch (start us, length us, event | category | flops | bytes accessed | tf_op | source)
XLA Modules:
  0.0 126.5 jit_solution(3092188085677372930)
XLA Ops:
  0.6 0.0 copy-start
  0.6 0.0 copy-start.4
  0.7 0.0 copy-start.2
  0.7 2.1 %broadcast_in_dim.11 = bf16[16,48,768]{2,1,0:T(8,128)(2,1)} broadcast(bf16[48,768]{1,0:T(8,128)(2,1)} %bitcast.32), dimensions={1,2} | broadcast | bytes 1253376 | tf_op jit(solution)/shard_map/broadcast_in_dim | solution.py:71
  2.8 7.1 %all-to-all-start = ((bf16[16,48,768]{2,1,0:T(8,128)(2,1)}), bf16[16,48,768]{2,1,0:T(8,128)(2,1)}, u32[]{:S(2)}, u32[]{:S(2)}) async-start(bf16[16,48,768]{2,1,0:T(8,128)(2,1)} %broadcast_in_dim.11), calls=%async_computation | async-start | bytes 2359296 | tf_op jit(solution)/shard_map/all_to_all | solution.py:72
  9.9 0.0 copy-done.4
  9.9 0.0 copy-done.2
  9.9 3.8 %broadcast_multiply_fusion = bf16[1024,64,64]{0,2,1:T(8,128)(2,1)} fusion(bf16[1024,64]{0,1:T(8,128)(2,1)S(1)} %copy-done.2, bf16[1024,64]{0,1:T(8,128)(2,1)S(1)} %fusion.12), kind=kLoop, calls=%fused_computation | loop fusion | flops 4194304 | bytes 8650752 | tf_op jit(solution)/shard_map/mul | solution.py:91
  13.7 0.0 copy-done
  13.7 5.8 %convolution_convert_fusion = bf16[1024,256]{0,1:T(8,128)(2,1)S(1)} fusion(bf16[1024,4096]{0,1:T(8,128)(2,1)} %bitcast.23, bf16[4096,256]{1,0:T(8,128)(2,1)S(1)} %copy-done), kind=kOutput, calls=%fused_computation.10 | convolution fusion | flops 2147745792 | bytes 11010048 | tf_op jit(solution)/shard_map/dot_general | solution.py:94
  19.5 9.8 %all-to-all-done = bf16[16,48,768]{2,1,0:T(8,128)(2,1)} async-done(((bf16[16,48,768]{2,1,0:T(8,128)(2,1)}), bf16[16,48,768]{2,1,0:T(8,128)(2,1)}, u32[]{:S(2)}, u32[]{:S(2)}) %all-to-all-start) | async-done | bytes 1179680 | tf_op jit(solution)/shard_map/all_to_all | solution.py:72
  29.3 0.0 copy-done.5
  29.3 2.8 %fusion = f32[1024,768]{1,0:T(8,128)S(1)} fusion(bf16[768,768]{1,0:T(8,128)(2,1)} %bitcast.2, s32[1024]{0:T(1024)S(1)} %copy-done.5), kind=kOutput, calls=%fused_computation.3 | convolution fusion | flops 1208745984 | bytes 4329472 | tf_op jit(solution)/shard_map/dot_general | solution.py:100
  32.1 0.0 copy-done.3
  32.1 0.0 copy-start.1
  32.1 0.7 fusion.1
  32.9 0.8 dynamic-slice_bitcast_fusion
  33.7 2.6 %collective-permute-start = (f32[128,768]{1,0:T(8,128)}, f32[128,768]{1,0:T(8,128)}, u32[]{:S(2)}, u32[]{:S(2)}) collective-permute-start(f32[128,768]{1,0:T(8,128)} %dynamic-slice_bitcast_fusion), channel_id=1, source_target_pairs={{0,16},{16,0},{1,17},{17,1},{2,18},{18,2},{3,19},{19,3},{4,20},{20... | collective-permute-start | bytes 1179656 | tf_op jit(solution)/shard_map/ppermute | solution.py:58
  36.3 0.6 fusion.9
  36.9 0.7 all_to_all.22
  37.6 3.9 %all-to-all-start.1 = ((f32[16,1,64]{2,1,0:T(1,128)}), f32[16,1,64]{2,1,0:T(1,128)S(1)}, u32[]{:S(2)}, u32[]{:S(2)}) async-start(f32[16,1,64]{2,1,0:T(1,128)} %all_to_all.22), calls=%async_computation.1 | async-start | bytes 16384 | tf_op jit(solution)/shard_map/all_to_all | solution.py:78
  41.5 7.6 %all-to-all-done.1 = f32[16,1,64]{2,1,0:T(1,128)S(1)} async-done(((f32[16,1,64]{2,1,0:T(1,128)}), f32[16,1,64]{2,1,0:T(1,128)S(1)}, u32[]{:S(2)}, u32[]{:S(2)}) %all-to-all-start.1) | async-done | bytes 4128 | tf_op jit(solution)/shard_map/all_to_all | solution.py:78
  49.1 0.5 reduce_sum.37
  49.6 0.0 collective-permute-done
  49.6 1.0 bitcast_add_fusion
  50.7 15.7 %all_to_all.34 = f32[4,32,768]{2,1,0:T(8,128)S(1)} all-to-all(f32[4,32,768]{2,1,0:T(8,128)S(1)} %bitcast.26), channel_id=1, replica_groups=mesh['za'=4,'zb'=4,'wy'=2,'orb'=16] {'zb'}, dimensions={0} | all-to-all | bytes 786432 | tf_op jit(solution)/shard_map/all_to_all | solution.py:78
  66.4 25.7 %all_to_all.35 = f32[4,8,768]{2,1,0:T(8,128)S(1)} all-to-all(f32[4,8,768]{2,1,0:T(8,128)S(1)} %bitcast.29), channel_id=1, replica_groups=mesh['za'=4,'zb'=4,'wy'=2,'orb'=16] {'za'}, dimensions={0} | all-to-all | bytes 196608 | tf_op jit(solution)/shard_map/all_to_all | solution.py:78
  92.1 16.3 %all_to_all.36 = bf16[4,8,768]{2,1,0:T(8,128)(2,1)S(1)} all-to-all(bf16[4,8,768]{2,1,0:T(8,128)(2,1)S(1)} %broadcast_in_dim.12), channel_id=1, replica_groups=mesh['za'=4,'zb'=4,'wy'=2,'orb'=16] {'za'}, dimensions={0} | all-to-all | bytes 98304 | tf_op jit(solution)/shard_map/all_to_all | solution.py:72
  108.4 9.5 %all_to_all.37 = bf16[4,32,768]{2,1,0:T(8,128)(2,1)S(1)} all-to-all(bf16[4,32,768]{2,1,0:T(8,128)(2,1)S(1)} %broadcast_in_dim.14), channel_id=1, replica_groups=mesh['za'=4,'zb'=4,'wy'=2,'orb'=16] {'zb'}, dimensions={0} | all-to-all | bytes 393216 | tf_op jit(solution)/shard_map/all_to_all | solution.py:72
  117.9 2.7 %collective-permute-start.1 = (bf16[128,768]{1,0:T(8,128)(2,1)S(1)}, bf16[128,768]{1,0:T(8,128)(2,1)S(1)}, u32[]{:S(2)}, u32[]{:S(2)}) collective-permute-start(bf16[128,768]{1,0:T(8,128)(2,1)S(1)} %bitcast.27), channel_id=1, source_target_pairs={{0,16},{16,0},{1,17},{17,1},{2,18},{18,2},{3,19},{19,3},{4,20},{20... | collective-permute-start | bytes 589832 | tf_op jit(solution)/shard_map/ppermute | solution.py:64
  120.6 4.9 %collective-permute-done.1 = bf16[128,768]{1,0:T(8,128)(2,1)S(1)} collective-permute-done((bf16[128,768]{1,0:T(8,128)(2,1)S(1)}, bf16[128,768]{1,0:T(8,128)(2,1)S(1)}, u32[]{:S(2)}, u32[]{:S(2)}) %collective-permute-start.1) | collective-permute-done | bytes 196640 | tf_op jit(solution)/shard_map/ppermute | solution.py:64
  125.5 1.0 bitcast_convert_fusion
  (9 shorter events, 0.1 us)
Async XLA Ops:
  0.6 13.1 %copy-start = (bf16[4096,256]{1,0:T(8,128)(2,1)S(1)}, bf16[4096,256]{1,0:T(8,128)(2,1)}, u32[]{:S(2)}) copy-start(bf16[4096,256]{1,0:T(8,128)(2,1)} %param.11) | copy-start | bytes 6291460
  0.6 9.2 %copy-start.4 = (s32[1024]{0:T(1024)S(1)}, s32[1024]{0:T(1024)}, u32[]{:S(2)}) copy-start(s32[1024]{0:T(1024)} %param.7) | copy-start | bytes 12292
  0.7 9.3 %copy-start.2 = (bf16[1024,64]{0,1:T(8,128)(2,1)S(1)}, bf16[1024,64]{0,1:T(8,128)(2,1)}, u32[]{:S(2)}) copy-start(bf16[1024,64]{0,1:T(8,128)(2,1)} %param.8) | copy-start | bytes 393220
  2.8 26.5 %all-to-all-start = ((bf16[16,48,768]{2,1,0:T(8,128)(2,1)}), bf16[16,48,768]{2,1,0:T(8,128)(2,1)}, u32[]{:S(2)}, u32[]{:S(2)}) async-start(bf16[16,48,768]{2,1,0:T(8,128)(2,1)} %broadcast_in_dim.11), calls=%async_computation | async-start | bytes 2359296 | tf_op jit(solution)/shard_map/all_to_all | solution.py:72
  13.7 15.6 %copy-start.5 = (s32[1024]{0:T(1024)S(1)}, s32[1024]{0:T(1024)}, u32[]{:S(2)}) copy-start(s32[1024]{0:T(1024)} %param.9) | copy-start | bytes 12292
  29.3 2.8 %copy-start.3 = (f32[1024]{0:T(1024)S(1)}, f32[1024]{0:T(1024)}, u32[]{:S(2)}) copy-start(f32[1024]{0:T(1024)} %param.10) | copy-start | bytes 12292
  32.1 4.1 %copy-start.1 = (bf16[256,768]{1,0:T(8,128)(2,1)S(1)}, bf16[256,768]{1,0:T(8,128)(2,1)}, u32[]{:S(2)}) copy-start(bf16[256,768]{1,0:T(8,128)(2,1)} %param.12) | copy-start | bytes 1179652
  33.7 16.0 %collective-permute-start = (f32[128,768]{1,0:T(8,128)}, f32[128,768]{1,0:T(8,128)}, u32[]{:S(2)}, u32[]{:S(2)}) collective-permute-start(f32[128,768]{1,0:T(8,128)} %dynamic-slice_bitcast_fusion), channel_id=1, source_target_pairs={{0,16},{16,0},{1,17},{17,1},{2,18},{18,2},{3,19},{19,3},{4,20},{20... | collective-permute-start | bytes 1179656 | tf_op jit(solution)/shard_map/ppermute | solution.py:58
  37.6 11.5 %all-to-all-start.1 = ((f32[16,1,64]{2,1,0:T(1,128)}), f32[16,1,64]{2,1,0:T(1,128)S(1)}, u32[]{:S(2)}, u32[]{:S(2)}) async-start(f32[16,1,64]{2,1,0:T(1,128)} %all_to_all.22), calls=%async_computation.1 | async-start | bytes 16384 | tf_op jit(solution)/shard_map/all_to_all | solution.py:78
  117.9 7.6 %collective-permute-start.1 = (bf16[128,768]{1,0:T(8,128)(2,1)S(1)}, bf16[128,768]{1,0:T(8,128)(2,1)S(1)}, u32[]{:S(2)}, u32[]{:S(2)}) collective-permute-start(bf16[128,768]{1,0:T(8,128)(2,1)S(1)} %bitcast.27), channel_id=1, source_target_pairs={{0,16},{16,0},{1,17},{17,1},{2,18},{18,2},{3,19},{19,3},{4,20},{20... | collective-permute-start | bytes 589832 | tf_op jit(solution)/shard_map/ppermute | solution.py:64

commit v8 on v6

--- a/solution.py
+++ b/solution.py
@@ -81,8 +81,11 @@
     coeffs = weights.shape[1]
     tiles_count = spline_table.shape[0] // coeffs
     electrons = inverse.shape[2]
-    _, orb_bits = _bits("orb")
-    inverse_full = gather_by_all_to_all(inverse[0], "orb").reshape(-1, electrons)
+    own_core = gather_by_all_to_all(inverse[0], "oq")
+    core = lax.axis_index("oc")
+    other_core = lax.ppermute(own_core, "oc", [(0, 1), (1, 0)])
+    pair = jnp.where(core == 0, jnp.stack([own_core, other_core], 1), jnp.stack([other_core, own_core], 1))
+    inverse_full = pair.reshape(-1, electrons)
     onehot = (tile_index[:, None] == jnp.arange(tiles_count, dtype=jnp.int32)[None, :]).astype(
         jnp.bfloat16
     )
@@ -109,7 +112,7 @@
         preferred_element_type=jnp.float32,
     )
     partial_ratio = jnp.sum(orbital_values.astype(jnp.float32) * rotated_columns, axis=1)
-    ratios = reduce_scatter_by_all_to_all(partial_ratio, "orb")
+    ratios = reduce_scatter_by_all_to_all(partial_ratio, ("oq", "oc"))
     gradient, ratios = all_reduce_walker(local_gradient, ratios)
     return (ratios, gradient)
 
@@ -117,17 +120,19 @@
 def solution(mesh):
     sizes = dict(mesh.shape)
     split = Mesh(
-        mesh.devices.reshape(sizes["walker"] // 2, 2, sizes["orb"]), ("wz", "wy", "orb")
+        mesh.devices.reshape(sizes["walker"] // 2, 2, sizes["orb"] // 2, 2),
+        ("wz", "wy", "oq", "oc"),
     )
     walker = ("wz", "wy")
+    orb = ("oq", "oc")
     in_specs = (
         P(walker),
         P(walker, None),
         P(walker),
         P(walker),
-        P(None, "orb"),
-        P("orb", None),
-        P(walker, "orb", None),
+        P(None, orb),
+        P(orb, None),
+        P(walker, orb, None),
     )
-    out_specs = (P(walker + ("orb",)), P("orb", None))
+    out_specs = (P(walker + orb), P(orb, None))
     return jax.shard_map(body, mesh=split, in_specs=in_specs, out_specs=out_specs, check_vma=False)

time: 121 us -> 118 us (0.975)
  waiting for transfers between devices: 22.6 us -> 19.2 us
  starting transfers between devices: 16.3 us -> 18.1 us
  matrix products: 9.94 us -> 8.66 us
    all_to_all x1, waiting for transfers between devices: 9.79 us -> 6.1 us  [gather_by_all_to_all(): return lax.all_to_all(copies, axis, 0, 0, tiled=True)]
    ppermute x0 -> x1, starting transfers between devices: none -> 1.91 us  [body(): other_core = lax.ppermute(own_core, 'oc', [(0, 1), (1, 0)])]
    dot_general x1, matrix products: 2.81 us -> 1.54 us  [body(): lax.dot_general(pick, inverse_full, (((1,), (1,)), ((), ())), preferred_e...]
  transfers between devices with their start and end apart: 4 -> 5, of which waited for: 3 -> 3; matrix products, arithmetic and copies ran while one was open for 9% -> 10% of each run, Pallas kernels for 0% -> 0%
where the time goes in v8:
time: 118 us
  blocking collectives  59.8 us (51%)
  waiting for transfers between devices  19.2 us (16%)
  starting transfers between devices  18.1 us (15%)
  matrix products  8.66 us (7%)
  other arithmetic  7.11 us (6%)
  local copies, waits for them, and re-layouts  3.93 us (3%)
    all_to_all x1, blocking collectives, reduce_scatter_by_all_to_all(): return jnp.sum(lax.all_to_all(parts, axis, 0, 0, tiled=True), axis=0)  36.8 us
    all_to_all x1, blocking collectives, gather_by_all_to_all(): return lax.all_to_all(copies, axis, 0, 0, tiled=True)  23 us
    all_to_all x1, waiting for transfers between devices, reduce_scatter_by_all_to_all(): return jnp.sum(lax.all_to_all(parts, axis, 0, 0, tiled=True), axis=0)  7.59 us
    all_to_all x1, starting transfers between devices, gather_by_all_to_all(): return lax.all_to_all(copies, axis, 0, 0, tiled=True)  6.93 us
    all_to_all x1, waiting for transfers between devices, gather_by_all_to_all(): return lax.all_to_all(copies, axis, 0, 0, tiled=True)  6.1 us
    dot_general x1, matrix products, body(): jnp.dot(stencil_matrix, spline_table, preferred_element_type=jnp.float32)  5.75 us
    ppermute x1, waiting for transfers between devices, all_reduce_walker(): other = lax.ppermute(half, 'wy', [(0, 1), (1, 0)])  5.46 us
    mul x1, other arithmetic, body(): onehot[:, :, None] * weights[:, None, :]  4.67 us
  transfers between devices with their start and end apart: 5, of which 3 were waited for; matrix products, arithmetic and copies ran while one was open for 10% of the time, Pallas kernels for 0%

profile of v8, /device:TPU:32, one launch (start us, length us, event | category | flops | bytes accessed | tf_op | source)
XLA Modules:
  0.0 117.6 jit_solution(7207745577924800094)
XLA Ops:
  0.6 0.0 copy-start
  0.6 1.9 %broadcast_in_dim.7 = bf16[8,48,768]{2,1,0:T(8,128)(2,1)} broadcast(bf16[48,768]{1,0:T(8,128)(2,1)} %bitcast.33), dimensions={1,2} | broadcast | bytes 663552 | tf_op jit(solution)/shard_map/broadcast_in_dim | solution.py:69
  2.5 6.9 %all-to-all-start = ((bf16[8,48,768]{2,1,0:T(8,128)(2,1)}), bf16[8,48,768]{2,1,0:T(8,128)(2,1)S(1)}, u32[]{:S(2)}, u32[]{:S(2)}) async-start(bf16[8,48,768]{2,1,0:T(8,128)(2,1)} %broadcast_in_dim.7), calls=%async_computation | async-start | bytes 1179648 | tf_op jit(solution)/shard_map/all_to_all | solution.py:70
  9.5 0.7 fusion.12
  10.2 4.7 %broadcast_multiply_fusion = bf16[1024,64,64]{0,2,1:T(8,128)(2,1)} fusion(bf16[1024,64]{0,1:T(8,128)(2,1)} %param.8, bf16[1024,64]{0,1:T(8,128)(2,1)S(1)} %fusion.12), kind=kLoop, calls=%fused_computation | loop fusion | flops 4194304 | bytes 8650752 | tf_op jit(solution)/shard_map/mul | solution.py:92
  14.9 6.1 %all-to-all-done = bf16[8,48,768]{2,1,0:T(8,128)(2,1)S(1)} async-done(((bf16[8,48,768]{2,1,0:T(8,128)(2,1)}), bf16[8,48,768]{2,1,0:T(8,128)(2,1)S(1)}, u32[]{:S(2)}, u32[]{:S(2)}) %all-to-all-start) | async-done | bytes 589856 | tf_op jit(solution)/shard_map/all_to_all | solution.py:70
  21.0 1.9 %collective-permute-start = (bf16[8,48,768]{2,1,0:T(8,128)(2,1)S(1)}, bf16[8,48,768]{2,1,0:T(8,128)(2,1)S(1)}, u32[]{:S(2)}, u32[]{:S(2)}) collective-permute-start(bf16[8,48,768]{2,1,0:T(8,128)(2,1)S(1)} %all-to-all-done), channel_id=1, source_target_pairs={{0,1},{1,0},{2,3},{3,2},{4,5},{5,4},{6,7},{7,6},{8,9},{9,8},{10,11... | collective-permute-start | bytes 1769480 | tf_op jit(solution)/shard_map/ppermute | solution.py:86
  22.9 0.0 copy-done
  22.9 5.8 %convolution_convert_fusion = bf16[1024,256]{0,1:T(8,128)(2,1)S(1)} fusion(bf16[1024,4096]{0,1:T(8,128)(2,1)} %bitcast.23, bf16[4096,256]{1,0:T(8,128)(2,1)S(1)} %copy-done), kind=kOutput, calls=%fused_computation.10 | convolution fusion | flops 2147745792 | bytes 11010048 | tf_op jit(solution)/shard_map/dot_general | solution.py:95
  28.6 0.0 copy-start.3
  28.7 0.0 collective-permute-done
  28.7 0.1 maximum_select_fusion
  28.8 0.5 copy-done.3
  29.3 0.0 copy-start.2
  29.3 1.5 %fusion = f32[1024,768]{1,0:T(8,128)S(1)} fusion(bf16[768,768]{1,0:T(8,128)(2,1)S(1)} %bitcast.28, s32[1024]{0:T(1024)S(1)} %copy-done.3), kind=kOutput, calls=%fused_computation.3 | convolution fusion | flops 1208745984 | bytes 4329472 | tf_op jit(solution)/shard_map/dot_general | solution.py:101
  30.9 0.0 copy-done.2
  30.9 0.0 copy-start.1
  30.9 0.7 fusion.1
  31.6 0.8 dynamic-slice_bitcast_fusion
  32.4 2.6 %collective-permute-start.1 = (f32[128,768]{1,0:T(8,128)}, f32[128,768]{1,0:T(8,128)S(1)}, u32[]{:S(2)}, u32[]{:S(2)}) collective-permute-start(f32[128,768]{1,0:T(8,128)} %dynamic-slice_bitcast_fusion), channel_id=1, source_target_pairs={{0,16},{16,0},{1,17},{17,1},{2,18},{18,2},{3,19},{19,3},{4,20},{20... | collective-permute-start | bytes 1179656 | tf_op jit(solution)/shard_map/ppermute | solution.py:58
  35.0 0.0 copy-done.1
  35.0 0.6 fusion.9
  35.7 0.7 all_to_all.16
  36.3 4.2 %all-to-all-start.1 = ((f32[16,1,64]{2,1,0:T(1,128)}), f32[16,1,64]{2,1,0:T(1,128)S(1)}, u32[]{:S(2)}, u32[]{:S(2)}) async-start(f32[16,1,64]{2,1,0:T(1,128)} %all_to_all.16), calls=%async_computation.1 | async-start | bytes 16384 | tf_op jit(solution)/shard_map/all_to_all | solution.py:76
  40.6 7.6 %all-to-all-done.1 = f32[16,1,64]{2,1,0:T(1,128)S(1)} async-done(((f32[16,1,64]{2,1,0:T(1,128)}), f32[16,1,64]{2,1,0:T(1,128)S(1)}, u32[]{:S(2)}, u32[]{:S(2)}) %all-to-all-start.1) | async-done | bytes 4128 | tf_op jit(solution)/shard_map/all_to_all | solution.py:76
  48.2 0.5 reduce_sum.28
  48.7 0.0 collective-permute-done.1
  48.8 36.8 %all_to_all.24 = f32[16,8,768]{2,1,0:T(8,128)S(1)} all-to-all(f32[16,8,768]{2,1,0:T(8,128)S(1)} %bitcast.27), channel_id=1, replica_groups=mesh['wz'=16,'wy'=2,'oq'=8,'oc'=2] {'wz'}, dimensions={0} | all-to-all | bytes 786432 | tf_op jit(solution)/shard_map/all_to_all | solution.py:76
  85.6 23.0 %all_to_all.25 = bf16[16,8,768]{2,1,0:T(8,128)(2,1)S(1)} all-to-all(bf16[16,8,768]{2,1,0:T(8,128)(2,1)S(1)} %broadcast_in_dim.8), channel_id=1, replica_groups=mesh['wz'=16,'wy'=2,'oq'=8,'oc'=2] {'wz'}, dimensions={0} | all-to-all | bytes 393216 | tf_op jit(solution)/shard_map/all_to_all | solution.py:70
  108.6 2.4 %collective-permute-start.2 = (bf16[128,768]{1,0:T(8,128)(2,1)S(1)}, bf16[128,768]{1,0:T(8,128)(2,1)S(1)}, u32[]{:S(2)}, u32[]{:S(2)}) collective-permute-start(bf16[128,768]{1,0:T(8,128)(2,1)S(1)} %bitcast.29), channel_id=1, source_target_pairs={{0,16},{16,0},{1,17},{17,1},{2,18},{18,2},{3,19},{19,3},{4,20},{20... | collective-permute-start | bytes 589832 | tf_op jit(solution)/shard_map/ppermute | solution.py:62
  111.1 5.5 %collective-permute-done.2 = bf16[128,768]{1,0:T(8,128)(2,1)S(1)} collective-permute-done((bf16[128,768]{1,0:T(8,128)(2,1)S(1)}, bf16[128,768]{1,0:T(8,128)(2,1)S(1)}, u32[]{:S(2)}, u32[]{:S(2)}) %collective-permute-start.2) | collective-permute-done | bytes 196640 | tf_op jit(solution)/shard_map/ppermute | solution.py:62
  116.6 1.0 bitcast_convert_fusion
  (4 shorter events, 0.1 us)
Async XLA Ops:
  0.6 22.2 %copy-start = (bf16[4096,256]{1,0:T(8,128)(2,1)S(1)}, bf16[4096,256]{1,0:T(8,128)(2,1)}, u32[]{:S(2)}) copy-start(bf16[4096,256]{1,0:T(8,128)(2,1)} %param.11) | copy-start | bytes 6291460
  2.5 18.4 %all-to-all-start = ((bf16[8,48,768]{2,1,0:T(8,128)(2,1)}), bf16[8,48,768]{2,1,0:T(8,128)(2,1)S(1)}, u32[]{:S(2)}, u32[]{:S(2)}) async-start(bf16[8,48,768]{2,1,0:T(8,128)(2,1)} %broadcast_in_dim.7), calls=%async_computation | async-start | bytes 1179648 | tf_op jit(solution)/shard_map/all_to_all | solution.py:70
  21.0 7.7 %collective-permute-start = (bf16[8,48,768]{2,1,0:T(8,128)(2,1)S(1)}, bf16[8,48,768]{2,1,0:T(8,128)(2,1)S(1)}, u32[]{:S(2)}, u32[]{:S(2)}) collective-permute-start(bf16[8,48,768]{2,1,0:T(8,128)(2,1)S(1)} %all-to-all-done), channel_id=1, source_target_pairs={{0,1},{1,0},{2,3},{3,2},{4,5},{5,4},{6,7},{7,6},{8,9},{9,8},{10,11... | collective-permute-start | bytes 1769480 | tf_op jit(solution)/shard_map/ppermute | solution.py:86
  28.6 0.7 copy-start.3
  29.3 1.6 %copy-start.2 = (f32[1024]{0:T(1024)S(1)}, f32[1024]{0:T(1024)}, u32[]{:S(2)}) copy-start(f32[1024]{0:T(1024)} %param.10) | copy-start | bytes 12292
  30.9 4.1 %copy-start.1 = (bf16[256,768]{1,0:T(8,128)(2,1)S(1)}, bf16[256,768]{1,0:T(8,128)(2,1)}, u32[]{:S(2)}) copy-start(bf16[256,768]{1,0:T(8,128)(2,1)} %param.12) | copy-start | bytes 1179652
  32.4 16.3 %collective-permute-start.1 = (f32[128,768]{1,0:T(8,128)}, f32[128,768]{1,0:T(8,128)S(1)}, u32[]{:S(2)}, u32[]{:S(2)}) collective-permute-start(f32[128,768]{1,0:T(8,128)} %dynamic-slice_bitcast_fusion), channel_id=1, source_target_pairs={{0,16},{16,0},{1,17},{17,1},{2,18},{18,2},{3,19},{19,3},{4,20},{20... | collective-permute-start | bytes 1179656 | tf_op jit(solution)/shard_map/ppermute | solution.py:58
  36.3 11.8 %all-to-all-start.1 = ((f32[16,1,64]{2,1,0:T(1,128)}), f32[16,1,64]{2,1,0:T(1,128)S(1)}, u32[]{:S(2)}, u32[]{:S(2)}) async-start(f32[16,1,64]{2,1,0:T(1,128)} %all_to_all.16), calls=%async_computation.1 | async-start | bytes 16384 | tf_op jit(solution)/shard_map/all_to_all | solution.py:76
  108.6 7.9 %collective-permute-start.2 = (bf16[128,768]{1,0:T(8,128)(2,1)S(1)}, bf16[128,768]{1,0:T(8,128)(2,1)S(1)}, u32[]{:S(2)}, u32[]{:S(2)}) collective-permute-start(bf16[128,768]{1,0:T(8,128)(2,1)S(1)} %bitcast.29), channel_id=1, source_target_pairs={{0,16},{16,0},{1,17},{17,1},{2,18},{18,2},{3,19},{19,3},{4,20},{20... | collective-permute-start | bytes 589832 | tf_op jit(solution)/shard_map/ppermute | solution.py:62

commit v9 on v8

--- a/solution.py
+++ b/solution.py
@@ -81,11 +81,6 @@
     coeffs = weights.shape[1]
     tiles_count = spline_table.shape[0] // coeffs
     electrons = inverse.shape[2]
-    own_core = gather_by_all_to_all(inverse[0], "oq")
-    core = lax.axis_index("oc")
-    other_core = lax.ppermute(own_core, "oc", [(0, 1), (1, 0)])
-    pair = jnp.where(core == 0, jnp.stack([own_core, other_core], 1), jnp.stack([other_core, own_core], 1))
-    inverse_full = pair.reshape(-1, electrons)
     onehot = (tile_index[:, None] == jnp.arange(tiles_count, dtype=jnp.int32)[None, :]).astype(
         jnp.bfloat16
     )
@@ -95,6 +90,12 @@
     orbital_values = jnp.dot(
         stencil_matrix, spline_table, preferred_element_type=jnp.float32
     ).astype(jnp.bfloat16)
+    own_core = gather_by_all_to_all(inverse[0], "oq")
+    orbital_values, own_core = lax.optimization_barrier((orbital_values, own_core))
+    core = lax.axis_index("oc")
+    other_core = lax.ppermute(own_core, "oc", [(0, 1), (1, 0)])
+    pair = jnp.where(core == 0, jnp.stack([own_core, other_core], 1), jnp.stack([other_core, own_core], 1))
+    inverse_full = pair.reshape(-1, electrons)
     pick = (electron[:, None] == jnp.arange(electrons, dtype=jnp.int32)[None, :]).astype(
         jnp.bfloat16
     )

time: 118 us -> 116 us (0.983)
  the two profiles are of different devices: /device:TPU:32 before, /device:TPU:34 now
where the time goes in v9:
time: 116 us
  blocking collectives  60.8 us (52%)
  starting transfers between devices  19.7 us (17%)
  waiting for transfers between devices  19.4 us (17%)
  other arithmetic  6.16 us (5%)
  matrix products  5.46 us (5%)
  local copies, waits for them, and re-layouts  3.39 us (3%)
    all_to_all x1, blocking collectives, reduce_scatter_by_all_to_all(): return jnp.sum(lax.all_to_all(parts, axis, 0, 0, tiled=True), axis=0)  37.1 us
    all_to_all x1, blocking collectives, gather_by_all_to_all(): return lax.all_to_all(copies, axis, 0, 0, tiled=True)  23.7 us
    all_to_all x1, starting transfers between devices, gather_by_all_to_all(): return lax.all_to_all(copies, axis, 0, 0, tiled=True)  7.46 us
    all_to_all x1, waiting for transfers between devices, reduce_scatter_by_all_to_all(): return jnp.sum(lax.all_to_all(parts, axis, 0, 0, tiled=True), axis=0)  6.07 us
    ppermute x1, waiting for transfers between devices, all_reduce_walker(): other = lax.ppermute(half, 'wy', [(0, 1), (1, 0)])  5.64 us
    all_to_all x1, waiting for transfers between devices, gather_by_all_to_all(): return lax.all_to_all(copies, axis, 0, 0, tiled=True)  5.59 us
    all_to_all x1, starting transfers between devices, reduce_scatter_by_all_to_all(): return jnp.sum(lax.all_to_all(parts, axis, 0, 0, tiled=True), axis=0)  5.41 us
    ppermute x1, starting transfers between devices, all_reduce_walker(): half = keep + lax.ppermute(_pick(halves, 1 - me), 'wy', [(0, 1), (1, 0)])  2.57 us
  transfers between devices with their start and end apart: 5, of which 4 were waited for; matrix products, arithmetic and copies ran while one was open for 5% of the time, Pallas kernels for 0%

profile of v9, /device:TPU:34, one launch (start us, length us, event | category | flops | bytes accessed | tf_op | source)
XLA Modules:
  0.0 115.7 jit_solution(1378194459910954226)
XLA Ops:
  0.6 0.0 copy-start
  0.6 1.9 %broadcast_in_dim.7 = bf16[8,48,768]{2,1,0:T(8,128)(2,1)} broadcast(bf16[48,768]{1,0:T(8,128)(2,1)} %bitcast.32), dimensions={1,2} | broadcast | bytes 663552 | tf_op jit(solution)/shard_map/broadcast_in_dim | solution.py:69
  2.5 7.5 %all-to-all-start = ((bf16[8,48,768]{2,1,0:T(8,128)(2,1)}), bf16[8,48,768]{2,1,0:T(8,128)(2,1)S(1)}, u32[]{:S(2)}, u32[]{:S(2)}) async-start(bf16[8,48,768]{2,1,0:T(8,128)(2,1)} %broadcast_in_dim.7), calls=%async_computation | async-start | bytes 1179648 | tf_op jit(solution)/shard_map/all_to_all | solution.py:70
  10.0 0.7 fusion.12
  10.7 1.5 %broadcast_multiply_fusion = bf16[1024,64,64]{0,2,1:T(8,128)(2,1)S(1)} fusion(bf16[1024,64]{0,1:T(8,128)(2,1)} %param.8, bf16[1024,64]{0,1:T(8,128)(2,1)S(1)} %fusion.12), kind=kLoop, calls=%fused_computation | loop fusion | flops 4194304 | bytes 8650752 | tf_op jit(solution)/shard_map/mul | solution.py:87
  12.2 0.0 copy-done
  12.2 2.5 %convolution_convert_fusion = bf16[1024,256]{1,0:T(8,128)(2,1)S(1)} fusion(bf16[1024,4096]{0,1:T(8,128)(2,1)S(1)} %bitcast.23, bf16[4096,256]{1,0:T(8,128)(2,1)S(1)} %copy-done), kind=kOutput, calls=%fused_computation.10 | convolution fusion | flops 2147745792 | bytes 11010048 | tf_op jit(solution)/shard_map/dot_general | solution.py:90
  14.6 0.0 copy-start.3
  14.6 5.6 %all-to-all-done = bf16[8,48,768]{2,1,0:T(8,128)(2,1)S(1)} async-done(((bf16[8,48,768]{2,1,0:T(8,128)(2,1)}), bf16[8,48,768]{2,1,0:T(8,128)(2,1)S(1)}, u32[]{:S(2)}, u32[]{:S(2)}) %all-to-all-start) | async-done | bytes 589856 | tf_op jit(solution)/shard_map/all_to_all | solution.py:70
  20.2 1.9 %collective-permute-start = (bf16[8,48,768]{2,1,0:T(8,128)(2,1)S(1)}, bf16[8,48,768]{2,1,0:T(8,128)(2,1)}, u32[]{:S(2)}, u32[]{:S(2)}) collective-permute-start(bf16[8,48,768]{2,1,0:T(8,128)(2,1)S(1)} %all-to-all-done), channel_id=1, source_target_pairs={{0,1},{1,0},{2,3},{3,2},{4,5},{5,4},{6,7},{7,6},{8,9},{9,8},{10,11... | collective-permute-start | bytes 1769480 | tf_op jit(solution)/shard_map/ppermute | solution.py:96
  22.2 2.1 %collective-permute-done = bf16[8,48,768]{2,1,0:T(8,128)(2,1)} collective-permute-done((bf16[8,48,768]{2,1,0:T(8,128)(2,1)S(1)}, bf16[8,48,768]{2,1,0:T(8,128)(2,1)}, u32[]{:S(2)}, u32[]{:S(2)}) %collective-permute-start) | collective-permute-done | bytes 589856 | tf_op jit(solution)/shard_map/ppermute | solution.py:96
  24.3 1.4 %maximum_select_fusion = bf16[8,2,48,768]{3,2,1,0:T(8,128)(2,1)S(1)} fusion(bf16[8,1,48,768]{3,2,1,0:T(8,128)(2,1)} %bitcast.3, bf16[8,1,48,768]{3,2,1,0:T(8,128)(2,1)S(1)} %bitcast.26, pred[]{:T(512)S(6)} %eq.42), kind=kLoop, calls=%fused_computation.12 | loop fusion | flops 1769472 | bytes 2359297 | tf_op jit(solution)/shard_map/jit(_where)/select_n | solution.py:97
  25.6 0.0 copy-done.3
  25.7 0.0 copy-start.2
  25.7 1.5 %fusion = f32[1024,768]{1,0:T(8,128)S(1)} fusion(bf16[768,768]{1,0:T(8,128)(2,1)S(1)} %bitcast.28, s32[1024]{0:T(1024)S(1)} %copy-done.3), kind=kOutput, calls=%fused_computation.3 | convolution fusion | flops 1208745984 | bytes 4329472 | tf_op jit(solution)/shard_map/dot_general | solution.py:102
  27.2 0.0 copy-start.1
  27.2 0.8 fusion.1
  28.0 0.8 dynamic-slice_bitcast_fusion
  28.8 2.6 %collective-permute-start.1 = (f32[128,768]{1,0:T(8,128)}, f32[128,768]{1,0:T(8,128)}, u32[]{:S(2)}, u32[]{:S(2)}) collective-permute-start(f32[128,768]{1,0:T(8,128)} %dynamic-slice_bitcast_fusion), channel_id=1, source_target_pairs={{0,16},{16,0},{1,17},{17,1},{2,18},{18,2},{3,19},{19,3},{4,20},{20... | collective-permute-start | bytes 1179656 | tf_op jit(solution)/shard_map/ppermute | solution.py:58
  31.4 0.0 copy-done.1
  31.4 0.7 fusion.9
  32.1 0.7 all_to_all.16
  32.8 5.4 %all-to-all-start.1 = ((f32[16,1,64]{2,1,0:T(1,128)}), f32[16,1,64]{2,1,0:T(1,128)S(1)}, u32[]{:S(2)}, u32[]{:S(2)}) async-start(f32[16,1,64]{2,1,0:T(1,128)} %all_to_all.16), calls=%async_computation.1 | async-start | bytes 16384 | tf_op jit(solution)/shard_map/all_to_all | solution.py:76
  38.2 6.1 %all-to-all-done.1 = f32[16,1,64]{2,1,0:T(1,128)S(1)} async-done(((f32[16,1,64]{2,1,0:T(1,128)}), f32[16,1,64]{2,1,0:T(1,128)S(1)}, u32[]{:S(2)}, u32[]{:S(2)}) %all-to-all-start.1) | async-done | bytes 4128 | tf_op jit(solution)/shard_map/all_to_all | solution.py:76
  44.2 0.5 reduce_sum.28
  44.8 0.0 collective-permute-done.1
  44.8 1.0 bitcast_add_fusion
  45.8 37.1 %all_to_all.24 = f32[16,8,768]{2,1,0:T(8,128)S(1)} all-to-all(f32[16,8,768]{2,1,0:T(8,128)S(1)} %bitcast.27), channel_id=1, replica_groups=mesh['wz'=16,'wy'=2,'oq'=8,'oc'=2] {'wz'}, dimensions={0} | all-to-all | bytes 786432 | tf_op jit(solution)/shard_map/all_to_all | solution.py:76
  82.9 23.7 %all_to_all.25 = bf16[16,8,768]{2,1,0:T(8,128)(2,1)S(1)} all-to-all(bf16[16,8,768]{2,1,0:T(8,128)(2,1)S(1)} %broadcast_in_dim.8), channel_id=1, replica_groups=mesh['wz'=16,'wy'=2,'oq'=8,'oc'=2] {'wz'}, dimensions={0} | all-to-all | bytes 393216 | tf_op jit(solution)/shard_map/all_to_all | solution.py:70
  106.7 2.4 %collective-permute-start.2 = (bf16[128,768]{1,0:T(8,128)(2,1)S(1)}, bf16[128,768]{1,0:T(8,128)(2,1)S(1)}, u32[]{:S(2)}, u32[]{:S(2)}) collective-permute-start(bf16[128,768]{1,0:T(8,128)(2,1)S(1)} %bitcast.29), channel_id=1, source_target_pairs={{0,16},{16,0},{1,17},{17,1},{2,18},{18,2},{3,19},{19,3},{4,20},{20... | collective-permute-start | bytes 589832 | tf_op jit(solution)/shard_map/ppermute | solution.py:62
  109.1 5.6 %collective-permute-done.2 = bf16[128,768]{1,0:T(8,128)(2,1)S(1)} collective-permute-done((bf16[128,768]{1,0:T(8,128)(2,1)S(1)}, bf16[128,768]{1,0:T(8,128)(2,1)S(1)}, u32[]{:S(2)}, u32[]{:S(2)}) %collective-permute-start.2) | collective-permute-done | bytes 196640 | tf_op jit(solution)/shard_map/ppermute | solution.py:62
  114.8 1.0 bitcast_convert_fusion
  (4 shorter events, 0.1 us)
Async XLA Ops:
  0.6 11.5 %copy-start = (bf16[4096,256]{1,0:T(8,128)(2,1)S(1)}, bf16[4096,256]{1,0:T(8,128)(2,1)}, u32[]{:S(2)}) copy-start(bf16[4096,256]{1,0:T(8,128)(2,1)} %param.11) | copy-start | bytes 6291460
  2.5 17.7 %all-to-all-start = ((bf16[8,48,768]{2,1,0:T(8,128)(2,1)}), bf16[8,48,768]{2,1,0:T(8,128)(2,1)S(1)}, u32[]{:S(2)}, u32[]{:S(2)}) async-start(bf16[8,48,768]{2,1,0:T(8,128)(2,1)} %broadcast_in_dim.7), calls=%async_computation | async-start | bytes 1179648 | tf_op jit(solution)/shard_map/all_to_all | solution.py:70
  14.6 11.0 %copy-start.3 = (s32[1024]{0:T(1024)S(1)}, s32[1024]{0:T(1024)}, u32[]{:S(2)}) copy-start(s32[1024]{0:T(1024)} %param.9) | copy-start | bytes 12292
  20.2 4.0 %collective-permute-start = (bf16[8,48,768]{2,1,0:T(8,128)(2,1)S(1)}, bf16[8,48,768]{2,1,0:T(8,128)(2,1)}, u32[]{:S(2)}, u32[]{:S(2)}) collective-permute-start(bf16[8,48,768]{2,1,0:T(8,128)(2,1)S(1)} %all-to-all-done), channel_id=1, source_target_pairs={{0,1},{1,0},{2,3},{3,2},{4,5},{5,4},{6,7},{7,6},{8,9},{9,8},{10,11... | collective-permute-start | bytes 1769480 | tf_op jit(solution)/shard_map/ppermute | solution.py:96
  25.7 1.6 %copy-start.2 = (f32[1024]{0:T(1024)S(1)}, f32[1024]{0:T(1024)}, u32[]{:S(2)}) copy-start(f32[1024]{0:T(1024)} %param.10) | copy-start | bytes 12292
  27.2 4.1 %copy-start.1 = (bf16[256,768]{1,0:T(8,128)(2,1)S(1)}, bf16[256,768]{1,0:T(8,128)(2,1)}, u32[]{:S(2)}) copy-start(bf16[256,768]{1,0:T(8,128)(2,1)} %param.12) | copy-start | bytes 1179652
  28.8 16.0 %collective-permute-start.1 = (f32[128,768]{1,0:T(8,128)}, f32[128,768]{1,0:T(8,128)}, u32[]{:S(2)}, u32[]{:S(2)}) collective-permute-start(f32[128,768]{1,0:T(8,128)} %dynamic-slice_bitcast_fusion), channel_id=1, source_target_pairs={{0,16},{16,0},{1,17},{17,1},{2,18},{18,2},{3,19},{19,3},{4,20},{20... | collective-permute-start | bytes 1179656 | tf_op jit(solution)/shard_map/ppermute | solution.py:58
  32.8 11.5 %all-to-all-start.1 = ((f32[16,1,64]{2,1,0:T(1,128)}), f32[16,1,64]{2,1,0:T(1,128)S(1)}, u32[]{:S(2)}, u32[]{:S(2)}) async-start(f32[16,1,64]{2,1,0:T(1,128)} %all_to_all.16), calls=%async_computation.1 | async-start | bytes 16384 | tf_op jit(solution)/shard_map/all_to_all | solution.py:76
  106.7 8.0 %collective-permute-start.2 = (bf16[128,768]{1,0:T(8,128)(2,1)S(1)}, bf16[128,768]{1,0:T(8,128)(2,1)S(1)}, u32[]{:S(2)}, u32[]{:S(2)}) collective-permute-start(bf16[128,768]{1,0:T(8,128)(2,1)S(1)} %bitcast.29), channel_id=1, source_target_pairs={{0,16},{16,0},{1,17},{17,1},{2,18},{18,2},{3,19},{19,3},{4,20},{20... | collective-permute-start | bytes 589832 | tf_op jit(solution)/shard_map/ppermute | solution.py:62

commit v10 on v9

--- a/solution.py
+++ b/solution.py
@@ -94,26 +94,43 @@
     orbital_values, own_core = lax.optimization_barrier((orbital_values, own_core))
     core = lax.axis_index("oc")
     other_core = lax.ppermute(own_core, "oc", [(0, 1), (1, 0)])
-    pair = jnp.where(core == 0, jnp.stack([own_core, other_core], 1), jnp.stack([other_core, own_core], 1))
-    inverse_full = pair.reshape(-1, electrons)
     pick = (electron[:, None] == jnp.arange(electrons, dtype=jnp.int32)[None, :]).astype(
         jnp.bfloat16
     )
-    columns = lax.dot_general(
-        pick, inverse_full, (((1,), (1,)), ((), ())), preferred_element_type=jnp.float32
-    )
-    adjoint = (columns * strength[:, None]).astype(jnp.bfloat16)
-    local_gradient = lax.dot_general(
-        orbital_values, adjoint, (((0,), (0,)), ((), ())), preferred_element_type=jnp.float32
-    )
-    rotated_columns = lax.dot_general(
-        columns.astype(jnp.bfloat16),
-        rotation,
-        (((1,), (1,)), ((), ())),
-        preferred_element_type=jnp.float32,
-    )
+    rows_per_block = inverse.shape[1]
+    blocks = own_core.shape[0]
+    rotation_blocks = rotation.reshape(rotation.shape[0], blocks, 2, rows_per_block)
+
+    def half_terms(half_inverse, position):
+        columns = lax.dot_general(
+            pick,
+            half_inverse.reshape(-1, electrons),
+            (((1,), (1,)), ((), ())),
+            preferred_element_type=jnp.float32,
+        )
+        adjoint = (columns * strength[:, None]).astype(jnp.bfloat16)
+        gradient_half = lax.dot_general(
+            orbital_values, adjoint, (((0,), (0,)), ((), ())), preferred_element_type=jnp.float32
+        )
+        rotation_half = lax.dynamic_index_in_dim(rotation_blocks, position, 2, keepdims=False)
+        rotated_half = lax.dot_general(
+            columns.astype(jnp.bfloat16),
+            rotation_half.reshape(rotation.shape[0], -1),
+            (((1,), (1,)), ((), ())),
+            preferred_element_type=jnp.float32,
+        )
+        return gradient_half.reshape(-1, blocks, rows_per_block), rotated_half
+
+    own_gradient, own_rotated = half_terms(own_core, core)
+    other_gradient, other_rotated = half_terms(other_core, 1 - core)
+    rotated_columns = own_rotated + other_rotated
     partial_ratio = jnp.sum(orbital_values.astype(jnp.float32) * rotated_columns, axis=1)
     ratios = reduce_scatter_by_all_to_all(partial_ratio, ("oq", "oc"))
+    local_gradient = jnp.where(
+        core == 0,
+        jnp.stack([own_gradient, other_gradient], 2),
+        jnp.stack([other_gradient, own_gradient], 2),
+    ).reshape(orbital_values.shape[1], -1)
     gradient, ratios = all_reduce_walker(local_gradient, ratios)
     return (ratios, gradient)
 

time: 116 us -> 124 us (1.069)
  the two profiles are of different devices: /device:TPU:34 before, /device:TPU:32 now
where the time goes in v10:
time: 124 us
  blocking collectives  59.8 us (48%)
  starting transfers between devices  19.7 us (16%)
  waiting for transfers between devices  14.9 us (12%)
  matrix products  13.7 us (11%)
  local copies, waits for them, and re-layouts  9.24 us (7%)
  other arithmetic  5.48 us (4%)
    all_to_all x1, blocking collectives, reduce_scatter_by_all_to_all(): return jnp.sum(lax.all_to_all(parts, axis, 0, 0, tiled=True), axis=0)  36.8 us
    all_to_all x1, blocking collectives, gather_by_all_to_all(): return lax.all_to_all(copies, axis, 0, 0, tiled=True)  23 us
    all_to_all x1, waiting for transfers between devices, reduce_scatter_by_all_to_all(): return jnp.sum(lax.all_to_all(parts, axis, 0, 0, tiled=True), axis=0)  7.25 us
    all_to_all x1, starting transfers between devices, gather_by_all_to_all(): return lax.all_to_all(copies, axis, 0, 0, tiled=True)  6.93 us
    all_to_all x1, starting transfers between devices, reduce_scatter_by_all_to_all(): return jnp.sum(lax.all_to_all(parts, axis, 0, 0, tiled=True), axis=0)  6.13 us
    ppermute x1, waiting for transfers between devices, all_reduce_walker(): other = lax.ppermute(half, 'wy', [(0, 1), (1, 0)])  5.86 us
    dot_general x1, matrix products, body(): jnp.dot(stencil_matrix, spline_table, preferred_element_type=jnp.float32)  5.77 us
    dot_general x2, matrix products, half_terms(): lax.dot_general(pick, half_inverse.reshape(-1, electrons), (((1,), (1,)),...  4.19 us
  transfers between devices with their start and end apart: 5, of which 3 were waited for; matrix products, arithmetic and copies ran while one was open for 13% of the time, Pallas kernels for 0%

profile of v10, /device:TPU:32, one launch (start us, length us, event | category | flops | bytes accessed | tf_op | source)
XLA Modules:
  0.0 123.8 jit_solution(1049276518130571596)
XLA Ops:
  0.7 1.9 %broadcast_in_dim.7 = bf16[8,48,768]{2,1,0:T(8,128)(2,1)} broadcast(bf16[48,768]{1,0:T(8,128)(2,1)} %bitcast.43), dimensions={1,2} | broadcast | bytes 663552 | tf_op jit(solution)/shard_map/broadcast_in_dim | solution.py:69
  2.6 6.9 %all-to-all-start = ((bf16[8,48,768]{2,1,0:T(8,128)(2,1)}), bf16[8,48,768]{2,1,0:T(8,128)(2,1)}, u32[]{:S(2)}, u32[]{:S(2)}) async-start(bf16[8,48,768]{2,1,0:T(8,128)(2,1)} %broadcast_in_dim.7), calls=%async_computation | async-start | bytes 1179648 | tf_op jit(solution)/shard_map/all_to_all | solution.py:70
  9.5 0.2 copy.45
  9.7 3.8 %broadcast_multiply_fusion = bf16[1024,64,64]{0,2,1:T(8,128)(2,1)} fusion(bf16[1024,64]{0,1:T(8,128)(2,1)S(1)} %copy-done.6, bf16[1024,64]{0,1:T(8,128)(2,1)S(1)} %fusion.13), kind=kLoop, calls=%fused_computation | loop fusion | flops 4194304 | bytes 8650752 | tf_op jit(solution)/shard_map/mul | solution.py:87
  13.5 5.8 %convolution_convert_fusion = bf16[1024,256]{1,0:T(8,128)(2,1)S(1)} fusion(bf16[1024,4096]{0,1:T(8,128)(2,1)} %bitcast.32, bf16[4096,256]{1,0:T(8,128)(2,1)S(1)} %copy-done), kind=kOutput, calls=%fused_computation.10 | convolution fusion | flops 2147745792 | bytes 11010048 | tf_op jit(solution)/shard_map/dot_general | solution.py:90
  19.3 1.8 %all-to-all-done = bf16[8,48,768]{2,1,0:T(8,128)(2,1)} async-done(((bf16[8,48,768]{2,1,0:T(8,128)(2,1)}), bf16[8,48,768]{2,1,0:T(8,128)(2,1)}, u32[]{:S(2)}, u32[]{:S(2)}) %all-to-all-start) | async-done | bytes 589856 | tf_op jit(solution)/shard_map/all_to_all | solution.py:70
  21.1 1.9 %collective-permute-start = (bf16[8,48,768]{2,1,0:T(8,128)(2,1)}, bf16[8,48,768]{2,1,0:T(8,128)(2,1)}, u32[]{:S(2)}, u32[]{:S(2)}) collective-permute-start(bf16[8,48,768]{2,1,0:T(8,128)(2,1)} %all-to-all-done), channel_id=1, source_target_pairs={{0,1},{1,0},{2,3},{3,2},{4,5},{5,4},{6,7},{7,6},{8,9},{9,8},{10,11... | collective-permute-start | bytes 1769480 | tf_op jit(solution)/shard_map/ppermute | solution.py:96
  23.0 0.8 constant_dynamic-slice_fusion
  23.8 2.1 %fusion.1 = f32[1024,384]{1,0:T(8,128)S(1)} fusion(bf16[384,768]{1,0:T(8,128)(2,1)} %bitcast.2, s32[1024]{0:T(1024)S(1)} %copy-done.9), kind=kOutput, calls=%fused_computation.3 | convolution fusion | flops 604766208 | bytes 2166784 | tf_op jit(solution)/shard_map/dot_general | solution.py:105
  25.9 0.7 fusion.6
  26.7 0.4 copy-done.3
  27.1 2.1 %fusion = f32[1024,384]{1,0:T(8,128)S(1)} fusion(bf16[384,768]{1,0:T(8,128)(2,1)} %bitcast.4, s32[1024]{0:T(1024)S(1)} %copy-done.9), kind=kOutput, calls=%fused_computation.2 | convolution fusion | flops 604766208 | bytes 2166784 | tf_op jit(solution)/shard_map/dot_general | solution.py:105
  29.2 0.7 fusion.7
  29.9 0.1 maximum_select_fusion
  30.0 0.4 copy-done.1
  30.3 0.1 copy.42
  30.4 1.3 %select_n.38 = f32[2,128,768]{1,0,2:T(2,128)} reshape(f32[256,8,2,48]{0,3,2,1:T(8,128)S(1)} %copy.42) | data formatting | bytes 1572864 | tf_op jit(solution)/shard_map/jit(_where)/select_n | solution.py:129
  31.7 2.2 %constant_dynamic-slice_fusion.3 = (f32[1,128,768]{1,0,2:T(1,128)S(1)}, f32[1,128,768]{1,0,2:T(1,128)S(1)}) fusion(f32[2,128,768]{1,0,2:T(2,128)} %select_n.38, s32[]{:T(128)S(6)} %select_n.39, s32[]{:T(128)S(6)} %select_n.40), kind=kLoop, calls=%fused_computation.28 | loop fusion | bytes 1572872 | tf_op jit(solution)/shard_map/jit(dynamic_index_in_dim)/dynamic_slice | solution.py:20
  33.9 1.0 copy.44
  34.9 2.7 %collective-permute-start.1 = (f32[128,768]{1,0:T(8,128)}, f32[128,768]{1,0:T(8,128)S(1)}, u32[]{:S(2)}, u32[]{:S(2)}) collective-permute-start(f32[128,768]{1,0:T(8,128)} %bitcast.41), channel_id=1, source_target_pairs={{0,16},{16,0},{1,17},{17,1},{2,18},{18,2},{3,19},{19,3},{4,20},{20... | collective-permute-start | bytes 1179656 | tf_op jit(solution)/shard_map/ppermute | solution.py:58
  37.6 1.8 %fusion.9 = f32[1024,256]{1,0:T(8,128)S(1)} fusion(bf16[256,384]{0,1:T(8,128)(2,1)} %bitcast.40, f32[1024,384]{1,0:T(8,128)} %copy-done.3), kind=kOutput, calls=%fused_computation.16 | convolution fusion | flops 201719808 | bytes 2818048 | tf_op jit(solution)/shard_map/dot_general | solution.py:116
  39.4 0.5 fusion.5
  40.0 0.7 all_to_all.16
  40.6 6.1 %all-to-all-start.1 = ((f32[16,1,64]{2,1,0:T(1,128)}), f32[16,1,64]{2,1,0:T(1,128)S(1)}, u32[]{:S(2)}, u32[]{:S(2)}) async-start(f32[16,1,64]{2,1,0:T(1,128)} %all_to_all.16), calls=%async_computation.1 | async-start | bytes 16384 | tf_op jit(solution)/shard_map/all_to_all | solution.py:76
  46.8 0.3 copy.43
  47.1 7.2 %all-to-all-done.1 = f32[16,1,64]{2,1,0:T(1,128)S(1)} async-done(((f32[16,1,64]{2,1,0:T(1,128)}), f32[16,1,64]{2,1,0:T(1,128)S(1)}, u32[]{:S(2)}, u32[]{:S(2)}) %all-to-all-start.1) | async-done | bytes 4128 | tf_op jit(solution)/shard_map/all_to_all | solution.py:76
  54.4 0.5 reduce_sum.28
  54.9 36.8 %all_to_all.24 = f32[16,8,768]{2,1,0:T(8,128)S(1)} all-to-all(f32[16,8,768]{2,1,0:T(8,128)S(1)} %bitcast.36), channel_id=1, replica_groups=mesh['wz'=16,'wy'=2,'oq'=8,'oc'=2] {'wz'}, dimensions={0} | all-to-all | bytes 786432 | tf_op jit(solution)/shard_map/all_to_all | solution.py:76
  91.8 23.0 %all_to_all.25 = bf16[16,8,768]{2,1,0:T(8,128)(2,1)S(1)} all-to-all(bf16[16,8,768]{2,1,0:T(8,128)(2,1)S(1)} %broadcast_in_dim.8), channel_id=1, replica_groups=mesh['wz'=16,'wy'=2,'oq'=8,'oc'=2] {'wz'}, dimensions={0} | all-to-all | bytes 393216 | tf_op jit(solution)/shard_map/all_to_all | solution.py:70
  114.8 2.0 %collective-permute-start.2 = (bf16[128,768]{1,0:T(8,128)(2,1)S(1)}, bf16[128,768]{1,0:T(8,128)(2,1)S(1)}, u32[]{:S(2)}, u32[]{:S(2)}) collective-permute-start(bf16[128,768]{1,0:T(8,128)(2,1)S(1)} %bitcast.38), channel_id=1, source_target_pairs={{0,16},{16,0},{1,17},{17,1},{2,18},{18,2},{3,19},{19,3},{4,20},{20... | collective-permute-start | bytes 589832 | tf_op jit(solution)/shard_map/ppermute | solution.py:62
  116.9 5.9 %collective-permute-done.2 = bf16[128,768]{1,0:T(8,128)(2,1)S(1)} collective-permute-done((bf16[128,768]{1,0:T(8,128)(2,1)S(1)}, bf16[128,768]{1,0:T(8,128)(2,1)S(1)}, u32[]{:S(2)}, u32[]{:S(2)}) %collective-permute-start.2) | collective-permute-done | bytes 196640 | tf_op jit(solution)/shard_map/ppermute | solution.py:62
  122.8 1.0 bitcast_convert_fusion
  (25 shorter events, 0.2 us)
Async XLA Ops:
  0.6 12.9 %copy-start = (bf16[4096,256]{1,0:T(8,128)(2,1)S(1)}, bf16[4096,256]{1,0:T(8,128)(2,1)}, u32[]{:S(2)}) copy-start(bf16[4096,256]{1,0:T(8,128)(2,1)} %param.11) | copy-start | bytes 6291460
  0.6 8.9 %copy-start.8 = (s32[1024]{0:T(1024)S(1)}, s32[1024]{0:T(1024)}, u32[]{:S(2)}) copy-start(s32[1024]{0:T(1024)} %param.7) | copy-start | bytes 12292
  0.7 8.9 %copy-start.5 = (bf16[256,768]{1,0:T(8,128)(2,1)S(1)}, bf16[256,768]{1,0:T(8,128)(2,1)}, u32[]{:S(2)}) copy-start(bf16[256,768]{1,0:T(8,128)(2,1)} %param.12) | copy-start | bytes 1179652
  0.7 9.1 %copy-start.6 = (bf16[1024,64]{0,1:T(8,128)(2,1)S(1)}, bf16[1024,64]{0,1:T(8,128)(2,1)}, u32[]{:S(2)}) copy-start(bf16[1024,64]{0,1:T(8,128)(2,1)} %param.8) | copy-start | bytes 393220
  2.6 18.5 %all-to-all-start = ((bf16[8,48,768]{2,1,0:T(8,128)(2,1)}), bf16[8,48,768]{2,1,0:T(8,128)(2,1)}, u32[]{:S(2)}, u32[]{:S(2)}) async-start(bf16[8,48,768]{2,1,0:T(8,128)(2,1)} %broadcast_in_dim.7), calls=%async_computation | async-start | bytes 1179648 | tf_op jit(solution)/shard_map/all_to_all | solution.py:70
  13.5 10.3 %copy-start.9 = (s32[1024]{0:T(1024)S(1)}, s32[1024]{0:T(1024)}, u32[]{:S(2)}) copy-start(s32[1024]{0:T(1024)} %param.9) | copy-start | bytes 12292
  21.1 5.5 %collective-permute-start = (bf16[8,48,768]{2,1,0:T(8,128)(2,1)}, bf16[8,48,768]{2,1,0:T(8,128)(2,1)}, u32[]{:S(2)}, u32[]{:S(2)}) collective-permute-start(bf16[8,48,768]{2,1,0:T(8,128)(2,1)} %all-to-all-done), channel_id=1, source_target_pairs={{0,1},{1,0},{2,3},{3,2},{4,5},{5,4},{6,7},{7,6},{8,9},{9,8},{10,11... | collective-permute-start | bytes 1769480 | tf_op jit(solution)/shard_map/ppermute | solution.py:96
  23.8 2.1 %copy-start.7 = (f32[1024]{0:T(1024)S(1)}, f32[1024]{0:T(1024)}, u32[]{:S(2)}) copy-start(f32[1024]{0:T(1024)} %param.10) | copy-start | bytes 12292
  25.9 1.2 copy-start.3
  29.2 1.2 copy-start.1
  34.9 4.6 %copy-start.2 = (f32[1024,384]{1,0:T(8,128)S(1)}, f32[1024,384]{1,0:T(8,128)}, u32[]{:S(2)}) copy-start(f32[1024,384]{1,0:T(8,128)} %copy-done.1) | copy-start | bytes 4718596
  34.9 4.6 %copy-start.4 = (bf16[256,8,1,48]{0,3,2,1:T(8,128)(2,1)S(1)}, bf16[256,8,1,48]{0,3,2,1:T(8,128)(2,1)}, u32[]{:S(2)}) copy-start(bf16[256,8,1,48]{0,3,2,1:T(8,128)(2,1)} %get-tuple-element.12) | copy-start | bytes 589828
  34.9 20.0 %collective-permute-start.1 = (f32[128,768]{1,0:T(8,128)}, f32[128,768]{1,0:T(8,128)S(1)}, u32[]{:S(2)}, u32[]{:S(2)}) collective-permute-start(f32[128,768]{1,0:T(8,128)} %bitcast.41), channel_id=1, source_target_pairs={{0,16},{16,0},{1,17},{17,1},{2,18},{18,2},{3,19},{19,3},{4,20},{20... | collective-permute-start | bytes 1179656 | tf_op jit(solution)/shard_map/ppermute | solution.py:58
  40.6 13.7 %all-to-all-start.1 = ((f32[16,1,64]{2,1,0:T(1,128)}), f32[16,1,64]{2,1,0:T(1,128)S(1)}, u32[]{:S(2)}, u32[]{:S(2)}) async-start(f32[16,1,64]{2,1,0:T(1,128)} %all_to_all.16), calls=%async_computation.1 | async-start | bytes 16384 | tf_op jit(solution)/shard_map/all_to_all | solution.py:76
  114.8 7.9 %collective-permute-start.2 = (bf16[128,768]{1,0:T(8,128)(2,1)S(1)}, bf16[128,768]{1,0:T(8,128)(2,1)S(1)}, u32[]{:S(2)}, u32[]{:S(2)}) collective-permute-start(bf16[128,768]{1,0:T(8,128)(2,1)S(1)} %bitcast.38), channel_id=1, source_target_pairs={{0,16},{16,0},{1,17},{17,1},{2,18},{18,2},{3,19},{19,3},{4,20},{20... | collective-permute-start | bytes 589832 | tf_op jit(solution)/shard_map/ppermute | solution.py:62

commit v11 on v9

--- a/solution.py
+++ b/solution.py
@@ -114,7 +114,10 @@
     )
     partial_ratio = jnp.sum(orbital_values.astype(jnp.float32) * rotated_columns, axis=1)
     ratios = reduce_scatter_by_all_to_all(partial_ratio, ("oq", "oc"))
-    gradient, ratios = all_reduce_walker(local_gradient, ratios)
+    left, right = jnp.split(local_gradient, 2, axis=1)
+    left, ratios = all_reduce_walker(left, ratios)
+    right, _ = all_reduce_walker(right, right[:1, :1])
+    gradient = jnp.concatenate([left, right], axis=1)
     return (ratios, gradient)
 
 

time: 116 us -> 143 us (1.23)
  the two profiles are of different devices: /device:TPU:34 before, /device:TPU:32 now
where the time goes in v11:
time: 143 us; the launch traced here: 142 us
  waiting for transfers between devices  70.3 us (49%)
  starting transfers between devices  53.1 us (37%)
  other arithmetic  7.44 us (5%)
  matrix products  5.45 us (4%)
  local copies, waits for them, and re-layouts  4.66 us (3%)
    all_to_all x3, waiting for transfers between devices, gather_by_all_to_all(): return lax.all_to_all(copies, axis, 0, 0, tiled=True)  30 us
    all_to_all x3, waiting for transfers between devices, reduce_scatter_by_all_to_all(): return jnp.sum(lax.all_to_all(parts, axis, 0, 0, tiled=True), axis=0)  28.2 us
    all_to_all x3, starting transfers between devices, reduce_scatter_by_all_to_all(): return jnp.sum(lax.all_to_all(parts, axis, 0, 0, tiled=True), axis=0)  24.9 us
    all_to_all x3, starting transfers between devices, gather_by_all_to_all(): return lax.all_to_all(copies, axis, 0, 0, tiled=True)  16.5 us
    ppermute x2, waiting for transfers between devices, all_reduce_walker(): half = keep + lax.ppermute(_pick(halves, 1 - me), 'wy', [(0, 1), (1, 0)])  5.94 us
    ppermute x2, starting transfers between devices, all_reduce_walker(): half = keep + lax.ppermute(_pick(halves, 1 - me), 'wy', [(0, 1), (1, 0)])  4.98 us
    ppermute x2, starting transfers between devices, all_reduce_walker(): other = lax.ppermute(half, 'wy', [(0, 1), (1, 0)])  4.8 us
    ppermute x2, waiting for transfers between devices, all_reduce_walker(): other = lax.ppermute(half, 'wy', [(0, 1), (1, 0)])  4.05 us
  transfers between devices with their start and end apart: 11, of which 10 were waited for; matrix products, arithmetic and copies ran while one was open for 6% of the time, Pallas kernels for 0%

profile of v11, /device:TPU:32, one launch (start us, length us, event | category | flops | bytes accessed | tf_op | source)
XLA Modules:
  0.0 141.8 jit_solution(321360671384058215)
XLA Ops:
  0.6 1.9 %broadcast_in_dim.9 = bf16[8,48,768]{2,1,0:T(8,128)(2,1)} broadcast(bf16[48,768]{1,0:T(8,128)(2,1)} %bitcast.46), dimensions={1,2} | broadcast | bytes 663552 | tf_op jit(solution)/shard_map/broadcast_in_dim | solution.py:69
  2.5 6.9 %all-to-all-start = ((bf16[8,48,768]{2,1,0:T(8,128)(2,1)}), bf16[8,48,768]{2,1,0:T(8,128)(2,1)S(1)}, u32[]{:S(2)}, u32[]{:S(2)}) async-start(bf16[8,48,768]{2,1,0:T(8,128)(2,1)} %broadcast_in_dim.9), calls=%async_computation | async-start | bytes 1179648 | tf_op jit(solution)/shard_map/all_to_all | solution.py:70
  9.5 0.7 fusion.12
  10.2 1.5 %broadcast_multiply_fusion = bf16[1024,64,64]{0,2,1:T(8,128)(2,1)S(1)} fusion(bf16[1024,64]{0,1:T(8,128)(2,1)} %param.8, bf16[1024,64]{0,1:T(8,128)(2,1)S(1)} %fusion.12), kind=kLoop, calls=%fused_computation | loop fusion | flops 4194304 | bytes 8650752 | tf_op jit(solution)/shard_map/mul | solution.py:87
  11.6 2.4 %convolution_convert_fusion = bf16[1024,256]{1,0:T(8,128)(2,1)S(1)} fusion(bf16[1024,4096]{0,1:T(8,128)(2,1)S(1)} %bitcast.31, bf16[4096,256]{1,0:T(8,128)(2,1)S(1)} %copy-done), kind=kOutput, calls=%fused_computation.10 | convolution fusion | flops 2147745792 | bytes 11010048 | tf_op jit(solution)/shard_map/dot_general | solution.py:90
  14.1 6.8 %all-to-all-done = bf16[8,48,768]{2,1,0:T(8,128)(2,1)S(1)} async-done(((bf16[8,48,768]{2,1,0:T(8,128)(2,1)}), bf16[8,48,768]{2,1,0:T(8,128)(2,1)S(1)}, u32[]{:S(2)}, u32[]{:S(2)}) %all-to-all-start) | async-done | bytes 589856 | tf_op jit(solution)/shard_map/all_to_all | solution.py:70
  21.0 1.9 %collective-permute-start = (bf16[8,48,768]{2,1,0:T(8,128)(2,1)S(1)}, bf16[8,48,768]{2,1,0:T(8,128)(2,1)}, u32[]{:S(2)}, u32[]{:S(2)}) collective-permute-start(bf16[8,48,768]{2,1,0:T(8,128)(2,1)S(1)} %all-to-all-done), channel_id=1, source_target_pairs={{0,1},{1,0},{2,3},{3,2},{4,5},{5,4},{6,7},{7,6},{8,9},{9,8},{10,11... | collective-permute-start | bytes 1769480 | tf_op jit(solution)/shard_map/ppermute | solution.py:96
  22.9 2.1 %collective-permute-done = bf16[8,48,768]{2,1,0:T(8,128)(2,1)} collective-permute-done((bf16[8,48,768]{2,1,0:T(8,128)(2,1)S(1)}, bf16[8,48,768]{2,1,0:T(8,128)(2,1)}, u32[]{:S(2)}, u32[]{:S(2)}) %collective-permute-start) | collective-permute-done | bytes 589856 | tf_op jit(solution)/shard_map/ppermute | solution.py:96
  25.0 1.4 maximum_select_fusion
  26.4 1.5 %fusion = f32[1024,768]{1,0:T(8,128)S(1)} fusion(bf16[768,768]{1,0:T(8,128)(2,1)S(1)} %bitcast.37, s32[1024]{0:T(1024)S(1)} %copy-done.3), kind=kOutput, calls=%fused_computation.3 | convolution fusion | flops 1208745984 | bytes 4329472 | tf_op jit(solution)/shard_map/dot_general | solution.py:102
  27.9 0.8 fusion.1
  28.8 0.7 dynamic-slice_bitcast_fusion
  29.5 2.6 %collective-permute-start.3 = (f32[128,384]{1,0:T(8,128)}, f32[128,384]{1,0:T(8,128)}, u32[]{:S(2)}, u32[]{:S(2)}) collective-permute-start(f32[128,384]{1,0:T(8,128)} %dynamic-slice_bitcast_fusion), channel_id=1, source_target_pairs={{0,16},{16,0},{1,17},{17,1},{2,18},{18,2},{3,19},{19,3},{4,20},{20... | collective-permute-start | bytes 589832 | tf_op jit(solution)/shard_map/ppermute | solution.py:58
  32.1 0.7 fusion.9
  33.5 4.2 %all-to-all-start.1 = ((f32[16,1,64]{2,1,0:T(1,128)}), f32[16,1,64]{2,1,0:T(1,128)S(1)}, u32[]{:S(2)}, u32[]{:S(2)}) async-start(f32[16,1,64]{2,1,0:T(1,128)} %all_to_all.22), calls=%async_computation.1 | async-start | bytes 16384 | tf_op jit(solution)/shard_map/all_to_all | solution.py:76
  37.7 0.9 collective-permute-done.3
  38.6 1.6 %bitcast_add_fusion = f32[128,384]{1,0:T(8,128)} fusion(f32[128,384]{1,0:T(8,128)} %collective-permute-done.3, f32[2,128,384]{2,1,0:T(8,128)S(1)} %bitcast.36, s32[]{:T(128)S(6)} %select_n.40), kind=kLoop, calls=%fused_computation.18 | loop fusion | flops 49152 | bytes 589828 | tf_op jit(solution)/shard_map/add | solution.py:58
  40.2 5.1 %all-to-all-done.1 = f32[16,1,64]{2,1,0:T(1,128)S(1)} async-done(((f32[16,1,64]{2,1,0:T(1,128)}), f32[16,1,64]{2,1,0:T(1,128)S(1)}, u32[]{:S(2)}, u32[]{:S(2)}) %all-to-all-start.1) | async-done | bytes 4128 | tf_op jit(solution)/shard_map/all_to_all | solution.py:76
  45.3 15.2 %all-to-all-start.4 = ((f32[16,8,384]{2,1,0:T(8,128)}), f32[16,8,384]{2,1,0:T(8,128)S(1)}, u32[]{:S(2)}, u32[]{:S(2)}) async-start(f32[16,8,384]{2,1,0:T(8,128)} %bitcast.17), calls=%async_computation.4 | async-start | bytes 393216 | tf_op jit(solution)/shard_map/all_to_all | solution.py:76
  60.5 2.4 %collective-permute-start.1 = (f32[128,384]{1,0:T(8,128)S(1)}, f32[128,384]{1,0:T(8,128)S(1)}, u32[]{:S(2)}, u32[]{:S(2)}) collective-permute-start(f32[128,384]{1,0:T(8,128)S(1)} %dynamic-slice_bitcast_fusion.1), channel_id=1, source_target_pairs={{0,16},{16,0},{1,17},{17,1},{2,18},{18,2},{3,19},{19,3},{4,20},{20... | collective-permute-start | bytes 589832 | tf_op jit(solution)/shard_map/ppermute | solution.py:58
  63.5 5.0 %collective-permute-done.1 = f32[128,384]{1,0:T(8,128)S(1)} collective-permute-done((f32[128,384]{1,0:T(8,128)S(1)}, f32[128,384]{1,0:T(8,128)S(1)}, u32[]{:S(2)}, u32[]{:S(2)}) %collective-permute-start.1) | collective-permute-done | bytes 196640 | tf_op jit(solution)/shard_map/ppermute | solution.py:58
  69.2 7.2 %all-to-all-done.4 = f32[16,8,384]{2,1,0:T(8,128)S(1)} async-done(((f32[16,8,384]{2,1,0:T(8,128)}), f32[16,8,384]{2,1,0:T(8,128)S(1)}, u32[]{:S(2)}, u32[]{:S(2)}) %all-to-all-start.4) | async-done | bytes 196640 | tf_op jit(solution)/shard_map/all_to_all | solution.py:76
  76.4 5.4 %all-to-all-start.2 = ((f32[16,8,384]{2,1,0:T(8,128)}), f32[16,8,384]{2,1,0:T(8,128)S(1)}, u32[]{:S(2)}, u32[]{:S(2)}) async-start(f32[16,8,384]{2,1,0:T(8,128)} %bitcast.9), calls=%async_computation.2 | async-start | bytes 393216 | tf_op jit(solution)/shard_map/all_to_all | solution.py:76
  81.9 15.9 %all-to-all-done.2 = f32[16,8,384]{2,1,0:T(8,128)S(1)} async-done(((f32[16,8,384]{2,1,0:T(8,128)}), f32[16,8,384]{2,1,0:T(8,128)S(1)}, u32[]{:S(2)}, u32[]{:S(2)}) %all-to-all-start.2) | async-done | bytes 196640 | tf_op jit(solution)/shard_map/all_to_all | solution.py:76
  98.4 5.5 %all-to-all-start.5 = ((bf16[16,8,384]{2,1,0:T(8,128)(2,1)}), bf16[16,8,384]{2,1,0:T(8,128)(2,1)S(1)}, u32[]{:S(2)}, u32[]{:S(2)}) async-start(bf16[16,8,384]{2,1,0:T(8,128)(2,1)} %broadcast_in_dim.11), calls=%async_computation.5 | async-start | bytes 196608 | tf_op jit(solution)/shard_map/all_to_all | solution.py:70
  103.9 13.0 %all-to-all-done.5 = bf16[16,8,384]{2,1,0:T(8,128)(2,1)S(1)} async-done(((bf16[16,8,384]{2,1,0:T(8,128)(2,1)}), bf16[16,8,384]{2,1,0:T(8,128)(2,1)S(1)}, u32[]{:S(2)}, u32[]{:S(2)}) %all-to-all-start.5) | async-done | bytes 98336 | tf_op jit(solution)/shard_map/all_to_all | solution.py:70
  117.6 4.1 %all-to-all-start.3 = ((bf16[16,8,384]{2,1,0:T(8,128)(2,1)}), bf16[16,8,384]{2,1,0:T(8,128)(2,1)S(1)}, u32[]{:S(2)}, u32[]{:S(2)}) async-start(bf16[16,8,384]{2,1,0:T(8,128)(2,1)} %broadcast_in_dim.10), calls=%async_computation.3 | async-start | bytes 196608 | tf_op jit(solution)/shard_map/all_to_all | solution.py:70
  121.7 2.4 %collective-permute-start.4 = (bf16[128,384]{1,0:T(8,128)(2,1)S(1)}, bf16[128,384]{1,0:T(8,128)(2,1)S(1)}, u32[]{:S(2)}, u32[]{:S(2)}) collective-permute-start(bf16[128,384]{1,0:T(8,128)(2,1)S(1)} %bitcast.40), channel_id=1, source_target_pairs={{0,16},{16,0},{1,17},{17,1},{2,18},{18,2},{3,19},{19,3},{4,20},{20... | collective-permute-start | bytes 294920 | tf_op jit(solution)/shard_map/ppermute | solution.py:62
  124.1 10.2 %all-to-all-done.3 = bf16[16,8,384]{2,1,0:T(8,128)(2,1)S(1)} async-done(((bf16[16,8,384]{2,1,0:T(8,128)(2,1)}), bf16[16,8,384]{2,1,0:T(8,128)(2,1)S(1)}, u32[]{:S(2)}, u32[]{:S(2)}) %all-to-all-start.3) | async-done | bytes 98336 | tf_op jit(solution)/shard_map/all_to_all | solution.py:70
  134.3 2.4 %collective-permute-start.2 = (bf16[128,384]{1,0:T(8,128)(2,1)S(1)}, bf16[128,384]{1,0:T(8,128)(2,1)S(1)}, u32[]{:S(2)}, u32[]{:S(2)}) collective-permute-start(bf16[128,384]{1,0:T(8,128)(2,1)S(1)} %bitcast.42), channel_id=1, source_target_pairs={{0,16},{16,0},{1,17},{17,1},{2,18},{18,2},{3,19},{19,3},{4,20},{20... | collective-permute-start | bytes 294920 | tf_op jit(solution)/shard_map/ppermute | solution.py:62
  136.7 4.0 %collective-permute-done.2 = bf16[128,384]{1,0:T(8,128)(2,1)S(1)} collective-permute-done((bf16[128,384]{1,0:T(8,128)(2,1)S(1)}, bf16[128,384]{1,0:T(8,128)(2,1)S(1)}, u32[]{:S(2)}, u32[]{:S(2)}) %collective-permute-start.2) | collective-permute-done | bytes 98336 | tf_op jit(solution)/shard_map/ppermute | solution.py:62
  140.8 0.9 maximum_convert_fusion
  (20 shorter events, 3.4 us)
Async XLA Ops:
  0.6 11.0 %copy-start = (bf16[4096,256]{1,0:T(8,128)(2,1)S(1)}, bf16[4096,256]{1,0:T(8,128)(2,1)}, u32[]{:S(2)}) copy-start(bf16[4096,256]{1,0:T(8,128)(2,1)} %param.11) | copy-start | bytes 6291460
  2.5 18.4 %all-to-all-start = ((bf16[8,48,768]{2,1,0:T(8,128)(2,1)}), bf16[8,48,768]{2,1,0:T(8,128)(2,1)S(1)}, u32[]{:S(2)}, u32[]{:S(2)}) async-start(bf16[8,48,768]{2,1,0:T(8,128)(2,1)} %broadcast_in_dim.9), calls=%async_computation | async-start | bytes 1179648 | tf_op jit(solution)/shard_map/all_to_all | solution.py:70
  14.1 12.3 %copy-start.3 = (s32[1024]{0:T(1024)S(1)}, s32[1024]{0:T(1024)}, u32[]{:S(2)}) copy-start(s32[1024]{0:T(1024)} %param.9) | copy-start | bytes 12292
  21.0 4.0 %collective-permute-start = (bf16[8,48,768]{2,1,0:T(8,128)(2,1)S(1)}, bf16[8,48,768]{2,1,0:T(8,128)(2,1)}, u32[]{:S(2)}, u32[]{:S(2)}) collective-permute-start(bf16[8,48,768]{2,1,0:T(8,128)(2,1)S(1)} %all-to-all-done), channel_id=1, source_target_pairs={{0,1},{1,0},{2,3},{3,2},{4,5},{5,4},{6,7},{7,6},{8,9},{9,8},{10,11... | collective-permute-start | bytes 1769480 | tf_op jit(solution)/shard_map/ppermute | solution.py:96
  26.4 1.6 %copy-start.2 = (f32[1024]{0:T(1024)S(1)}, f32[1024]{0:T(1024)}, u32[]{:S(2)}) copy-start(f32[1024]{0:T(1024)} %param.10) | copy-start | bytes 12292
  28.7 3.4 %copy-start.1 = (bf16[256,768]{1,0:T(8,128)(2,1)S(1)}, bf16[256,768]{1,0:T(8,128)(2,1)}, u32[]{:S(2)}) copy-start(bf16[256,768]{1,0:T(8,128)(2,1)} %param.12) | copy-start | bytes 1179652
  29.5 9.1 %collective-permute-start.3 = (f32[128,384]{1,0:T(8,128)}, f32[128,384]{1,0:T(8,128)}, u32[]{:S(2)}, u32[]{:S(2)}) collective-permute-start(f32[128,384]{1,0:T(8,128)} %dynamic-slice_bitcast_fusion), channel_id=1, source_target_pairs={{0,16},{16,0},{1,17},{17,1},{2,18},{18,2},{3,19},{19,3},{4,20},{20... | collective-permute-start | bytes 589832 | tf_op jit(solution)/shard_map/ppermute | solution.py:58
  33.5 11.8 %all-to-all-start.1 = ((f32[16,1,64]{2,1,0:T(1,128)}), f32[16,1,64]{2,1,0:T(1,128)S(1)}, u32[]{:S(2)}, u32[]{:S(2)}) async-start(f32[16,1,64]{2,1,0:T(1,128)} %all_to_all.22), calls=%async_computation.1 | async-start | bytes 16384 | tf_op jit(solution)/shard_map/all_to_all | solution.py:76
  45.3 31.1 %all-to-all-start.4 = ((f32[16,8,384]{2,1,0:T(8,128)}), f32[16,8,384]{2,1,0:T(8,128)S(1)}, u32[]{:S(2)}, u32[]{:S(2)}) async-start(f32[16,8,384]{2,1,0:T(8,128)} %bitcast.17), calls=%async_computation.4 | async-start | bytes 393216 | tf_op jit(solution)/shard_map/all_to_all | solution.py:76
  60.5 8.0 %collective-permute-start.1 = (f32[128,384]{1,0:T(8,128)S(1)}, f32[128,384]{1,0:T(8,128)S(1)}, u32[]{:S(2)}, u32[]{:S(2)}) collective-permute-start(f32[128,384]{1,0:T(8,128)S(1)} %dynamic-slice_bitcast_fusion.1), channel_id=1, source_target_pairs={{0,16},{16,0},{1,17},{17,1},{2,18},{18,2},{3,19},{19,3},{4,20},{20... | collective-permute-start | bytes 589832 | tf_op jit(solution)/shard_map/ppermute | solution.py:58
  76.4 21.4 %all-to-all-start.2 = ((f32[16,8,384]{2,1,0:T(8,128)}), f32[16,8,384]{2,1,0:T(8,128)S(1)}, u32[]{:S(2)}, u32[]{:S(2)}) async-start(f32[16,8,384]{2,1,0:T(8,128)} %bitcast.9), calls=%async_computation.2 | async-start | bytes 393216 | tf_op jit(solution)/shard_map/all_to_all | solution.py:76
  98.4 18.5 %all-to-all-start.5 = ((bf16[16,8,384]{2,1,0:T(8,128)(2,1)}), bf16[16,8,384]{2,1,0:T(8,128)(2,1)S(1)}, u32[]{:S(2)}, u32[]{:S(2)}) async-start(bf16[16,8,384]{2,1,0:T(8,128)(2,1)} %broadcast_in_dim.11), calls=%async_computation.5 | async-start | bytes 196608 | tf_op jit(solution)/shard_map/all_to_all | solution.py:70
  117.6 16.7 %all-to-all-start.3 = ((bf16[16,8,384]{2,1,0:T(8,128)(2,1)}), bf16[16,8,384]{2,1,0:T(8,128)(2,1)S(1)}, u32[]{:S(2)}, u32[]{:S(2)}) async-start(bf16[16,8,384]{2,1,0:T(8,128)(2,1)} %broadcast_in_dim.10), calls=%async_computation.3 | async-start | bytes 196608 | tf_op jit(solution)/shard_map/all_to_all | solution.py:70
  121.7 15.0 %collective-permute-start.4 = (bf16[128,384]{1,0:T(8,128)(2,1)S(1)}, bf16[128,384]{1,0:T(8,128)(2,1)S(1)}, u32[]{:S(2)}, u32[]{:S(2)}) collective-permute-start(bf16[128,384]{1,0:T(8,128)(2,1)S(1)} %bitcast.40), channel_id=1, source_target_pairs={{0,16},{16,0},{1,17},{17,1},{2,18},{18,2},{3,19},{19,3},{4,20},{20... | collective-permute-start | bytes 294920 | tf_op jit(solution)/shard_map/ppermute | solution.py:62
  134.3 6.5 %collective-permute-start.2 = (bf16[128,384]{1,0:T(8,128)(2,1)S(1)}, bf16[128,384]{1,0:T(8,128)(2,1)S(1)}, u32[]{:S(2)}, u32[]{:S(2)}) collective-permute-start(bf16[128,384]{1,0:T(8,128)(2,1)S(1)} %bitcast.42), channel_id=1, source_target_pairs={{0,16},{16,0},{1,17},{17,1},{2,18},{18,2},{3,19},{19,3},{4,20},{20... | collective-permute-start | bytes 294920 | tf_op jit(solution)/shard_map/ppermute | solution.py:62

commit v12 on v9

--- a/solution.py
+++ b/solution.py
@@ -113,7 +113,9 @@
         preferred_element_type=jnp.float32,
     )
     partial_ratio = jnp.sum(orbital_values.astype(jnp.float32) * rotated_columns, axis=1)
-    ratios = reduce_scatter_by_all_to_all(partial_ratio, ("oq", "oc"))
+    share = partial_ratio.shape[0] // lax.axis_size(("oq", "oc"))
+    slot = lax.axis_index("oq") * lax.axis_size("oc") + lax.axis_index("oc")
+    ratios = lax.dynamic_slice_in_dim(lax.psum(partial_ratio, ("oq", "oc")), slot * share, share)
     gradient, ratios = all_reduce_walker(local_gradient, ratios)
     return (ratios, gradient)
 

time: 116 us -> 140 us (1.21)
  the two profiles are of different devices: /device:TPU:34 before, /device:TPU:32 now
where the time goes in v12:
time: 140 us
  blocking collectives  93.9 us (67%)
  starting transfers between devices  14.5 us (10%)
  waiting for transfers between devices  13.4 us (10%)
  matrix products  7.37 us (5%)
  other arithmetic  5.63 us (4%)
  local copies, waits for them, and re-layouts  4.18 us (3%)
    psum x1, blocking collectives, body(): lax.psum(partial_ratio, ('oq', 'oc'))  35.6 us
    all_to_all x1, blocking collectives, reduce_scatter_by_all_to_all(): return jnp.sum(lax.all_to_all(parts, axis, 0, 0, tiled=True), axis=0)  35 us
    all_to_all x1, blocking collectives, gather_by_all_to_all(): return lax.all_to_all(copies, axis, 0, 0, tiled=True)  23.4 us
    all_to_all x1, starting transfers between devices, gather_by_all_to_all(): return lax.all_to_all(copies, axis, 0, 0, tiled=True)  6.93 us
    all_to_all x1, waiting for transfers between devices, gather_by_all_to_all(): return lax.all_to_all(copies, axis, 0, 0, tiled=True)  6.85 us
    ppermute x1, waiting for transfers between devices, all_reduce_walker(): other = lax.ppermute(half, 'wy', [(0, 1), (1, 0)])  4.41 us
    ppermute x1, starting transfers between devices, all_reduce_walker(): other = lax.ppermute(half, 'wy', [(0, 1), (1, 0)])  3.13 us
  transfers between devices with their start and end apart: 4, of which 3 were waited for; matrix products, arithmetic and copies ran while one was open for 6% of the time, Pallas kernels for 0%

profile of v12, /device:TPU:32, one launch (start us, length us, event | category | flops | bytes accessed | tf_op | source)
XLA Modules:
  0.0 139.8 jit_solution(9458906931129414973)
XLA Ops:
  0.6 0.0 copy-start
  0.6 1.9 %broadcast_in_dim.7 = bf16[8,48,768]{2,1,0:T(8,128)(2,1)} broadcast(bf16[48,768]{1,0:T(8,128)(2,1)} %bitcast.31), dimensions={1,2} | broadcast | bytes 663552 | tf_op jit(solution)/shard_map/broadcast_in_dim | solution.py:69
  2.5 6.9 %all-to-all-start = ((bf16[8,48,768]{2,1,0:T(8,128)(2,1)}), bf16[8,48,768]{2,1,0:T(8,128)(2,1)S(1)}, u32[]{:S(2)}, u32[]{:S(2)}) async-start(bf16[8,48,768]{2,1,0:T(8,128)(2,1)} %broadcast_in_dim.7), calls=%async_computation | async-start | bytes 1179648 | tf_op jit(solution)/shard_map/all_to_all | solution.py:70
  9.5 0.7 fusion.12
  10.2 1.5 %broadcast_multiply_fusion = bf16[1024,64,64]{0,2,1:T(8,128)(2,1)S(1)} fusion(bf16[1024,64]{0,1:T(8,128)(2,1)} %param.8, bf16[1024,64]{0,1:T(8,128)(2,1)S(1)} %fusion.12), kind=kLoop, calls=%fused_computation | loop fusion | flops 4194304 | bytes 8650752 | tf_op jit(solution)/shard_map/mul | solution.py:87
  11.6 0.0 copy-done
  11.6 2.4 %convolution_convert_fusion = bf16[1024,256]{1,0:T(8,128)(2,1)S(1)} fusion(bf16[1024,4096]{0,1:T(8,128)(2,1)S(1)} %bitcast.22, bf16[4096,256]{1,0:T(8,128)(2,1)S(1)} %copy-done), kind=kOutput, calls=%fused_computation.10 | convolution fusion | flops 2147745792 | bytes 11010048 | tf_op jit(solution)/shard_map/dot_general | solution.py:90
  14.1 0.0 copy-start.3
  14.1 6.8 %all-to-all-done = bf16[8,48,768]{2,1,0:T(8,128)(2,1)S(1)} async-done(((bf16[8,48,768]{2,1,0:T(8,128)(2,1)}), bf16[8,48,768]{2,1,0:T(8,128)(2,1)S(1)}, u32[]{:S(2)}, u32[]{:S(2)}) %all-to-all-start) | async-done | bytes 589856 | tf_op jit(solution)/shard_map/all_to_all | solution.py:70
  21.0 1.9 %collective-permute-start = (bf16[8,48,768]{2,1,0:T(8,128)(2,1)S(1)}, bf16[8,48,768]{2,1,0:T(8,128)(2,1)}, u32[]{:S(2)}, u32[]{:S(2)}) collective-permute-start(bf16[8,48,768]{2,1,0:T(8,128)(2,1)S(1)} %all-to-all-done), channel_id=1, source_target_pairs={{0,1},{1,0},{2,3},{3,2},{4,5},{5,4},{6,7},{7,6},{8,9},{9,8},{10,11... | collective-permute-start | bytes 1769480 | tf_op jit(solution)/shard_map/ppermute | solution.py:96
  22.9 2.1 %collective-permute-done = bf16[8,48,768]{2,1,0:T(8,128)(2,1)} collective-permute-done((bf16[8,48,768]{2,1,0:T(8,128)(2,1)S(1)}, bf16[8,48,768]{2,1,0:T(8,128)(2,1)}, u32[]{:S(2)}, u32[]{:S(2)}) %collective-permute-start) | collective-permute-done | bytes 589856 | tf_op jit(solution)/shard_map/ppermute | solution.py:96
  25.0 1.4 maximum_select_fusion
  26.4 0.0 copy-done.3
  26.4 0.0 copy-start.2
  26.4 1.5 %fusion = f32[1024,768]{1,0:T(8,128)S(1)} fusion(bf16[768,768]{1,0:T(8,128)(2,1)S(1)} %bitcast.27, s32[1024]{0:T(1024)S(1)} %copy-done.3), kind=kOutput, calls=%fused_computation.3 | convolution fusion | flops 1208745984 | bytes 4329472 | tf_op jit(solution)/shard_map/dot_general | solution.py:102
  27.9 0.0 copy-done.2
  27.9 0.0 copy-start.1
  28.0 0.7 fusion.1
  28.7 0.9 copy-done.1
  29.6 0.8 dynamic-slice_bitcast_fusion
  30.4 2.6 %collective-permute-start.1 = (f32[128,768]{1,0:T(8,128)}, f32[128,768]{1,0:T(8,128)}, u32[]{:S(2)}, u32[]{:S(2)}) collective-permute-start(f32[128,768]{1,0:T(8,128)} %dynamic-slice_bitcast_fusion), channel_id=1, source_target_pairs={{0,16},{16,0},{1,17},{17,1},{2,18},{18,2},{3,19},{19,3},{4,20},{20... | collective-permute-start | bytes 1179656 | tf_op jit(solution)/shard_map/ppermute | solution.py:58
  33.0 2.6 %fusion.9 = f32[1024]{0:T(1024)S(1)} fusion(bf16[256,768]{1,0:T(8,128)(2,1)} %param.12, f32[1024,768]{1,0:T(8,128)} %copy-done.1, bf16[1024,256]{1,0:T(8,128)(2,1)S(1)} %convolution_convert_fusion), kind=kOutput, calls=%fused_computation.11 | convolution fusion | flops 404225024 | bytes 4067328 | tf_op jit(solution)/shard_map/dot_general | solution.py:109
  35.6 35.6 %psum.7 = f32[1024]{0:T(1024)S(1)} all-reduce(f32[1024]{0:T(1024)S(1)} %fusion.9), channel_id=1, replica_groups=mesh['wz'=16,'wy'=2,'oq'=8,'oc'=2] {'oq','oc'}, use_global_device_ids=true, to_apply=%region_1.2 | all-reduce | flops 1024 | bytes 8192 | tf_op jit(solution)/shard_map/psum | solution.py:118
  71.2 0.6 dynamic_slice.12
  71.8 0.0 collective-permute-done.1
  71.8 1.0 bitcast_add_fusion
  72.8 35.0 %all_to_all.15 = f32[16,8,768]{2,1,0:T(8,128)S(1)} all-to-all(f32[16,8,768]{2,1,0:T(8,128)S(1)} %bitcast.26), channel_id=1, replica_groups=mesh['wz'=16,'wy'=2,'oq'=8,'oc'=2] {'wz'}, dimensions={0} | all-to-all | bytes 786432 | tf_op jit(solution)/shard_map/all_to_all | solution.py:76
  107.8 23.4 %all_to_all.16 = bf16[16,8,768]{2,1,0:T(8,128)(2,1)S(1)} all-to-all(bf16[16,8,768]{2,1,0:T(8,128)(2,1)S(1)} %broadcast_in_dim.8), channel_id=1, replica_groups=mesh['wz'=16,'wy'=2,'oq'=8,'oc'=2] {'wz'}, dimensions={0} | all-to-all | bytes 393216 | tf_op jit(solution)/shard_map/all_to_all | solution.py:70
  131.2 3.1 %collective-permute-start.2 = (bf16[128,768]{1,0:T(8,128)(2,1)S(1)}, bf16[128,768]{1,0:T(8,128)(2,1)S(1)}, u32[]{:S(2)}, u32[]{:S(2)}) collective-permute-start(bf16[128,768]{1,0:T(8,128)(2,1)S(1)} %bitcast.28), channel_id=1, source_target_pairs={{0,16},{16,0},{1,17},{17,1},{2,18},{18,2},{3,19},{19,3},{4,20},{20... | collective-permute-start | bytes 589832 | tf_op jit(solution)/shard_map/ppermute | solution.py:62
  134.4 4.4 %collective-permute-done.2 = bf16[128,768]{1,0:T(8,128)(2,1)S(1)} collective-permute-done((bf16[128,768]{1,0:T(8,128)(2,1)S(1)}, bf16[128,768]{1,0:T(8,128)(2,1)S(1)}, u32[]{:S(2)}, u32[]{:S(2)}) %collective-permute-start.2) | collective-permute-done | bytes 196640 | tf_op jit(solution)/shard_map/ppermute | solution.py:62
  138.8 1.0 bitcast_convert_fusion
  (3 shorter events, 0.1 us)
Async XLA Ops:
  0.6 11.0 %copy-start = (bf16[4096,256]{1,0:T(8,128)(2,1)S(1)}, bf16[4096,256]{1,0:T(8,128)(2,1)}, u32[]{:S(2)}) copy-start(bf16[4096,256]{1,0:T(8,128)(2,1)} %param.11) | copy-start | bytes 6291460
  2.5 18.4 %all-to-all-start = ((bf16[8,48,768]{2,1,0:T(8,128)(2,1)}), bf16[8,48,768]{2,1,0:T(8,128)(2,1)S(1)}, u32[]{:S(2)}, u32[]{:S(2)}) async-start(bf16[8,48,768]{2,1,0:T(8,128)(2,1)} %broadcast_in_dim.7), calls=%async_computation | async-start | bytes 1179648 | tf_op jit(solution)/shard_map/all_to_all | solution.py:70
  14.1 12.3 %copy-start.3 = (s32[1024]{0:T(1024)S(1)}, s32[1024]{0:T(1024)}, u32[]{:S(2)}) copy-start(s32[1024]{0:T(1024)} %param.9) | copy-start | bytes 12292
  21.0 4.0 %collective-permute-start = (bf16[8,48,768]{2,1,0:T(8,128)(2,1)S(1)}, bf16[8,48,768]{2,1,0:T(8,128)(2,1)}, u32[]{:S(2)}, u32[]{:S(2)}) collective-permute-start(bf16[8,48,768]{2,1,0:T(8,128)(2,1)S(1)} %all-to-all-done), channel_id=1, source_target_pairs={{0,1},{1,0},{2,3},{3,2},{4,5},{5,4},{6,7},{7,6},{8,9},{9,8},{10,11... | collective-permute-start | bytes 1769480 | tf_op jit(solution)/shard_map/ppermute | solution.py:96
  26.4 1.6 %copy-start.2 = (f32[1024]{0:T(1024)S(1)}, f32[1024]{0:T(1024)}, u32[]{:S(2)}) copy-start(f32[1024]{0:T(1024)} %param.10) | copy-start | bytes 12292
  27.9 1.7 %copy-start.1 = (f32[1024,768]{1,0:T(8,128)}, f32[1024,768]{1,0:T(8,128)S(1)}, u32[]{:S(2)}) copy-start(f32[1024,768]{1,0:T(8,128)S(1)} %fusion) | copy-start | bytes 9437188
  30.4 41.4 %collective-permute-start.1 = (f32[128,768]{1,0:T(8,128)}, f32[128,768]{1,0:T(8,128)}, u32[]{:S(2)}, u32[]{:S(2)}) collective-permute-start(f32[128,768]{1,0:T(8,128)} %dynamic-slice_bitcast_fusion), channel_id=1, source_target_pairs={{0,16},{16,0},{1,17},{17,1},{2,18},{18,2},{3,19},{19,3},{4,20},{20... | collective-permute-start | bytes 1179656 | tf_op jit(solution)/shard_map/ppermute | solution.py:58
  131.2 7.6 %collective-permute-start.2 = (bf16[128,768]{1,0:T(8,128)(2,1)S(1)}, bf16[128,768]{1,0:T(8,128)(2,1)S(1)}, u32[]{:S(2)}, u32[]{:S(2)}) collective-permute-start(bf16[128,768]{1,0:T(8,128)(2,1)S(1)} %bitcast.28), channel_id=1, source_target_pairs={{0,16},{16,0},{1,17},{17,1},{2,18},{18,2},{3,19},{19,3},{4,20},{20... | collective-permute-start | bytes 589832 | tf_op jit(solution)/shard_map/ppermute | solution.py:62

commit v13 on v9

--- a/solution.py
+++ b/solution.py
@@ -94,7 +94,9 @@
     orbital_values, own_core = lax.optimization_barrier((orbital_values, own_core))
     core = lax.axis_index("oc")
     other_core = lax.ppermute(own_core, "oc", [(0, 1), (1, 0)])
-    pair = jnp.where(core == 0, jnp.stack([own_core, other_core], 1), jnp.stack([other_core, own_core], 1))
+    pair = jnp.zeros((own_core.shape[0], 2) + own_core.shape[1:], own_core.dtype)
+    pair = lax.dynamic_update_index_in_dim(pair, own_core, core, 1)
+    pair = lax.dynamic_update_index_in_dim(pair, other_core, 1 - core, 1)
     inverse_full = pair.reshape(-1, electrons)
     pick = (electron[:, None] == jnp.arange(electrons, dtype=jnp.int32)[None, :]).astype(
         jnp.bfloat16

time: 116 us -> 116 us (level)
  other arithmetic: 6.16 us -> 4.77 us
  local copies, waits for them, and re-layouts: 3.39 us -> 4.62 us
    select_n x1 -> x0, other arithmetic: 1.38 us -> none  [body(): jnp.where(core == 0, jnp.stack([own_core, other_core], 1), jnp.stack([oth...]
where the time goes in v13:
time: 116 us; the launch traced here: 115 us
  blocking collectives  60.8 us (52%)
  starting transfers between devices  19.7 us (17%)
  waiting for transfers between devices  19.3 us (17%)
  matrix products  5.46 us (5%)
  other arithmetic  4.77 us (4%)
  local copies, waits for them, and re-layouts  4.62 us (4%)
    all_to_all x1, blocking collectives, reduce_scatter_by_all_to_all(): return jnp.sum(lax.all_to_all(parts, axis, 0, 0, tiled=True), axis=0)  37.1 us
    all_to_all x1, blocking collectives, gather_by_all_to_all(): return lax.all_to_all(copies, axis, 0, 0, tiled=True)  23.7 us
    all_to_all x1, starting transfers between devices, gather_by_all_to_all(): return lax.all_to_all(copies, axis, 0, 0, tiled=True)  7.46 us
    all_to_all x1, waiting for transfers between devices, reduce_scatter_by_all_to_all(): return jnp.sum(lax.all_to_all(parts, axis, 0, 0, tiled=True), axis=0)  6.07 us
    ppermute x1, waiting for transfers between devices, all_reduce_walker(): other = lax.ppermute(half, 'wy', [(0, 1), (1, 0)])  5.64 us
    all_to_all x1, waiting for transfers between devices, gather_by_all_to_all(): return lax.all_to_all(copies, axis, 0, 0, tiled=True)  5.59 us
    all_to_all x1, starting transfers between devices, reduce_scatter_by_all_to_all(): return jnp.sum(lax.all_to_all(parts, axis, 0, 0, tiled=True), axis=0)  5.41 us
    ppermute x1, starting transfers between devices, all_reduce_walker(): half = keep + lax.ppermute(_pick(halves, 1 - me), 'wy', [(0, 1), (1, 0)])  2.58 us
  transfers between devices with their start and end apart: 5, of which 4 were waited for; matrix products, arithmetic and copies ran while one was open for 5% of the time, Pallas kernels for 0%

profile of v13, /device:TPU:34, one launch (start us, length us, event | category | flops | bytes accessed | tf_op | source)
XLA Modules:
  0.0 115.4 jit_solution(15371275101367406218)
XLA Ops:
  0.6 0.0 copy-start
  0.6 1.9 %broadcast_in_dim.16 = bf16[8,48,768]{2,1,0:T(8,128)(2,1)} broadcast(bf16[48,768]{1,0:T(8,128)(2,1)} %bitcast.35), dimensions={1,2} | broadcast | bytes 663552 | tf_op jit(solution)/shard_map/broadcast_in_dim | solution.py:69
  2.5 7.5 %all-to-all-start = ((bf16[8,48,768]{2,1,0:T(8,128)(2,1)}), bf16[8,48,768]{2,1,0:T(8,128)(2,1)S(1)}, u32[]{:S(2)}, u32[]{:S(2)}) async-start(bf16[8,48,768]{2,1,0:T(8,128)(2,1)} %broadcast_in_dim.16), calls=%async_computation | async-start | bytes 1179648 | tf_op jit(solution)/shard_map/all_to_all | solution.py:70
  10.0 0.7 fusion.12
  10.7 1.5 %broadcast_multiply_fusion = bf16[1024,64,64]{0,2,1:T(8,128)(2,1)S(1)} fusion(bf16[1024,64]{0,1:T(8,128)(2,1)} %param.8, bf16[1024,64]{0,1:T(8,128)(2,1)S(1)} %fusion.12), kind=kLoop, calls=%fused_computation | loop fusion | flops 4194304 | bytes 8650752 | tf_op jit(solution)/shard_map/mul | solution.py:87
  12.2 0.0 copy-done
  12.2 2.5 %convolution_convert_fusion = bf16[1024,256]{1,0:T(8,128)(2,1)S(1)} fusion(bf16[1024,4096]{0,1:T(8,128)(2,1)S(1)} %bitcast.27, bf16[4096,256]{1,0:T(8,128)(2,1)S(1)} %copy-done), kind=kOutput, calls=%fused_computation.10 | convolution fusion | flops 2147745792 | bytes 11010048 | tf_op jit(solution)/shard_map/dot_general | solution.py:90
  14.6 0.0 copy-start.3
  14.6 5.6 %all-to-all-done = bf16[8,48,768]{2,1,0:T(8,128)(2,1)S(1)} async-done(((bf16[8,48,768]{2,1,0:T(8,128)(2,1)}), bf16[8,48,768]{2,1,0:T(8,128)(2,1)S(1)}, u32[]{:S(2)}, u32[]{:S(2)}) %all-to-all-start) | async-done | bytes 589856 | tf_op jit(solution)/shard_map/all_to_all | solution.py:70
  20.2 1.9 %collective-permute-start = (bf16[8,48,768]{2,1,0:T(8,128)(2,1)S(1)}, bf16[8,48,768]{2,1,0:T(8,128)(2,1)}, u32[]{:S(2)}, u32[]{:S(2)}) collective-permute-start(bf16[8,48,768]{2,1,0:T(8,128)(2,1)S(1)} %all-to-all-done), channel_id=1, source_target_pairs={{0,1},{1,0},{2,3},{3,2},{4,5},{5,4},{6,7},{7,6},{8,9},{9,8},{10,11... | collective-permute-start | bytes 1769480 | tf_op jit(solution)/shard_map/ppermute | solution.py:96
  22.2 0.1 broadcast_in_dim.32
  22.3 2.0 %collective-permute-done = bf16[8,48,768]{2,1,0:T(8,128)(2,1)} collective-permute-done((bf16[8,48,768]{2,1,0:T(8,128)(2,1)S(1)}, bf16[8,48,768]{2,1,0:T(8,128)(2,1)}, u32[]{:S(2)}, u32[]{:S(2)}) %collective-permute-start) | collective-permute-done | bytes 589856 | tf_op jit(solution)/shard_map/ppermute | solution.py:96
  24.3 1.1 bitcast_dynamic-update-slice_fusion.1
  25.4 0.0 copy-start.2
  25.4 1.5 %fusion = f32[1024,768]{1,0:T(8,128)S(1)} fusion(bf16[768,768]{1,0:T(8,128)(2,1)S(1)} %bitcast.31, s32[1024]{0:T(1024)S(1)} %copy-done.3), kind=kOutput, calls=%fused_computation.3 | convolution fusion | flops 1208745984 | bytes 4329472 | tf_op jit(solution)/shard_map/dot_general | solution.py:104
  26.9 0.0 copy-done.2
  26.9 0.0 copy-start.1
  27.0 0.8 fusion.1
  27.7 0.8 dynamic-slice_bitcast_fusion
  28.5 2.6 %collective-permute-start.1 = (f32[128,768]{1,0:T(8,128)}, f32[128,768]{1,0:T(8,128)}, u32[]{:S(2)}, u32[]{:S(2)}) collective-permute-start(f32[128,768]{1,0:T(8,128)} %dynamic-slice_bitcast_fusion), channel_id=1, source_target_pairs={{0,16},{16,0},{1,17},{17,1},{2,18},{18,2},{3,19},{19,3},{4,20},{20... | collective-permute-start | bytes 1179656 | tf_op jit(solution)/shard_map/ppermute | solution.py:58
  31.1 0.7 fusion.9
  31.8 0.7 all_to_all.16
  32.5 5.4 %all-to-all-start.1 = ((f32[16,1,64]{2,1,0:T(1,128)}), f32[16,1,64]{2,1,0:T(1,128)S(1)}, u32[]{:S(2)}, u32[]{:S(2)}) async-start(f32[16,1,64]{2,1,0:T(1,128)} %all_to_all.16), calls=%async_computation.1 | async-start | bytes 16384 | tf_op jit(solution)/shard_map/all_to_all | solution.py:76
  37.9 6.1 %all-to-all-done.1 = f32[16,1,64]{2,1,0:T(1,128)S(1)} async-done(((f32[16,1,64]{2,1,0:T(1,128)}), f32[16,1,64]{2,1,0:T(1,128)S(1)}, u32[]{:S(2)}, u32[]{:S(2)}) %all-to-all-start.1) | async-done | bytes 4128 | tf_op jit(solution)/shard_map/all_to_all | solution.py:76
  44.0 0.5 reduce_sum.28
  44.5 0.0 collective-permute-done.1
  44.5 1.0 bitcast_add_fusion
  45.5 37.1 %all_to_all.24 = f32[16,8,768]{2,1,0:T(8,128)S(1)} all-to-all(f32[16,8,768]{2,1,0:T(8,128)S(1)} %bitcast.30), channel_id=1, replica_groups=mesh['wz'=16,'wy'=2,'oq'=8,'oc'=2] {'wz'}, dimensions={0} | all-to-all | bytes 786432 | tf_op jit(solution)/shard_map/all_to_all | solution.py:76
  82.7 23.7 %all_to_all.25 = bf16[16,8,768]{2,1,0:T(8,128)(2,1)S(1)} all-to-all(bf16[16,8,768]{2,1,0:T(8,128)(2,1)S(1)} %broadcast_in_dim.35), channel_id=1, replica_groups=mesh['wz'=16,'wy'=2,'oq'=8,'oc'=2] {'wz'}, dimensions={0} | all-to-all | bytes 393216 | tf_op jit(solution)/shard_map/all_to_all | solution.py:70
  106.4 2.4 %collective-permute-start.2 = (bf16[128,768]{1,0:T(8,128)(2,1)S(1)}, bf16[128,768]{1,0:T(8,128)(2,1)S(1)}, u32[]{:S(2)}, u32[]{:S(2)}) collective-permute-start(bf16[128,768]{1,0:T(8,128)(2,1)S(1)} %bitcast.32), channel_id=1, source_target_pairs={{0,16},{16,0},{1,17},{17,1},{2,18},{18,2},{3,19},{19,3},{4,20},{20... | collective-permute-start | bytes 589832 | tf_op jit(solution)/shard_map/ppermute | solution.py:62
  108.8 5.6 %collective-permute-done.2 = bf16[128,768]{1,0:T(8,128)(2,1)S(1)} collective-permute-done((bf16[128,768]{1,0:T(8,128)(2,1)S(1)}, bf16[128,768]{1,0:T(8,128)(2,1)S(1)}, u32[]{:S(2)}, u32[]{:S(2)}) %collective-permute-start.2) | collective-permute-done | bytes 196640 | tf_op jit(solution)/shard_map/ppermute | solution.py:62
  114.5 1.0 bitcast_convert_fusion
  (6 shorter events, 0.1 us)
Async XLA Ops:
  0.6 11.5 %copy-start = (bf16[4096,256]{1,0:T(8,128)(2,1)S(1)}, bf16[4096,256]{1,0:T(8,128)(2,1)}, u32[]{:S(2)}) copy-start(bf16[4096,256]{1,0:T(8,128)(2,1)} %param.11) | copy-start | bytes 6291460
  2.5 17.7 %all-to-all-start = ((bf16[8,48,768]{2,1,0:T(8,128)(2,1)}), bf16[8,48,768]{2,1,0:T(8,128)(2,1)S(1)}, u32[]{:S(2)}, u32[]{:S(2)}) async-start(bf16[8,48,768]{2,1,0:T(8,128)(2,1)} %broadcast_in_dim.16), calls=%async_computation | async-start | bytes 1179648 | tf_op jit(solution)/shard_map/all_to_all | solution.py:70
  14.6 10.7 %copy-start.3 = (s32[1024]{0:T(1024)S(1)}, s32[1024]{0:T(1024)}, u32[]{:S(2)}) copy-start(s32[1024]{0:T(1024)} %param.9) | copy-start | bytes 12292
  20.2 4.0 %collective-permute-start = (bf16[8,48,768]{2,1,0:T(8,128)(2,1)S(1)}, bf16[8,48,768]{2,1,0:T(8,128)(2,1)}, u32[]{:S(2)}, u32[]{:S(2)}) collective-permute-start(bf16[8,48,768]{2,1,0:T(8,128)(2,1)S(1)} %all-to-all-done), channel_id=1, source_target_pairs={{0,1},{1,0},{2,3},{3,2},{4,5},{5,4},{6,7},{7,6},{8,9},{9,8},{10,11... | collective-permute-start | bytes 1769480 | tf_op jit(solution)/shard_map/ppermute | solution.py:96
  25.4 1.6 %copy-start.2 = (f32[1024]{0:T(1024)S(1)}, f32[1024]{0:T(1024)}, u32[]{:S(2)}) copy-start(f32[1024]{0:T(1024)} %param.10) | copy-start | bytes 12292
  26.9 4.1 %copy-start.1 = (bf16[256,768]{1,0:T(8,128)(2,1)S(1)}, bf16[256,768]{1,0:T(8,128)(2,1)}, u32[]{:S(2)}) copy-start(bf16[256,768]{1,0:T(8,128)(2,1)} %param.12) | copy-start | bytes 1179652
  28.5 16.0 %collective-permute-start.1 = (f32[128,768]{1,0:T(8,128)}, f32[128,768]{1,0:T(8,128)}, u32[]{:S(2)}, u32[]{:S(2)}) collective-permute-start(f32[128,768]{1,0:T(8,128)} %dynamic-slice_bitcast_fusion), channel_id=1, source_target_pairs={{0,16},{16,0},{1,17},{17,1},{2,18},{18,2},{3,19},{19,3},{4,20},{20... | collective-permute-start | bytes 1179656 | tf_op jit(solution)/shard_map/ppermute | solution.py:58
  32.5 11.5 %all-to-all-start.1 = ((f32[16,1,64]{2,1,0:T(1,128)}), f32[16,1,64]{2,1,0:T(1,128)S(1)}, u32[]{:S(2)}, u32[]{:S(2)}) async-start(f32[16,1,64]{2,1,0:T(1,128)} %all_to_all.16), calls=%async_computation.1 | async-start | bytes 16384 | tf_op jit(solution)/shard_map/all_to_all | solution.py:76
  106.4 8.0 %collective-permute-start.2 = (bf16[128,768]{1,0:T(8,128)(2,1)S(1)}, bf16[128,768]{1,0:T(8,128)(2,1)S(1)}, u32[]{:S(2)}, u32[]{:S(2)}) collective-permute-start(bf16[128,768]{1,0:T(8,128)(2,1)S(1)} %bitcast.32), channel_id=1, source_target_pairs={{0,16},{16,0},{1,17},{17,1},{2,18},{18,2},{3,19},{19,3},{4,20},{20... | collective-permute-start | bytes 589832 | tf_op jit(solution)/shard_map/ppermute | solution.py:62

commit v14 on v13

--- a/solution.py
+++ b/solution.py
@@ -60,8 +60,10 @@
     reduced = reduce_scatter_by_all_to_all(half, "wz").astype(jnp.bfloat16)
     half = gather_by_all_to_all(reduced, "wz").reshape(half.shape)
     other = lax.ppermute(half, "wy", [(0, 1), (1, 0)])
-    full = jnp.where(me == 0, jnp.stack([half, other]), jnp.stack([other, half]))
-    return full.reshape(x.shape).astype(x.dtype), rider
+    full = jnp.zeros((2,) + half.shape, x.dtype)
+    full = lax.dynamic_update_index_in_dim(full, half.astype(x.dtype), me, 0)
+    full = lax.dynamic_update_index_in_dim(full, other.astype(x.dtype), 1 - me, 0)
+    return full.reshape(x.shape), rider
 
 
 def gather_by_all_to_all(x, axis):

time: 116 us -> 117 us (level)
  the two profiles are of different devices: /device:TPU:34 before, /device:TPU:32 now
where the time goes in v14:
time: 117 us; the launch traced here: 116 us
  blocking collectives  60.7 us (52%)
  waiting for transfers between devices  21.8 us (19%)
  starting transfers between devices  18.1 us (15%)
  local copies, waits for them, and re-layouts  5.54 us (5%)
  matrix products  5.45 us (5%)
  other arithmetic  3.83 us (3%)
    all_to_all x1, blocking collectives, reduce_scatter_by_all_to_all(): return jnp.sum(lax.all_to_all(parts, axis, 0, 0, tiled=True), axis=0)  37 us
    all_to_all x1, blocking collectives, gather_by_all_to_all(): return lax.all_to_all(copies, axis, 0, 0, tiled=True)  23.7 us
    all_to_all x1, waiting for transfers between devices, reduce_scatter_by_all_to_all(): return jnp.sum(lax.all_to_all(parts, axis, 0, 0, tiled=True), axis=0)  7.44 us
    all_to_all x1, starting transfers between devices, gather_by_all_to_all(): return lax.all_to_all(copies, axis, 0, 0, tiled=True)  6.93 us
    all_to_all x1, waiting for transfers between devices, gather_by_all_to_all(): return lax.all_to_all(copies, axis, 0, 0, tiled=True)  6.85 us
    ppermute x1, waiting for transfers between devices, all_reduce_walker(): other = lax.ppermute(half, 'wy', [(0, 1), (1, 0)])  5.52 us
    all_to_all x1, starting transfers between devices, reduce_scatter_by_all_to_all(): return jnp.sum(lax.all_to_all(parts, axis, 0, 0, tiled=True), axis=0)  4.24 us
    ppermute x1, starting transfers between devices, all_reduce_walker(): half = keep + lax.ppermute(_pick(halves, 1 - me), 'wy', [(0, 1), (1, 0)])  2.58 us
  transfers between devices with their start and end apart: 5, of which 4 were waited for; matrix products, arithmetic and copies ran while one was open for 5% of the time, Pallas kernels for 0%

profile of v14, /device:TPU:32, one launch (start us, length us, event | category | flops | bytes accessed | tf_op | source)
XLA Modules:
  0.0 116.2 jit_solution(6351316583681266550)
XLA Ops:
  0.6 0.0 copy-start
  0.6 1.9 %broadcast_in_dim.42 = bf16[8,48,768]{2,1,0:T(8,128)(2,1)} broadcast(bf16[48,768]{1,0:T(8,128)(2,1)} %bitcast.36), dimensions={1,2} | broadcast | bytes 663552 | tf_op jit(solution)/shard_map/broadcast_in_dim | solution.py:71
  2.5 6.9 %all-to-all-start = ((bf16[8,48,768]{2,1,0:T(8,128)(2,1)}), bf16[8,48,768]{2,1,0:T(8,128)(2,1)S(1)}, u32[]{:S(2)}, u32[]{:S(2)}) async-start(bf16[8,48,768]{2,1,0:T(8,128)(2,1)} %broadcast_in_dim.42), calls=%async_computation | async-start | bytes 1179648 | tf_op jit(solution)/shard_map/all_to_all | solution.py:72
  9.5 0.7 fusion.12
  10.2 1.5 %broadcast_multiply_fusion = bf16[1024,64,64]{0,2,1:T(8,128)(2,1)S(1)} fusion(bf16[1024,64]{0,1:T(8,128)(2,1)} %param.8, bf16[1024,64]{0,1:T(8,128)(2,1)S(1)} %fusion.12), kind=kLoop, calls=%fused_computation | loop fusion | flops 4194304 | bytes 8650752 | tf_op jit(solution)/shard_map/mul | solution.py:89
  11.6 2.4 %convolution_convert_fusion = bf16[1024,256]{1,0:T(8,128)(2,1)S(1)} fusion(bf16[1024,4096]{0,1:T(8,128)(2,1)S(1)} %bitcast.29, bf16[4096,256]{1,0:T(8,128)(2,1)S(1)} %copy-done), kind=kOutput, calls=%fused_computation.10 | convolution fusion | flops 2147745792 | bytes 11010048 | tf_op jit(solution)/shard_map/dot_general | solution.py:92
  14.1 0.0 copy-start.4
  14.1 6.8 %all-to-all-done = bf16[8,48,768]{2,1,0:T(8,128)(2,1)S(1)} async-done(((bf16[8,48,768]{2,1,0:T(8,128)(2,1)}), bf16[8,48,768]{2,1,0:T(8,128)(2,1)S(1)}, u32[]{:S(2)}, u32[]{:S(2)}) %all-to-all-start) | async-done | bytes 589856 | tf_op jit(solution)/shard_map/all_to_all | solution.py:72
  21.0 1.9 %collective-permute-start = (bf16[8,48,768]{2,1,0:T(8,128)(2,1)S(1)}, bf16[8,48,768]{2,1,0:T(8,128)(2,1)}, u32[]{:S(2)}, u32[]{:S(2)}) collective-permute-start(bf16[8,48,768]{2,1,0:T(8,128)(2,1)S(1)} %all-to-all-done), channel_id=1, source_target_pairs={{0,1},{1,0},{2,3},{3,2},{4,5},{5,4},{6,7},{7,6},{8,9},{9,8},{10,11... | collective-permute-start | bytes 1769480 | tf_op jit(solution)/shard_map/ppermute | solution.py:98
  22.9 0.1 broadcast_in_dim.43
  23.0 2.0 %collective-permute-done = bf16[8,48,768]{2,1,0:T(8,128)(2,1)} collective-permute-done((bf16[8,48,768]{2,1,0:T(8,128)(2,1)S(1)}, bf16[8,48,768]{2,1,0:T(8,128)(2,1)}, u32[]{:S(2)}, u32[]{:S(2)}) %collective-permute-start) | collective-permute-done | bytes 589856 | tf_op jit(solution)/shard_map/ppermute | solution.py:98
  25.0 1.1 bitcast_dynamic-update-slice_fusion.1
  26.1 0.0 copy-start.3
  26.1 1.5 %fusion = f32[1024,768]{1,0:T(8,128)S(1)} fusion(bf16[768,768]{1,0:T(8,128)(2,1)S(1)} %bitcast.33, s32[1024]{0:T(1024)S(1)} %copy-done.4), kind=kOutput, calls=%fused_computation.3 | convolution fusion | flops 1208745984 | bytes 4329472 | tf_op jit(solution)/shard_map/dot_general | solution.py:106
  27.7 0.0 copy-start.2
  27.7 0.8 fusion.1
  28.4 0.8 dynamic-slice_bitcast_fusion
  29.2 2.6 %collective-permute-start.1 = (f32[128,768]{1,0:T(8,128)}, f32[128,768]{1,0:T(8,128)}, u32[]{:S(2)}, u32[]{:S(2)}) collective-permute-start(f32[128,768]{1,0:T(8,128)} %dynamic-slice_bitcast_fusion), channel_id=1, source_target_pairs={{0,16},{16,0},{1,17},{17,1},{2,18},{18,2},{3,19},{19,3},{4,20},{20... | collective-permute-start | bytes 1179656 | tf_op jit(solution)/shard_map/ppermute | solution.py:58
  31.8 0.7 fusion.9
  32.5 0.7 all_to_all.16
  33.2 4.2 %all-to-all-start.1 = ((f32[16,1,64]{2,1,0:T(1,128)}), f32[16,1,64]{2,1,0:T(1,128)S(1)}, u32[]{:S(2)}, u32[]{:S(2)}) async-start(f32[16,1,64]{2,1,0:T(1,128)} %all_to_all.16), calls=%async_computation.1 | async-start | bytes 16384 | tf_op jit(solution)/shard_map/all_to_all | solution.py:78
  37.4 7.4 %all-to-all-done.1 = f32[16,1,64]{2,1,0:T(1,128)S(1)} async-done(((f32[16,1,64]{2,1,0:T(1,128)}), f32[16,1,64]{2,1,0:T(1,128)S(1)}, u32[]{:S(2)}, u32[]{:S(2)}) %all-to-all-start.1) | async-done | bytes 4128 | tf_op jit(solution)/shard_map/all_to_all | solution.py:78
  44.9 0.5 reduce_sum.28
  45.4 0.0 collective-permute-done.1
  45.4 1.0 bitcast_add_fusion
  46.5 37.0 %all_to_all.24 = f32[16,8,768]{2,1,0:T(8,128)S(1)} all-to-all(f32[16,8,768]{2,1,0:T(8,128)S(1)} %bitcast.32), channel_id=1, replica_groups=mesh['wz'=16,'wy'=2,'oq'=8,'oc'=2] {'wz'}, dimensions={0} | all-to-all | bytes 786432 | tf_op jit(solution)/shard_map/all_to_all | solution.py:78
  83.6 23.7 %all_to_all.25 = bf16[16,8,768]{2,1,0:T(8,128)(2,1)S(1)} all-to-all(bf16[16,8,768]{2,1,0:T(8,128)(2,1)S(1)} %broadcast_in_dim.47), channel_id=1, replica_groups=mesh['wz'=16,'wy'=2,'oq'=8,'oc'=2] {'wz'}, dimensions={0} | all-to-all | bytes 393216 | tf_op jit(solution)/shard_map/all_to_all | solution.py:72
  107.2 2.4 %collective-permute-start.2 = (bf16[128,768]{1,0:T(8,128)(2,1)S(1)}, bf16[128,768]{1,0:T(8,128)(2,1)S(1)}, u32[]{:S(2)}, u32[]{:S(2)}) collective-permute-start(bf16[128,768]{1,0:T(8,128)(2,1)S(1)} %bitcast.35), channel_id=1, source_target_pairs={{0,16},{16,0},{1,17},{17,1},{2,18},{18,2},{3,19},{19,3},{4,20},{20... | collective-permute-start | bytes 589832 | tf_op jit(solution)/shard_map/ppermute | solution.py:62
  109.7 0.1 broadcast_in_dim.46
  109.8 5.5 %collective-permute-done.2 = bf16[128,768]{1,0:T(8,128)(2,1)S(1)} collective-permute-done((bf16[128,768]{1,0:T(8,128)(2,1)S(1)}, bf16[128,768]{1,0:T(8,128)(2,1)S(1)}, u32[]{:S(2)}, u32[]{:S(2)}) %collective-permute-start.2) | collective-permute-done | bytes 196640 | tf_op jit(solution)/shard_map/ppermute | solution.py:62
  115.3 0.0 copy-start.1
  115.3 0.9 copy-done.1
  (9 shorter events, 0.2 us)
Async XLA Ops:
  0.6 11.0 %copy-start = (bf16[4096,256]{1,0:T(8,128)(2,1)S(1)}, bf16[4096,256]{1,0:T(8,128)(2,1)}, u32[]{:S(2)}) copy-start(bf16[4096,256]{1,0:T(8,128)(2,1)} %param.11) | copy-start | bytes 6291460
  2.5 18.4 %all-to-all-start = ((bf16[8,48,768]{2,1,0:T(8,128)(2,1)}), bf16[8,48,768]{2,1,0:T(8,128)(2,1)S(1)}, u32[]{:S(2)}, u32[]{:S(2)}) async-start(bf16[8,48,768]{2,1,0:T(8,128)(2,1)} %broadcast_in_dim.42), calls=%async_computation | async-start | bytes 1179648 | tf_op jit(solution)/shard_map/all_to_all | solution.py:72
  14.1 12.0 %copy-start.4 = (s32[1024]{0:T(1024)S(1)}, s32[1024]{0:T(1024)}, u32[]{:S(2)}) copy-start(s32[1024]{0:T(1024)} %param.9) | copy-start | bytes 12292
  21.0 4.0 %collective-permute-start = (bf16[8,48,768]{2,1,0:T(8,128)(2,1)S(1)}, bf16[8,48,768]{2,1,0:T(8,128)(2,1)}, u32[]{:S(2)}, u32[]{:S(2)}) collective-permute-start(bf16[8,48,768]{2,1,0:T(8,128)(2,1)S(1)} %all-to-all-done), channel_id=1, source_target_pairs={{0,1},{1,0},{2,3},{3,2},{4,5},{5,4},{6,7},{7,6},{8,9},{9,8},{10,11... | collective-permute-start | bytes 1769480 | tf_op jit(solution)/shard_map/ppermute | solution.py:98
  26.1 1.6 %copy-start.3 = (f32[1024]{0:T(1024)S(1)}, f32[1024]{0:T(1024)}, u32[]{:S(2)}) copy-start(f32[1024]{0:T(1024)} %param.10) | copy-start | bytes 12292
  27.7 4.1 %copy-start.2 = (bf16[256,768]{1,0:T(8,128)(2,1)S(1)}, bf16[256,768]{1,0:T(8,128)(2,1)}, u32[]{:S(2)}) copy-start(bf16[256,768]{1,0:T(8,128)(2,1)} %param.12) | copy-start | bytes 1179652
  29.2 16.2 %collective-permute-start.1 = (f32[128,768]{1,0:T(8,128)}, f32[128,768]{1,0:T(8,128)}, u32[]{:S(2)}, u32[]{:S(2)}) collective-permute-start(f32[128,768]{1,0:T(8,128)} %dynamic-slice_bitcast_fusion), channel_id=1, source_target_pairs={{0,16},{16,0},{1,17},{17,1},{2,18},{18,2},{3,19},{19,3},{4,20},{20... | collective-permute-start | bytes 1179656 | tf_op jit(solution)/shard_map/ppermute | solution.py:58
  33.2 11.7 %all-to-all-start.1 = ((f32[16,1,64]{2,1,0:T(1,128)}), f32[16,1,64]{2,1,0:T(1,128)S(1)}, u32[]{:S(2)}, u32[]{:S(2)}) async-start(f32[16,1,64]{2,1,0:T(1,128)} %all_to_all.16), calls=%async_computation.1 | async-start | bytes 16384 | tf_op jit(solution)/shard_map/all_to_all | solution.py:78
  107.2 8.0 %collective-permute-start.2 = (bf16[128,768]{1,0:T(8,128)(2,1)S(1)}, bf16[128,768]{1,0:T(8,128)(2,1)S(1)}, u32[]{:S(2)}, u32[]{:S(2)}) collective-permute-start(bf16[128,768]{1,0:T(8,128)(2,1)S(1)} %bitcast.35), channel_id=1, source_target_pairs={{0,16},{16,0},{1,17},{17,1},{2,18},{18,2},{3,19},{19,3},{4,20},{20... | collective-permute-start | bytes 589832 | tf_op jit(solution)/shard_map/ppermute | solution.py:62
  115.3 0.9 copy-start.1

commit v15 on v13

--- a/solution.py
+++ b/solution.py
@@ -51,17 +51,16 @@
     return all_gather_bits(reduced, axis, order[::-1]).reshape(tail)
 
 
-def all_reduce_walker(x, rider):
+def all_reduce_walker(half_of, rider, shape):
     me = lax.axis_index("wy")
-    halves = x.reshape((2, x.shape[0] // 2) + x.shape[1:])
-    keep = _pick(halves, me)
-    half = keep + lax.ppermute(_pick(halves, 1 - me), "wy", [(0, 1), (1, 0)])
+    sent = lax.ppermute(half_of(1 - me), "wy", [(0, 1), (1, 0)])
+    half = half_of(me) + sent
     half, rider = lax.optimization_barrier((half, rider))
     reduced = reduce_scatter_by_all_to_all(half, "wz").astype(jnp.bfloat16)
     half = gather_by_all_to_all(reduced, "wz").reshape(half.shape)
     other = lax.ppermute(half, "wy", [(0, 1), (1, 0)])
     full = jnp.where(me == 0, jnp.stack([half, other]), jnp.stack([other, half]))
-    return full.reshape(x.shape).astype(x.dtype), rider
+    return full.reshape(shape).astype(jnp.float32), rider
 
 
 def gather_by_all_to_all(x, axis):
@@ -105,9 +104,14 @@
         pick, inverse_full, (((1,), (1,)), ((), ())), preferred_element_type=jnp.float32
     )
     adjoint = (columns * strength[:, None]).astype(jnp.bfloat16)
-    local_gradient = lax.dot_general(
-        orbital_values, adjoint, (((0,), (0,)), ((), ())), preferred_element_type=jnp.float32
-    )
+    half_rows = orbital_values.shape[1] // 2
+
+    def gradient_half(which):
+        values_half = lax.dynamic_slice_in_dim(orbital_values, which * half_rows, half_rows, 1)
+        return lax.dot_general(
+            values_half, adjoint, (((0,), (0,)), ((), ())), preferred_element_type=jnp.float32
+        )
+
     rotated_columns = lax.dot_general(
         columns.astype(jnp.bfloat16),
         rotation,
@@ -116,7 +120,9 @@
     )
     partial_ratio = jnp.sum(orbital_values.astype(jnp.float32) * rotated_columns, axis=1)
     ratios = reduce_scatter_by_all_to_all(partial_ratio, ("oq", "oc"))
-    gradient, ratios = all_reduce_walker(local_gradient, ratios)
+    gradient, ratios = all_reduce_walker(
+        gradient_half, ratios, (orbital_values.shape[1], adjoint.shape[1])
+    )
     return (ratios, gradient)
 
 

time: 116 us -> 116 us (level)
  the two profiles are of different devices: /device:TPU:34 before, /device:TPU:32 now
where the time goes in v15:
time: 116 us
  blocking collectives  59.8 us (52%)
  waiting for transfers between devices  21.8 us (19%)
  starting transfers between devices  18.1 us (16%)
  matrix products  7.69 us (7%)
  local copies, waits for them, and re-layouts  3.85 us (3%)
  other arithmetic  3.73 us (3%)
    all_to_all x1, blocking collectives, reduce_scatter_by_all_to_all(): return jnp.sum(lax.all_to_all(parts, axis, 0, 0, tiled=True), axis=0)  36.8 us
    all_to_all x1, blocking collectives, gather_by_all_to_all(): return lax.all_to_all(copies, axis, 0, 0, tiled=True)  23 us
    all_to_all x1, waiting for transfers between devices, reduce_scatter_by_all_to_all(): return jnp.sum(lax.all_to_all(parts, axis, 0, 0, tiled=True), axis=0)  7.51 us
    all_to_all x1, starting transfers between devices, gather_by_all_to_all(): return lax.all_to_all(copies, axis, 0, 0, tiled=True)  6.93 us
    all_to_all x1, waiting for transfers between devices, gather_by_all_to_all(): return lax.all_to_all(copies, axis, 0, 0, tiled=True)  6.85 us
    ppermute x1, waiting for transfers between devices, all_reduce_walker(): other = lax.ppermute(half, 'wy', [(0, 1), (1, 0)])  5.48 us
    all_to_all x1, starting transfers between devices, reduce_scatter_by_all_to_all(): return jnp.sum(lax.all_to_all(parts, axis, 0, 0, tiled=True), axis=0)  4.23 us
    dot_general x2, matrix products, gradient_half(): lax.dot_general(values_half, adjoint, (((0,), (0,)), ((), ())), preferred...  2.98 us
  transfers between devices with their start and end apart: 5, of which 4 were waited for; matrix products, arithmetic and copies ran while one was open for 5% of the time, Pallas kernels for 0%

profile of v15, /device:TPU:32, one launch (start us, length us, event | category | flops | bytes accessed | tf_op | source)
XLA Modules:
  0.0 115.8 jit_solution(13419313825821175809)
XLA Ops:
  0.6 0.0 copy-start
  0.6 1.9 %broadcast_in_dim.16 = bf16[8,48,768]{2,1,0:T(8,128)(2,1)} broadcast(bf16[48,768]{1,0:T(8,128)(2,1)} %bitcast.27), dimensions={1,2} | broadcast | bytes 663552 | tf_op jit(solution)/shard_map/broadcast_in_dim | solution.py:68
  2.5 6.9 %all-to-all-start = ((bf16[8,48,768]{2,1,0:T(8,128)(2,1)}), bf16[8,48,768]{2,1,0:T(8,128)(2,1)S(1)}, u32[]{:S(2)}, u32[]{:S(2)}) async-start(bf16[8,48,768]{2,1,0:T(8,128)(2,1)} %broadcast_in_dim.16), calls=%async_computation | async-start | bytes 1179648 | tf_op jit(solution)/shard_map/all_to_all | solution.py:69
  9.5 0.7 fusion.13
  10.2 1.5 %broadcast_multiply_fusion = bf16[1024,64,64]{0,2,1:T(8,128)(2,1)S(1)} fusion(bf16[1024,64]{0,1:T(8,128)(2,1)} %param.8, bf16[1024,64]{0,1:T(8,128)(2,1)S(1)} %fusion.13), kind=kLoop, calls=%fused_computation | loop fusion | flops 4194304 | bytes 8650752 | tf_op jit(solution)/shard_map/mul | solution.py:86
  11.6 0.0 copy-done
  11.6 2.5 %convolution_convert_fusion = bf16[1024,256]{1,0:T(8,128)(2,1)S(1)} fusion(bf16[1024,4096]{0,1:T(8,128)(2,1)S(1)} %bitcast.21, bf16[4096,256]{1,0:T(8,128)(2,1)S(1)} %copy-done), kind=kOutput, calls=%fused_computation.8 | convolution fusion | flops 2147745792 | bytes 11010048 | tf_op jit(solution)/shard_map/dot_general | solution.py:89
  14.1 0.0 copy-start.4
  14.1 6.8 %all-to-all-done = bf16[8,48,768]{2,1,0:T(8,128)(2,1)S(1)} async-done(((bf16[8,48,768]{2,1,0:T(8,128)(2,1)}), bf16[8,48,768]{2,1,0:T(8,128)(2,1)S(1)}, u32[]{:S(2)}, u32[]{:S(2)}) %all-to-all-start) | async-done | bytes 589856 | tf_op jit(solution)/shard_map/all_to_all | solution.py:69
  21.0 1.9 %collective-permute-start = (bf16[8,48,768]{2,1,0:T(8,128)(2,1)S(1)}, bf16[8,48,768]{2,1,0:T(8,128)(2,1)}, u32[]{:S(2)}, u32[]{:S(2)}) collective-permute-start(bf16[8,48,768]{2,1,0:T(8,128)(2,1)S(1)} %all-to-all-done), channel_id=1, source_target_pairs={{0,1},{1,0},{2,3},{3,2},{4,5},{5,4},{6,7},{7,6},{8,9},{9,8},{10,11... | collective-permute-start | bytes 1769480 | tf_op jit(solution)/shard_map/ppermute | solution.py:95
  22.9 0.1 broadcast_in_dim.32
  23.0 2.0 %collective-permute-done = bf16[8,48,768]{2,1,0:T(8,128)(2,1)} collective-permute-done((bf16[8,48,768]{2,1,0:T(8,128)(2,1)S(1)}, bf16[8,48,768]{2,1,0:T(8,128)(2,1)}, u32[]{:S(2)}, u32[]{:S(2)}) %collective-permute-start) | collective-permute-done | bytes 589856 | tf_op jit(solution)/shard_map/ppermute | solution.py:95
  25.0 1.1 bitcast_dynamic-update-slice_fusion.1
  26.1 0.0 copy-done.4
  26.1 0.0 copy-start.3
  26.1 1.5 %fusion = f32[1024,768]{1,0:T(8,128)S(1)} fusion(bf16[768,768]{1,0:T(8,128)(2,1)S(1)} %bitcast.23, s32[1024]{0:T(1024)S(1)} %copy-done.4), kind=kOutput, calls=%fused_computation.3 | convolution fusion | flops 1208745984 | bytes 4329472 | tf_op jit(solution)/shard_map/dot_general | solution.py:103
  27.7 0.0 copy-done.3
  27.7 0.0 copy-start.2
  27.7 0.6 fusion.10
  28.3 2.6 %collective-permute-start.1 = (f32[128,768]{1,0:T(8,128)S(1)}, f32[128,768]{1,0:T(8,128)S(1)}, u32[]{:S(2)}, u32[]{:S(2)}) collective-permute-start(f32[128,768]{1,0:T(8,128)S(1)} %fusion.10), channel_id=1, source_target_pairs={{0,16},{16,0},{1,17},{17,1},{2,18},{18,2},{3,19},{19,3},{4,20},{20... | collective-permute-start | bytes 1179656 | tf_op jit(solution)/shard_map/ppermute | solution.py:56
  30.9 0.7 fusion.7
  31.6 0.7 all_to_all.16
  32.3 4.2 %all-to-all-start.1 = ((f32[16,1,64]{2,1,0:T(1,128)}), f32[16,1,64]{2,1,0:T(1,128)S(1)}, u32[]{:S(2)}, u32[]{:S(2)}) async-start(f32[16,1,64]{2,1,0:T(1,128)} %all_to_all.16), calls=%async_computation.1 | async-start | bytes 16384 | tf_op jit(solution)/shard_map/all_to_all | solution.py:75
  36.5 7.5 %all-to-all-done.1 = f32[16,1,64]{2,1,0:T(1,128)S(1)} async-done(((f32[16,1,64]{2,1,0:T(1,128)}), f32[16,1,64]{2,1,0:T(1,128)S(1)}, u32[]{:S(2)}, u32[]{:S(2)}) %all-to-all-start.1) | async-done | bytes 4128 | tf_op jit(solution)/shard_map/all_to_all | solution.py:75
  44.0 0.5 reduce_sum.28
  44.6 0.0 collective-permute-done.1
  44.6 2.4 %convolution_add_fusion = f32[128,768]{1,0:T(8,128)S(1)} fusion(f32[128,768]{1,0:T(8,128)S(1)} %collective-permute-done.1, bf16[1024,256]{1,0:T(8,128)(2,1)S(1)} %convolution_convert_fusion, s32[]{:T(128)S(6)} %select_n.23, f32[1024,768]{1,0:T(8,128)} %copy-done.1, f32[1024]{0:T(1024)S(1)} %copy-done.3), kind=kOutput, calls=%fused_computation.10 | convolution fusion | flops 202997760 | bytes 4198404 | tf_op jit(solution)/shard_map/dot_general | solution.py:111
  47.0 36.8 %all_to_all.24 = f32[16,8,768]{2,1,0:T(8,128)S(1)} all-to-all(f32[16,8,768]{2,1,0:T(8,128)S(1)} %bitcast.22), channel_id=1, replica_groups=mesh['wz'=16,'wy'=2,'oq'=8,'oc'=2] {'wz'}, dimensions={0} | all-to-all | bytes 786432 | tf_op jit(solution)/shard_map/all_to_all | solution.py:75
  83.9 23.0 %all_to_all.25 = bf16[16,8,768]{2,1,0:T(8,128)(2,1)S(1)} all-to-all(bf16[16,8,768]{2,1,0:T(8,128)(2,1)S(1)} %broadcast_in_dim.35), channel_id=1, replica_groups=mesh['wz'=16,'wy'=2,'oq'=8,'oc'=2] {'wz'}, dimensions={0} | all-to-all | bytes 393216 | tf_op jit(solution)/shard_map/all_to_all | solution.py:69
  106.9 2.4 %collective-permute-start.2 = (bf16[128,768]{1,0:T(8,128)(2,1)S(1)}, bf16[128,768]{1,0:T(8,128)(2,1)S(1)}, u32[]{:S(2)}, u32[]{:S(2)}) collective-permute-start(bf16[128,768]{1,0:T(8,128)(2,1)S(1)} %bitcast.24), channel_id=1, source_target_pairs={{0,16},{16,0},{1,17},{17,1},{2,18},{18,2},{3,19},{19,3},{4,20},{20... | collective-permute-start | bytes 589832 | tf_op jit(solution)/shard_map/ppermute | solution.py:61
  109.3 5.5 %collective-permute-done.2 = bf16[128,768]{1,0:T(8,128)(2,1)S(1)} collective-permute-done((bf16[128,768]{1,0:T(8,128)(2,1)S(1)}, bf16[128,768]{1,0:T(8,128)(2,1)S(1)}, u32[]{:S(2)}, u32[]{:S(2)}) %collective-permute-start.2) | collective-permute-done | bytes 196640 | tf_op jit(solution)/shard_map/ppermute | solution.py:61
  114.8 1.0 bitcast_convert_fusion
  (7 shorter events, 0.1 us)
Async XLA Ops:
  0.6 11.0 %copy-start = (bf16[4096,256]{1,0:T(8,128)(2,1)S(1)}, bf16[4096,256]{1,0:T(8,128)(2,1)}, u32[]{:S(2)}) copy-start(bf16[4096,256]{1,0:T(8,128)(2,1)} %param.11) | copy-start | bytes 6291460
  2.5 18.4 %all-to-all-start = ((bf16[8,48,768]{2,1,0:T(8,128)(2,1)}), bf16[8,48,768]{2,1,0:T(8,128)(2,1)S(1)}, u32[]{:S(2)}, u32[]{:S(2)}) async-start(bf16[8,48,768]{2,1,0:T(8,128)(2,1)} %broadcast_in_dim.16), calls=%async_computation | async-start | bytes 1179648 | tf_op jit(solution)/shard_map/all_to_all | solution.py:69
  14.1 12.0 %copy-start.4 = (s32[1024]{0:T(1024)S(1)}, s32[1024]{0:T(1024)}, u32[]{:S(2)}) copy-start(s32[1024]{0:T(1024)} %param.9) | copy-start | bytes 12292
  21.0 4.0 %collective-permute-start = (bf16[8,48,768]{2,1,0:T(8,128)(2,1)S(1)}, bf16[8,48,768]{2,1,0:T(8,128)(2,1)}, u32[]{:S(2)}, u32[]{:S(2)}) collective-permute-start(bf16[8,48,768]{2,1,0:T(8,128)(2,1)S(1)} %all-to-all-done), channel_id=1, source_target_pairs={{0,1},{1,0},{2,3},{3,2},{4,5},{5,4},{6,7},{7,6},{8,9},{9,8},{10,11... | collective-permute-start | bytes 1769480 | tf_op jit(solution)/shard_map/ppermute | solution.py:95
  26.1 1.6 %copy-start.3 = (f32[1024]{0:T(1024)S(1)}, f32[1024]{0:T(1024)}, u32[]{:S(2)}) copy-start(f32[1024]{0:T(1024)} %param.10) | copy-start | bytes 12292
  27.7 3.2 %copy-start.1 = (f32[1024,768]{1,0:T(8,128)}, f32[1024,768]{1,0:T(8,128)S(1)}, u32[]{:S(2)}) copy-start(f32[1024,768]{1,0:T(8,128)S(1)} %fusion) | copy-start | bytes 9437188
  27.7 3.2 %copy-start.2 = (bf16[256,768]{1,0:T(8,128)(2,1)S(1)}, bf16[256,768]{1,0:T(8,128)(2,1)}, u32[]{:S(2)}) copy-start(bf16[256,768]{1,0:T(8,128)(2,1)} %param.12) | copy-start | bytes 1179652
  28.3 16.3 %collective-permute-start.1 = (f32[128,768]{1,0:T(8,128)S(1)}, f32[128,768]{1,0:T(8,128)S(1)}, u32[]{:S(2)}, u32[]{:S(2)}) collective-permute-start(f32[128,768]{1,0:T(8,128)S(1)} %fusion.10), channel_id=1, source_target_pairs={{0,16},{16,0},{1,17},{17,1},{2,18},{18,2},{3,19},{19,3},{4,20},{20... | collective-permute-start | bytes 1179656 | tf_op jit(solution)/shard_map/ppermute | solution.py:56
  32.3 11.8 %all-to-all-start.1 = ((f32[16,1,64]{2,1,0:T(1,128)}), f32[16,1,64]{2,1,0:T(1,128)S(1)}, u32[]{:S(2)}, u32[]{:S(2)}) async-start(f32[16,1,64]{2,1,0:T(1,128)} %all_to_all.16), calls=%async_computation.1 | async-start | bytes 16384 | tf_op jit(solution)/shard_map/all_to_all | solution.py:75
  106.9 7.9 %collective-permute-start.2 = (bf16[128,768]{1,0:T(8,128)(2,1)S(1)}, bf16[128,768]{1,0:T(8,128)(2,1)S(1)}, u32[]{:S(2)}, u32[]{:S(2)}) collective-permute-start(bf16[128,768]{1,0:T(8,128)(2,1)S(1)} %bitcast.24), channel_id=1, source_target_pairs={{0,16},{16,0},{1,17},{17,1},{2,18},{18,2},{3,19},{19,3},{4,20},{20... | collective-permute-start | bytes 589832 | tf_op jit(solution)/shard_map/ppermute | solution.py:61
